TPU v7x, 128 devices: a whole 4x4x4 slice. The times are simulated.
128 devices in a mesh: expert: 16 (over z_hi, x, core), dp: 8 (over y, z_lo).
Axes of the slice: x: 4, y: 4, z: 4 (z_hi: 2, z_lo: 2; z = z_hi * 2 + z_lo), core: 2. Of those that a mesh axis runs over, the one named last changes fastest.
Arguments:
- tokens: bfloat16 [16384, 2048], P(('expert', 'dp')), may hold values from -6 to 6
- routes: int32 [16384, 2], P(('expert', 'dp')), may hold values from 0 to 127, all different within a row; in each aligned block of 128 rows (0 to 127, 128 to 255, ...) at most 4 rows name the same one
- gate_probs: float32 [16384, 2], P(('expert', 'dp')), may hold values from 0.05 to 1
- norm_gain: float32 [2048], replicated, may hold values from 0.1 to 1.9
- w_gate: bfloat16 [128, 2048, 768], P(('expert', 'dp')), may hold values from -0.125 to 0.125
- w_up: bfloat16 [128, 2048, 768], P(('expert', 'dp')), may hold values from -0.125 to 0.125
- w_down: bfloat16 [128, 768, 2048], P(('expert', 'dp')), may hold values from -0.21875 to 0.21875
- out_grad: bfloat16 [16384, 2048], P(('expert', 'dp')), may hold values from -6 to 6
Outputs:
- mixed: bfloat16 [16384, 2048], P(('expert', 'dp'))
- grad_probs: float32 [16384, 2], P(('expert', 'dp'))
- grad_gain: float32 [2048], replicated
- grad_tokens: bfloat16 [16384, 2048], P(('expert', 'dp'))
- grad_gate: bfloat16 [128, 2048, 768], P(('expert', 'dp'))
- grad_up: bfloat16 [128, 2048, 768], P(('expert', 'dp'))
- grad_down: bfloat16 [128, 768, 2048], P(('expert', 'dp'))
Inputs may be any that keep to these rules, and one draw needn't show every extreme that they name: `routes`: each row names 2 different experts. Among the 128 rows of one device no expert is named more than 4 times, a bound that some block reaches.
All inputs are finite; a program needn't handle non-finite values.
Results may differ from a plain program's by a relative error of at most 0.0072.
Values may be sent and summed in bfloat16 or wider, within the bound.
No kernel may reach another device: no remote copies, remote signals or barrier semaphores. Data moves between devices by JAX's collectives and lax.ppermute only.
A program may use at most 128 MiB of HBM per device.

v0:
```python
import jax
import jax.numpy as jnp
from jax import lax
from jax.sharding import PartitionSpec as P

AXES = ("expert", "dp")


def exchange(rows):
    return lax.all_to_all(rows, AXES, split_axis=0, concat_axis=0, tiled=True)


def contract(left, right, left_dim, right_dim):
    return lax.dot_general(
        left, right, (((left_dim,), (right_dim,)), ((), ())), preferred_element_type=jnp.float32
    )


def all_sum(part, devices_all):
    total = part
    step = 1
    while step < devices_all:
        pairs = [(i, i ^ step) for i in range(devices_all)]
        total = total + lax.ppermute(total, AXES, pairs)
        step *= 2
    return total


def expert_pass(arrived, arrived_grad, gate_matrix, up_matrix, down_matrix):
    pre_gate = jnp.dot(arrived, gate_matrix, preferred_element_type=jnp.float32)
    up_value = jnp.dot(arrived, up_matrix, preferred_element_type=jnp.float32)
    sigmoid_gate = jax.nn.sigmoid(pre_gate)
    activated = pre_gate * sigmoid_gate
    hidden = (activated * up_value).astype(jnp.bfloat16)
    expert_out = jnp.dot(hidden, down_matrix, preferred_element_type=jnp.float32).astype(
        jnp.bfloat16
    )
    grad_hidden = contract(arrived_grad, down_matrix, 1, 1)
    grad_down = contract(hidden, arrived_grad, 0, 0).astype(jnp.bfloat16)
    grad_pre = (
        grad_hidden * up_value * sigmoid_gate * (1.0 + pre_gate * (1.0 - sigmoid_gate))
    ).astype(jnp.bfloat16)
    grad_upval = (grad_hidden * activated).astype(jnp.bfloat16)
    grad_back = (
        contract(grad_pre, gate_matrix, 1, 1) + contract(grad_upval, up_matrix, 1, 1)
    ).astype(jnp.bfloat16)
    grad_gate = contract(arrived, grad_pre, 0, 0).astype(jnp.bfloat16)
    grad_up = contract(arrived, grad_upval, 0, 0).astype(jnp.bfloat16)
    return expert_out, grad_back, grad_gate, grad_up, grad_down


def on_device(tokens, routes, gate_probs, norm_gain, w_gate, w_up, w_down, out_grad):
    devices_all = lax.axis_size(AXES)
    tok_rows, width = tokens.shape
    top_count = routes.shape[1]
    assigned = tok_rows * top_count
    capacity = 2 * assigned // devices_all
    slots = devices_all * capacity
    inputs = tokens.astype(jnp.float32)
    inverse_rms = lax.rsqrt(jnp.mean(inputs * inputs, axis=1, keepdims=True) + 1e-06)
    normed = inputs * inverse_rms
    scaled = (normed * norm_gain).astype(jnp.bfloat16)
    flat_ids = routes.reshape(assigned)
    onehot = (flat_ids[:, None] == jnp.arange(devices_all, dtype=jnp.int32)[None, :]).astype(
        jnp.int32
    )
    earlier = jnp.cumsum(onehot, axis=0) - onehot
    slot_index = flat_ids * capacity + jnp.sum(earlier * onehot, axis=1)
    select = (slot_index[:, None] == jnp.arange(slots, dtype=jnp.int32)[None, :]).astype(
        jnp.bfloat16
    )
    select_tk = select.reshape(tok_rows, top_count, slots)
    select_tok = jnp.sum(select_tk, axis=1)
    grad_in = out_grad.astype(jnp.float32)
    grad_rows = (gate_probs[:, :, None] * grad_in[:, None, :]).astype(jnp.bfloat16)
    send_scaled = contract(select_tok, scaled, 0, 0).astype(jnp.bfloat16)
    send_grad = lax.dot_general(
        select_tk, grad_rows, (((0, 1), (0, 1)), ((), ())), preferred_element_type=jnp.float32
    ).astype(jnp.bfloat16)
    sent = jnp.concatenate([send_scaled, send_grad], axis=1).reshape(
        devices_all, capacity, 2 * width
    )
    arrived_all = exchange(sent).reshape(slots, 2 * width)
    arrived = arrived_all[:, :width]
    arrived_grad = arrived_all[:, width:]
    expert_out, grad_back, grad_gate, grad_up, grad_down = expert_pass(
        arrived, arrived_grad, w_gate[0], w_up[0], w_down[0]
    )
    back = jnp.concatenate([expert_out, grad_back], axis=1).reshape(
        devices_all, capacity, 2 * width
    )
    returned = exchange(back).reshape(slots, 2 * width)
    picked = [
        contract(select_tk[:, k, :], returned, 1, 0) for k in range(top_count)
    ]
    outs = [p[:, :width] for p in picked]
    backs = [p[:, width:] for p in picked]
    combined = gate_probs[:, 0:1] * outs[0]
    for k in range(1, top_count):
        combined = combined + gate_probs[:, k : k + 1] * outs[k]
    mixed = (inputs + combined).astype(jnp.bfloat16)
    grad_probs = jnp.stack([jnp.sum(grad_in * o, axis=1) for o in outs], axis=1)
    grad_normed = backs[0]
    for k in range(1, top_count):
        grad_normed = grad_normed + backs[k]
    gain_part = jnp.sum(grad_normed * normed, axis=0)
    grad_gain = all_sum(gain_part, devices_all)
    grad_scaled = grad_normed * norm_gain
    grad_tokens = (
        grad_in
        + inverse_rms
        * (grad_scaled - normed * jnp.mean(grad_scaled * normed, axis=1, keepdims=True))
    ).astype(jnp.bfloat16)
    return (
        mixed,
        grad_probs,
        grad_gain,
        grad_tokens,
        grad_gate[None],
        grad_up[None],
        grad_down[None],
    )


def solution(mesh):
    rows = P(AXES, None)
    stacked = P(AXES, None, None)
    return jax.shard_map(
        on_device,
        mesh=mesh,
        in_specs=(rows, rows, rows, P(), stacked, stacked, stacked, rows),
        out_specs=(rows, rows, P(), rows, stacked, stacked, stacked),
        check_vma=False,
    )
```

profile of v0, /device:TPU:0, one launch (start us, length us, event | category | flops | bytes accessed | tf_op | source)
XLA Modules:
  0.0 215.3 jit_solution(9445852117297091744)
XLA Ops:
  0.6 0.0 copy-start
  0.7 0.9 copy.29
  1.6 0.1 eq.44
  1.7 0.1 eq.40
  1.9 0.1 copy.31
  2.0 0.2 fusion.50
  2.2 0.0 copy-start.8
  2.3 0.2 fusion.52
  2.5 0.1 reduce_sum.69
  2.6 0.1 copy.33
  2.7 0.8 multiply_add_fusion
  3.5 0.1 fusion.46
  3.5 1.2 fusion.38
  4.8 1.1 convert_element_type.67
  5.9 0.8 bitcast_convert_fusion
  6.8 0.8 convolution_convert_fusion.3
  7.6 2.5 %pad_maximum_fusion = bf16[512,4096]{1,0:T(8,128)(2,1)} fusion(bf16[512,2048]{1,0:T(8,128)(2,1)S(1)} %bitcast_convert_fusion, bf16[512,2048]{1,0:T(8,128)(2,1)S(1)} %convolution_convert_fusion.3), kind=kLoop, calls=%fused_computation | loop fusion | flops 8388608 | bytes 8388608 | tf_op jit(solution)/shard_map/concatenate | solution.py:80
  10.0 7.2 %reshape.85 = bf16[128,4,4096]{2,1,0:T(4,128)(2,1)} reshape(bf16[512,4096]{1,0:T(8,128)(2,1)} %pad_maximum_fusion) | data formatting | bytes 8388608 | tf_op jit(solution)/shard_map/reshape | solution.py:80
  17.2 63.2 %all_to_all.10 = bf16[128,4,4096]{2,1,0:T(4,128)(2,1)} all-to-all(bf16[128,4,4096]{2,1,0:T(4,128)(2,1)} %reshape.85), channel_id=1, replica_groups=mesh['expert'=16,'dp'=8] {'expert','dp'}, dimensions={0} | all-to-all | bytes 8388608 | tf_op jit(solution)/shard_map/all_to_all | solution.py:10
  80.4 6.9 %reshape.86 = bf16[512,4096]{1,0:T(8,128)(2,1)} reshape(bf16[128,4,4096]{2,1,0:T(4,128)(2,1)} %all_to_all.10) | data formatting | bytes 8388608 | tf_op jit(solution)/shard_map/reshape | solution.py:83
  87.3 4.5 %fusion = f32[512,768]{1,0:T(8,128)S(1)} fusion(bf16[1,768,2048]{2,1,0:T(8,128)(2,1)} %param.14, bf16[512,4096]{1,0:T(8,128)(2,1)} %reshape.86), kind=kOutput, calls=%fused_computation.7 | convolution fusion | flops 1610612736 | bytes 6815744 | tf_op jit(solution)/shard_map/dot_general | solution.py:14
  91.8 0.0 copy-done.6
  91.8 0.2 copy-done.11
  92.0 1.8 fusion.10
  93.8 2.3 %multiply_convert_fusion.3 = (bf16[512,768]{1,0:T(8,128)(2,1)S(1)}, bf16[512,768]{1,0:T(8,128)(2,1)S(1)}, bf16[512,768]{1,0:T(8,128)(2,1)S(1)}) fusion(f32[512,768]{1,0:T(8,128)S(1)} %fusion.10, f32[512,768]{1,0:T(8,128)S(1)} %fusion, bf16[1,2048,768]{2,1,0:T(8,128)(2,1)S(1)} %copy-done, bf16[512,4096]{1,0:T(8,128)(2,1)S(1)} %copy-done.6), kind=kOutput, calls=%fused_computation.29 | convolution fusion | flops 1616510976 | bytes 10747904 | tf_op jit(solution)/shard_map/dot_general | solution.py:31
  96.1 0.0 copy-start.14
  96.1 0.0 copy-start.12
  96.2 0.0 copy-start.10
  96.2 1.8 fusion.4
  98.0 0.9 copy-done.10
  98.9 1.8 fusion.12
  100.7 1.8 add_convert_fusion
  102.5 2.5 %pad_maximum_fusion.1 = bf16[512,4096]{1,0:T(8,128)(2,1)} fusion(bf16[512,2048]{1,0:T(8,128)(2,1)S(1)} %add_convert_fusion, bf16[512,2048]{1,0:T(8,128)(2,1)S(1)} %fusion.12), kind=kLoop, calls=%fused_computation.1 | loop fusion | flops 8388608 | bytes 8388608 | tf_op jit(solution)/shard_map/concatenate | solution.py:89
  105.0 7.2 %reshape.87 = bf16[128,4,4096]{2,1,0:T(4,128)(2,1)} reshape(bf16[512,4096]{1,0:T(8,128)(2,1)} %pad_maximum_fusion.1) | data formatting | bytes 8388608 | tf_op jit(solution)/shard_map/reshape | solution.py:89
  112.2 7.1 %all-to-all-start.1 = ((bf16[128,4,4096]{2,1,0:T(4,128)(2,1)}), bf16[128,4,4096]{2,1,0:T(4,128)(2,1)}, u32[]{:S(2)}, u32[]{:S(2)}) async-start(bf16[128,4,4096]{2,1,0:T(4,128)(2,1)} %reshape.87), calls=%async_computation.1 | async-start | bytes 8388608 | tf_op jit(solution)/shard_map/all_to_all | solution.py:10
  119.3 0.1 iota_compare_fusion
  119.4 51.2 %all-to-all-done.1 = bf16[128,4,4096]{2,1,0:T(4,128)(2,1)} async-done(((bf16[128,4,4096]{2,1,0:T(4,128)(2,1)}), bf16[128,4,4096]{2,1,0:T(4,128)(2,1)}, u32[]{:S(2)}, u32[]{:S(2)}) %all-to-all-start.1) | async-done | bytes 4194336 | tf_op jit(solution)/shard_map/all_to_all | solution.py:10
  170.6 6.9 %reshape.88 = bf16[512,4096]{1,0:T(8,128)(2,1)} reshape(bf16[128,4,4096]{2,1,0:T(4,128)(2,1)} %all-to-all-done.1) | data formatting | bytes 8388608 | tf_op jit(solution)/shard_map/reshape | solution.py:92
  177.4 3.1 %fusion.49 = f32[128,4096]{1,0:T(8,128)S(1)} fusion(bf16[512,4096]{1,0:T(8,128)(2,1)} %reshape.88, pred[128,2,512]{0,2,1:T(32,128)(4,1)S(1)} %iota_compare_fusion), kind=kOutput, calls=%fused_computation.66 | convolution fusion | flops 536870912 | bytes 6356992 | tf_op jit(solution)/shard_map/dot_general | solution.py:14
  180.6 0.3 copy-done.2
  180.9 0.8 fusion.48
  181.7 0.3 copy-done.4
  181.9 0.2 copy-done.5
  182.1 0.7 fusion.33
  182.8 0.9 collective-permute-start
  183.7 2.8 %collective-permute-done = f32[2048]{0:T(1024)S(1)} collective-permute-done((f32[2048]{0:T(1024)S(1)}, f32[2048]{0:T(1024)S(1)}, u32[]{:S(2)}, u32[]{:S(2)}) %collective-permute-start) | collective-permute-done | bytes 8224 | tf_op jit(solution)/shard_map/ppermute | solution.py:24
  186.5 0.7 collective-permute-start.1
  187.2 3.5 %fusion.15 = bf16[1,2048,768]{2,1,0:T(8,128)(2,1)} fusion(bf16[512,768]{1,0:T(8,128)(2,1)S(1)} %copy-done.13, bf16[512,4096]{1,0:T(8,128)(2,1)S(1)} %copy-done.7), kind=kOutput, calls=%fused_computation.21 | convolution fusion | flops 1612185600 | bytes 6029312 | tf_op jit(solution)/shard_map/dot_general | solution.py:14
  190.8 0.0 collective-permute-done.1
  190.8 2.9 %collective-permute-start.2 = (f32[2048]{0:T(1024)S(1)}, f32[2048]{0:T(1024)S(1)}, u32[]{:S(2)}, u32[]{:S(2)}) collective-permute-start(f32[2048]{0:T(1024)S(1)} %add.70), channel_id=1, source_target_pairs={{0,4},{1,5},{2,6},{3,7},{4,0},{5,1},{6,2},{7,3},{8,12},{9,13},{10,... | collective-permute-start | bytes 24584 | tf_op jit(solution)/shard_map/ppermute | solution.py:24
  193.7 3.5 %fusion.16 = bf16[1,2048,768]{2,1,0:T(8,128)(2,1)} fusion(bf16[512,768]{1,0:T(8,128)(2,1)S(1)} %copy-done.15, bf16[512,4096]{1,0:T(8,128)(2,1)S(1)} %copy-done.7), kind=kOutput, calls=%fused_computation.22 | convolution fusion | flops 1612185600 | bytes 6029312 | tf_op jit(solution)/shard_map/dot_general | solution.py:14
  197.2 0.0 collective-permute-done.2
  197.2 0.0 collective-permute-start.3
  197.2 3.5 %fusion.17 = bf16[1,768,2048]{2,1,0:T(8,128)(2,1)} fusion(bf16[512,768]{1,0:T(8,128)(2,1)S(1)} %copy-done.17, bf16[512,4096]{1,0:T(8,128)(2,1)S(1)} %copy-done.7), kind=kOutput, calls=%fused_computation.23 | convolution fusion | flops 1612185600 | bytes 6029312 | tf_op jit(solution)/shard_map/dot_general | solution.py:14
  200.7 0.0 collective-permute-done.3
  200.8 0.6 collective-permute-start.4
  201.4 3.0 %collective-permute-done.4 = f32[2048]{0:T(1024)S(1)} collective-permute-done((f32[2048]{0:T(1024)S(1)}, f32[2048]{0:T(1024)S(1)}, u32[]{:S(2)}, u32[]{:S(2)}) %collective-permute-start.4) | collective-permute-done | bytes 8224 | tf_op jit(solution)/shard_map/ppermute | solution.py:24
  204.4 2.1 collective-permute-start.5
  206.5 1.4 fusion.37
  207.9 1.6 collective-permute-done.5
  209.6 0.8 collective-permute-start.6
  210.4 0.6 pad_maximum_fusion.2
  211.0 3.7 %collective-permute-done.6 = f32[2048]{0:T(1024)S(1)} collective-permute-done((f32[2048]{0:T(1024)S(1)}, f32[2048]{0:T(1024)S(1)}, u32[]{:S(2)}, u32[]{:S(2)}) %collective-permute-start.6) | collective-permute-done | bytes 8224 | tf_op jit(solution)/shard_map/ppermute | solution.py:24
  214.7 0.6 add.75
  (40 shorter events, 0.2 us)
Async XLA Ops:
  0.6 93.2 %copy-start = (bf16[1,2048,768]{2,1,0:T(8,128)(2,1)S(1)}, bf16[1,2048,768]{2,1,0:T(8,128)(2,1)}, u32[]{:S(2)}) copy-start(bf16[1,2048,768]{2,1,0:T(8,128)(2,1)} %param.13) | copy-start | bytes 9437188
  0.6 5.3 %copy-start.9 = (f32[128,2]{0,1:T(2,128)S(1)}, f32[128,2]{0,1:T(2,128)}, u32[]{:S(2)}) copy-start(f32[128,2]{0,1:T(2,128)} %param.10) | copy-start | bytes 3076
  2.2 4.6 %copy-start.8 = (f32[2048]{0:T(1024)S(1)}, f32[2048]{0:T(1024)}, u32[]{:S(2)}) copy-start(f32[2048]{0:T(1024)} %param.11) | copy-start | bytes 24580
  2.7 4.1 %copy-start.3 = (bf16[128,2048]{1,0:T(8,128)(2,1)S(1)}, bf16[128,2048]{1,0:T(8,128)(2,1)}, u32[]{:S(2)}) copy-start(bf16[128,2048]{1,0:T(8,128)(2,1)} %param.8) | copy-start | bytes 1572868
  87.3 4.5 %copy-start.6 = (bf16[512,4096]{1,0:T(8,128)(2,1)S(1)}, bf16[512,4096]{1,0:T(8,128)(2,1)}, u32[]{:S(2)}) copy-start(bf16[512,4096]{1,0:T(8,128)(2,1)} %reshape.86) | copy-start | bytes 12582916
  87.3 4.7 %copy-start.11 = (bf16[1,2048,768]{2,1,0:T(8,128)(2,1)S(1)}, bf16[1,2048,768]{2,1,0:T(8,128)(2,1)}, u32[]{:S(2)}) copy-start(bf16[1,2048,768]{2,1,0:T(8,128)(2,1)} %param.12) | copy-start | bytes 9437188
  96.1 1.9 copy-start.14
  96.1 1.9 copy-start.16
  96.1 4.5 %copy-start.12 = (bf16[512,768]{1,0:T(8,128)(2,1)}, bf16[512,768]{1,0:T(8,128)(2,1)S(1)}, u32[]{:S(2)}) copy-start(bf16[512,768]{1,0:T(8,128)(2,1)S(1)} %get-tuple-element.14) | copy-start | bytes 2359300
  96.2 2.7 %copy-start.10 = (bf16[1,768,2048]{2,1,0:T(8,128)(2,1)S(1)}, bf16[1,768,2048]{2,1,0:T(8,128)(2,1)}, u32[]{:S(2)}) copy-start(bf16[1,768,2048]{2,1,0:T(8,128)(2,1)} %param.14) | copy-start | bytes 9437188
  112.2 58.4 %all-to-all-start.1 = ((bf16[128,4,4096]{2,1,0:T(4,128)(2,1)}), bf16[128,4,4096]{2,1,0:T(4,128)(2,1)}, u32[]{:S(2)}, u32[]{:S(2)}) async-start(bf16[128,4,4096]{2,1,0:T(4,128)(2,1)} %reshape.87), calls=%async_computation.1 | async-start | bytes 8388608 | tf_op jit(solution)/shard_map/all_to_all | solution.py:10
  177.4 3.4 %copy-start.2 = (bf16[512,4096]{1,0:T(8,128)(2,1)S(1)}, bf16[512,4096]{1,0:T(8,128)(2,1)}, u32[]{:S(2)}) copy-start(bf16[512,4096]{1,0:T(8,128)(2,1)} %reshape.88) | copy-start | bytes 12582916
  180.9 1.0 copy-start.4
  180.9 1.2 copy-start.5
  182.1 5.1 %copy-start.7 = (bf16[512,4096]{1,0:T(8,128)(2,1)S(1)}, bf16[512,4096]{1,0:T(8,128)(2,1)}, u32[]{:S(2)}) copy-start(bf16[512,4096]{1,0:T(8,128)(2,1)} %reshape.86) | copy-start | bytes 12582916
  182.1 5.1 %copy-start.13 = (bf16[512,768]{1,0:T(8,128)(2,1)S(1)}, bf16[512,768]{1,0:T(8,128)(2,1)}, u32[]{:S(2)}) copy-start(bf16[512,768]{1,0:T(8,128)(2,1)} %copy-done.12) | copy-start | bytes 2359300
  182.8 3.7 %collective-permute-start = (f32[2048]{0:T(1024)S(1)}, f32[2048]{0:T(1024)S(1)}, u32[]{:S(2)}, u32[]{:S(2)}) collective-permute-start(f32[2048]{0:T(1024)S(1)} %get-tuple-element.8), channel_id=1, source_target_pairs={{0,1},{1,0},{2,3},{3,2},{4,5},{5,4},{6,7},{7,6},{8,9},{9,8},{10,11... | collective-permute-start | bytes 24584 | tf_op jit(solution)/shard_map/ppermute | solution.py:24
  186.5 7.2 %copy-start.15 = (bf16[512,768]{1,0:T(8,128)(2,1)S(1)}, bf16[512,768]{1,0:T(8,128)(2,1)}, u32[]{:S(2)}) copy-start(bf16[512,768]{1,0:T(8,128)(2,1)} %copy-done.14) | copy-start | bytes 2359300
  186.5 4.3 %collective-permute-start.1 = (f32[2048]{0:T(1024)S(1)}, f32[2048]{0:T(1024)S(1)}, u32[]{:S(2)}, u32[]{:S(2)}) collective-permute-start(f32[2048]{0:T(1024)S(1)} %add.69), channel_id=1, source_target_pairs={{0,2},{1,3},{2,0},{3,1},{4,6},{5,7},{6,4},{7,5},{8,10},{9,11},{10,... | collective-permute-start | bytes 24584 | tf_op jit(solution)/shard_map/ppermute | solution.py:24
  190.8 6.4 %copy-start.17 = (bf16[512,768]{1,0:T(8,128)(2,1)S(1)}, bf16[512,768]{1,0:T(8,128)(2,1)}, u32[]{:S(2)}) copy-start(bf16[512,768]{1,0:T(8,128)(2,1)} %copy-done.16) | copy-start | bytes 2359300
  190.8 6.4 %collective-permute-start.2 = (f32[2048]{0:T(1024)S(1)}, f32[2048]{0:T(1024)S(1)}, u32[]{:S(2)}, u32[]{:S(2)}) collective-permute-start(f32[2048]{0:T(1024)S(1)} %add.70), channel_id=1, source_target_pairs={{0,4},{1,5},{2,6},{3,7},{4,0},{5,1},{6,2},{7,3},{8,12},{9,13},{10,... | collective-permute-start | bytes 24584 | tf_op jit(solution)/shard_map/ppermute | solution.py:24
  197.2 3.5 %collective-permute-start.3 = (f32[2048]{0:T(1024)S(1)}, f32[2048]{0:T(1024)S(1)}, u32[]{:S(2)}, u32[]{:S(2)}) collective-permute-start(f32[2048]{0:T(1024)S(1)} %add.71), channel_id=1, source_target_pairs={{0,8},{1,9},{2,10},{3,11},{4,12},{5,13},{6,14},{7,15},{8,0},{9,1},... | collective-permute-start | bytes 24584 | tf_op jit(solution)/shard_map/ppermute | solution.py:24
  200.8 3.7 %collective-permute-start.4 = (f32[2048]{0:T(1024)S(1)}, f32[2048]{0:T(1024)S(1)}, u32[]{:S(2)}, u32[]{:S(2)}) collective-permute-start(f32[2048]{0:T(1024)S(1)} %add.72), channel_id=1, source_target_pairs={{0,16},{1,17},{2,18},{3,19},{4,20},{5,21},{6,22},{7,23},{8,24},{9,... | collective-permute-start | bytes 24584 | tf_op jit(solution)/shard_map/ppermute | solution.py:24
  204.4 5.2 %collective-permute-start.5 = (f32[2048]{0:T(1024)S(1)}, f32[2048]{0:T(1024)S(1)}, u32[]{:S(2)}, u32[]{:S(2)}) collective-permute-start(f32[2048]{0:T(1024)S(1)} %add.73), channel_id=1, source_target_pairs={{0,32},{1,33},{2,34},{3,35},{4,36},{5,37},{6,38},{7,39},{8,40},{9,... | collective-permute-start | bytes 24584 | tf_op jit(solution)/shard_map/ppermute | solution.py:24
  206.5 8.9 %copy-start.1 = (bf16[1,2048,768]{2,1,0:T(8,128)(2,1)S(1)}, bf16[1,2048,768]{2,1,0:T(8,128)(2,1)}, u32[]{:S(2)}) copy-start(bf16[1,2048,768]{2,1,0:T(8,128)(2,1)} %param.13) | copy-start | bytes 9437188
  209.6 5.2 %collective-permute-start.6 = (f32[2048]{0:T(1024)S(1)}, f32[2048]{0:T(1024)S(1)}, u32[]{:S(2)}, u32[]{:S(2)}) collective-permute-start(f32[2048]{0:T(1024)S(1)} %add.74), channel_id=1, source_target_pairs={{0,64},{1,65},{2,66},{3,67},{4,68},{5,69},{6,70},{7,71},{8,72},{9,... | collective-permute-start | bytes 24584 | tf_op jit(solution)/shard_map/ppermute | solution.py:24
where the time goes:
time: 216 us; the launch traced here: 215 us
  blocking collectives  63.2 us (29%)
  waiting for transfers between devices  62.4 us (29%)
  local copies, waits for them, and re-layouts  31.6 us (15%)
  matrix products  30.1 us (14%)
  starting transfers between devices  15.2 us (7%)
  other arithmetic  12 us (6%)
    all_to_all x1, blocking collectives, exchange(): return lax.all_to_all(rows, AXES, split_axis=0, concat_axis=0, tiled=True)  63.2 us
    all_to_all x1, waiting for transfers between devices, exchange(): return lax.all_to_all(rows, AXES, split_axis=0, concat_axis=0, tiled=True)  51.2 us
    dot_general x9, matrix products, contract(): lax.dot_general(left, right, (((left_dim,), (right_dim,)), ((), ())), pre...  23.4 us
    ppermute x7, waiting for transfers between devices, all_sum(): total = total + lax.ppermute(total, AXES, pairs)  11.2 us
    ppermute x7, starting transfers between devices, all_sum(): total = total + lax.ppermute(total, AXES, pairs)  8.05 us
    reshape x1, local copies, waits for them, and re-layouts, on_device(): jnp.concatenate([send_scaled, send_grad], axis=1)  7.17 us
    reshape x1, local copies, waits for them, and re-layouts, on_device(): jnp.concatenate([expert_out, grad_back], axis=1)  7.17 us
    all_to_all x1, starting transfers between devices, exchange(): return lax.all_to_all(rows, AXES, split_axis=0, concat_axis=0, tiled=True)  7.13 us
  transfers between devices with their start and end apart: 8, of which 5 were waited for; matrix products, arithmetic and copies ran while one was open for 6% of the time, Pallas kernels for 0%

commit v1 on v0

--- a/solution.py
+++ b/solution.py
@@ -17,12 +17,22 @@
 
 
 def all_sum(part, devices_all):
+    me = lax.axis_index(AXES)
     total = part
     step = 1
     while step < devices_all:
-        pairs = [(i, i ^ step) for i in range(devices_all)]
-        total = total + lax.ppermute(total, AXES, pairs)
-        step *= 2
+        radix = 4 if step * 4 <= devices_all else 2
+        held = [total] + [
+            lax.ppermute(total, AXES, [(i, i ^ (x * step)) for i in range(devices_all)])
+            for x in range(1, radix)
+        ]
+        position = (me // step) % radix
+        canon = [lax.select_n(position ^ q, *held) for q in range(radix)]
+        if radix == 4:
+            total = (canon[0] + canon[1]) + (canon[2] + canon[3])
+        else:
+            total = canon[0] + canon[1]
+        step *= radix
     return total
 
 
@@ -73,13 +83,13 @@
     select_tok = jnp.sum(select_tk, axis=1)
     grad_in = out_grad.astype(jnp.float32)
     grad_rows = (gate_probs[:, :, None] * grad_in[:, None, :]).astype(jnp.bfloat16)
-    send_scaled = contract(select_tok, scaled, 0, 0).astype(jnp.bfloat16)
+    sel_tok3 = select_tok.reshape(tok_rows, devices_all, capacity)
+    sel_tk3 = select_tk.reshape(tok_rows, top_count, devices_all, capacity)
+    send_scaled = lax.dot_general(sel_tok3, scaled, (((0,), (0,)), ((), ())), preferred_element_type=jnp.float32).astype(jnp.bfloat16)
     send_grad = lax.dot_general(
-        select_tk, grad_rows, (((0, 1), (0, 1)), ((), ())), preferred_element_type=jnp.float32
+        sel_tk3, grad_rows, (((0, 1), (0, 1)), ((), ())), preferred_element_type=jnp.float32
     ).astype(jnp.bfloat16)
-    sent = jnp.concatenate([send_scaled, send_grad], axis=1).reshape(
-        devices_all, capacity, 2 * width
-    )
+    sent = jnp.concatenate([send_scaled, send_grad], axis=2)
     arrived_all = exchange(sent).reshape(slots, 2 * width)
     arrived = arrived_all[:, :width]
     arrived_grad = arrived_all[:, width:]
@@ -89,7 +99,10 @@
     back = jnp.concatenate([expert_out, grad_back], axis=1).reshape(
         devices_all, capacity, 2 * width
     )
-    returned = exchange(back).reshape(slots, 2 * width)
+    returned, grad_gate, grad_up, grad_down = lax.optimization_barrier(
+        (exchange(back), grad_gate, grad_up, grad_down)
+    )
+    returned = returned.reshape(slots, 2 * width)
     picked = [
         contract(select_tk[:, k, :], returned, 1, 0) for k in range(top_count)
     ]

time: 216 us -> 208 us (0.963)
  waiting for transfers between devices: 62.4 us -> 47 us
  starting transfers between devices: 15.2 us -> 21.2 us
  matrix products: 30.1 us -> 32.8 us
  local copies, waits for them, and re-layouts: 31.6 us -> 29.3 us
    all_to_all x1, waiting for transfers between devices: 51.2 us -> 38.7 us  [exchange(): return lax.all_to_all(rows, AXES, split_axis=0, concat_axis=0, tiled=True)]
    reshape x2 -> x1, local copies, waits for them, and re-layouts: 14.1 us -> 6.89 us  [on_device(): returned = returned.reshape(slots, 2 * width)]
    ppermute x7 -> x10, starting transfers between devices: 8.05 us -> 14 us  [all_sum(): lax.ppermute(total, AXES, [(i, i ^ x * step) for i in range(devices_all)])]
    concatenate x0 -> x1, local copies, waits for them, and re-layouts: none -> 3.24 us  [on_device(): sent = jnp.concatenate([send_scaled, send_grad], axis=2)]
    ppermute x7 -> x10, waiting for transfers between devices: 11.2 us -> 8.31 us  [all_sum(): lax.ppermute(total, AXES, [(i, i ^ x * step) for i in range(devices_all)])]
    convert_element_type x1, other arithmetic: 1.45 us -> 4.06 us  [on_device(): grad_tokens = (grad_in + inverse_rms * (grad_scaled - normed * jnp.mean(g...]
    concatenate x1, other arithmetic: 2.46 us -> 0.27 us  [on_device(): sent = jnp.concatenate([send_scaled, send_grad], axis=2)]
    unnamed x38 -> x40, local copies, waits for them, and re-layouts: 2.85 us -> 4.34 us
  transfers between devices with their start and end apart: 8 -> 11, of which waited for: 5 -> 7; matrix products, arithmetic and copies ran while one was open for 6% -> 8% of each run, Pallas kernels for 0% -> 0%
where the time goes in v1:
time: 208 us; the launch traced here: 207 us
  blocking collectives  63 us (30%)
  waiting for transfers between devices  47 us (23%)
  matrix products  32.8 us (16%)
  local copies, waits for them, and re-layouts  29.3 us (14%)
  starting transfers between devices  21.2 us (10%)
  other arithmetic  12.5 us (6%)
    all_to_all x1, blocking collectives, exchange(): return lax.all_to_all(rows, AXES, split_axis=0, concat_axis=0, tiled=True)  63 us
    all_to_all x1, waiting for transfers between devices, exchange(): return lax.all_to_all(rows, AXES, split_axis=0, concat_axis=0, tiled=True)  38.7 us
    dot_general x8, matrix products, contract(): lax.dot_general(left, right, (((left_dim,), (right_dim,)), ((), ())), pre...  24.3 us
    ppermute x10, starting transfers between devices, all_sum(): lax.ppermute(total, AXES, [(i, i ^ x * step) for i in range(devices_all)])  14 us
    ppermute x10, waiting for transfers between devices, all_sum(): lax.ppermute(total, AXES, [(i, i ^ x * step) for i in range(devices_all)])  8.31 us
    reshape x1, local copies, waits for them, and re-layouts, on_device(): jnp.concatenate([expert_out, grad_back], axis=1)  7.19 us
    all_to_all x1, starting transfers between devices, exchange(): return lax.all_to_all(rows, AXES, split_axis=0, concat_axis=0, tiled=True)  7.13 us
    reshape x1, local copies, waits for them, and re-layouts, on_device(): arrived_all = exchange(sent).reshape(slots, 2 * width)  6.89 us
  transfers between devices with their start and end apart: 11, of which 7 were waited for; matrix products, arithmetic and copies ran while one was open for 8% of the time, Pallas kernels for 0%

profile of v1, /device:TPU:0, one launch (start us, length us, event | category | flops | bytes accessed | tf_op | source)
XLA Modules:
  0.0 206.8 jit_solution(17805475441629053553)
XLA Ops:
  0.6 0.0 copy-start
  0.7 0.9 copy.37
  1.6 0.1 eq.62
  1.7 0.1 eq.58
  1.9 0.1 copy.39
  2.0 0.2 fusion.50
  2.3 0.2 fusion.52
  2.5 0.1 reduce_sum.69
  2.6 0.1 copy.41
  2.7 0.7 multiply_add_fusion.1
  3.4 0.1 convert_reduce_fusion
  3.5 0.1 copy.42
  3.7 1.2 fusion.35
  4.9 1.1 convert_element_type.67
  6.1 1.8 convolution_convert_fusion.3
  7.9 0.8 bitcast_convert_fusion
  8.7 0.3 pad_maximum_fusion
  9.0 3.2 %copy.44 = bf16[128,4,4096]{2,1,0:T(4,128)(2,1)S(1)} copy(bf16[128,4,4096]{2,0,1:T(8,128)(2,1)S(1)} %pad_maximum_fusion) | data formatting | bytes 8388608 | tf_op jit(solution)/shard_map/concatenate | solution.py:92
  12.2 63.0 %all_to_all.10 = bf16[128,4,4096]{2,1,0:T(4,128)(2,1)} all-to-all(bf16[128,4,4096]{2,1,0:T(4,128)(2,1)S(1)} %copy.44), channel_id=1, replica_groups=mesh['expert'=16,'dp'=8] {'expert','dp'}, dimensions={0} | all-to-all | bytes 8388608 | tf_op jit(solution)/shard_map/all_to_all | solution.py:10
  75.2 6.9 %reshape.100 = bf16[512,4096]{1,0:T(8,128)(2,1)} reshape(bf16[128,4,4096]{2,1,0:T(4,128)(2,1)} %all_to_all.10) | data formatting | bytes 8388608 | tf_op jit(solution)/shard_map/reshape | solution.py:93
  82.1 4.5 %fusion = f32[512,768]{1,0:T(8,128)S(1)} fusion(bf16[1,768,2048]{2,1,0:T(8,128)(2,1)} %param.14, bf16[512,4096]{1,0:T(8,128)(2,1)} %reshape.100), kind=kOutput, calls=%fused_computation.7 | convolution fusion | flops 1610612736 | bytes 6815744 | tf_op jit(solution)/shard_map/dot_general | solution.py:14
  86.6 0.2 copy-done.12
  86.8 1.8 fusion.10
  88.7 2.3 %multiply_convert_fusion.3 = (bf16[512,768]{1,0:T(8,128)(2,1)S(1)}, bf16[512,768]{1,0:T(8,128)(2,1)S(1)}, bf16[512,768]{1,0:T(8,128)(2,1)S(1)}) fusion(f32[512,768]{1,0:T(8,128)S(1)} %fusion.10, f32[512,768]{1,0:T(8,128)S(1)} %fusion, bf16[1,2048,768]{2,1,0:T(8,128)(2,1)S(1)} %copy-done, bf16[512,4096]{1,0:T(8,128)(2,1)S(1)} %copy-done.7), kind=kOutput, calls=%fused_computation.26 | convolution fusion | flops 1616510976 | bytes 10747904 | tf_op jit(solution)/shard_map/dot_general | solution.py:41
  91.0 0.0 copy-start.15
  91.0 1.8 fusion.4
  92.8 0.9 copy-done.11
  93.7 1.8 fusion.12
  95.5 1.8 add_convert_fusion
  97.4 2.5 %pad_maximum_fusion.1 = bf16[512,4096]{1,0:T(8,128)(2,1)} fusion(bf16[512,2048]{1,0:T(8,128)(2,1)S(1)} %add_convert_fusion, bf16[512,2048]{1,0:T(8,128)(2,1)S(1)} %fusion.12), kind=kLoop, calls=%fused_computation.1 | loop fusion | flops 8388608 | bytes 8388608 | tf_op jit(solution)/shard_map/concatenate | solution.py:99
  99.9 7.2 %reshape.101 = bf16[128,4,4096]{2,1,0:T(4,128)(2,1)} reshape(bf16[512,4096]{1,0:T(8,128)(2,1)} %pad_maximum_fusion.1) | data formatting | bytes 8388608 | tf_op jit(solution)/shard_map/reshape | solution.py:99
  107.1 7.1 %all-to-all-start.1 = ((bf16[128,4,4096]{2,1,0:T(4,128)(2,1)}), bf16[128,4,4096]{2,1,0:T(4,128)(2,1)}, u32[]{:S(2)}, u32[]{:S(2)}) async-start(bf16[128,4,4096]{2,1,0:T(4,128)(2,1)} %reshape.101), calls=%async_computation.1 | async-start | bytes 8388608 | tf_op jit(solution)/shard_map/all_to_all | solution.py:10
  114.2 0.1 iota_compare_fusion
  114.4 5.2 %convolution_convert_fusion = bf16[768,2048]{1,0:T(8,128)(2,1)} fusion(bf16[512,768]{1,0:T(8,128)(2,1)S(1)} %copy-done.18, bf16[512,4096]{1,0:T(8,128)(2,1)} %reshape.100), kind=kOutput, calls=%fused_computation.4 | convolution fusion | flops 1612185600 | bytes 6029312 | tf_op jit(solution)/shard_map/dot_general | solution.py:14
  119.6 3.5 %convolution_convert_fusion.1 = bf16[2048,768]{1,0:T(8,128)(2,1)} fusion(bf16[512,768]{1,0:T(8,128)(2,1)S(1)} %copy-done.16, bf16[512,4096]{1,0:T(8,128)(2,1)S(1)} %copy-done.8), kind=kOutput, calls=%fused_computation.5 | convolution fusion | flops 1612185600 | bytes 6029312 | tf_op jit(solution)/shard_map/dot_general | solution.py:14
  123.2 3.5 %convolution_convert_fusion.2 = bf16[2048,768]{1,0:T(8,128)(2,1)} fusion(bf16[512,768]{1,0:T(8,128)(2,1)S(1)} %copy-done.14, bf16[512,4096]{1,0:T(8,128)(2,1)S(1)} %copy-done.8), kind=kOutput, calls=%fused_computation.6 | convolution fusion | flops 1612185600 | bytes 6029312 | tf_op jit(solution)/shard_map/dot_general | solution.py:14
  126.7 38.7 %all-to-all-done.1 = bf16[128,4,4096]{2,1,0:T(4,128)(2,1)} async-done(((bf16[128,4,4096]{2,1,0:T(4,128)(2,1)}), bf16[128,4,4096]{2,1,0:T(4,128)(2,1)}, u32[]{:S(2)}, u32[]{:S(2)}) %all-to-all-start.1) | async-done | bytes 4194336 | tf_op jit(solution)/shard_map/all_to_all | solution.py:10
  165.5 6.9 %reshape.102 = bf16[512,4096]{1,0:T(8,128)(2,1)} reshape(bf16[128,4,4096]{2,1,0:T(4,128)(2,1)} %all-to-all-done.1) | data formatting | bytes 8388608 | tf_op jit(solution)/shard_map/reshape | solution.py:105
  172.3 3.1 %fusion.49 = f32[128,4096]{1,0:T(8,128)S(1)} fusion(bf16[512,4096]{1,0:T(8,128)(2,1)} %reshape.102, pred[128,2,512]{2,0,1:T(32,128)(4,1)S(1)} %iota_compare_fusion), kind=kOutput, calls=%fused_computation.66 | convolution fusion | flops 536870912 | bytes 6356992 | tf_op jit(solution)/shard_map/dot_general | solution.py:14
  175.4 0.4 copy-done.2
  175.8 0.7 fusion.48
  176.5 0.6 copy-done.3
  177.1 0.1 copy-done.5
  177.2 0.6 copy-done.6
  177.8 0.7 fusion.30
  178.4 0.7 copy-done.4
  179.1 0.8 collective-permute-start
  179.9 0.9 collective-permute-start.1
  180.8 1.8 collective-permute-start.2
  182.6 0.2 collective-permute-done
  182.7 0.8 collective-permute-done.1
  183.6 1.8 collective-permute-done.2
  185.4 2.1 collective-permute-start.3
  187.4 1.7 collective-permute-start.5
  189.1 1.5 collective-permute-done.3
  190.6 1.4 collective-permute-done.5
  192.0 0.5 collective-permute-start.6
  192.6 2.8 %collective-permute-start.7 = (f32[2048]{0:T(1024)S(1)}, f32[2048]{0:T(1024)S(1)}, u32[]{:S(2)}, u32[]{:S(2)}) collective-permute-start(f32[2048]{0:T(1024)S(1)} %add_add_fusion.1), channel_id=1, source_target_pairs={{0,32},{1,33},{2,34},{3,35},{4,36},{5,37},{6,38},{7,39},{8,40},{9,... | collective-permute-start | bytes 24584 | tf_op jit(solution)/shard_map/ppermute | solution.py:26
  195.3 1.5 collective-permute-start.8
  196.8 4.1 %fusion.34 = (bf16[128,2048]{1,0:T(8,128)(2,1)}, bf16[128,2048]{1,0:T(8,128)(2,1)}) fusion(bf16[128,2048]{1,0:T(8,128)(2,1)} %param.8, bf16[128,2048]{1,0:T(8,128)(2,1)} %param.15, f32[128]{0:T(128)S(1)} %broadcast_multiply_fusion, f32[2048]{0:T(1024)S(1)} %copy-done.9, f32[128]{0:T(128)S(1)} %add_rsqrt_fusion, f32[128,4096]{1,0:T(8,128)} %copy-done.4, ...), kind=kLoop, calls=%fused_computation.46 | loop fusion | flops 3932160 | bytes 6301696 | tf_op jit(solution)/shard_map/convert_element_type | solution.py:126
  200.9 2.1 collective-permute-start.9
  203.0 0.6 pad_maximum_fusion.2
  203.5 2.6 %collective-permute-done.9 = f32[2048]{0:T(1024)S(1)} collective-permute-done((f32[2048]{0:T(1024)S(1)}, f32[2048]{0:T(1024)S(1)}, u32[]{:S(2)}, u32[]{:S(2)}) %collective-permute-start.9) | collective-permute-done | bytes 8224 | tf_op jit(solution)/shard_map/ppermute | solution.py:26
  206.2 0.6 select_add_fusion
  (47 shorter events, 0.2 us)
Async XLA Ops:
  0.6 88.0 %copy-start = (bf16[1,2048,768]{2,1,0:T(8,128)(2,1)S(1)}, bf16[1,2048,768]{2,1,0:T(8,128)(2,1)}, u32[]{:S(2)}) copy-start(bf16[1,2048,768]{2,1,0:T(8,128)(2,1)} %param.13) | copy-start | bytes 9437188
  0.6 5.4 %copy-start.9 = (f32[2048]{0:T(1024)S(1)}, f32[2048]{0:T(1024)}, u32[]{:S(2)}) copy-start(f32[2048]{0:T(1024)} %param.11) | copy-start | bytes 24580
  2.0 5.9 %copy-start.10 = (f32[128,2]{0,1:T(2,128)S(1)}, f32[128,2]{0,1:T(2,128)}, u32[]{:S(2)}) copy-start(f32[128,2]{0,1:T(2,128)} %param.10) | copy-start | bytes 3076
  82.1 4.5 %copy-start.7 = (bf16[512,4096]{1,0:T(8,128)(2,1)S(1)}, bf16[512,4096]{1,0:T(8,128)(2,1)}, u32[]{:S(2)}) copy-start(bf16[512,4096]{1,0:T(8,128)(2,1)} %reshape.100) | copy-start | bytes 12582916
  82.1 4.7 %copy-start.12 = (bf16[1,2048,768]{2,1,0:T(8,128)(2,1)S(1)}, bf16[1,2048,768]{2,1,0:T(8,128)(2,1)}, u32[]{:S(2)}) copy-start(bf16[1,2048,768]{2,1,0:T(8,128)(2,1)} %param.12) | copy-start | bytes 9437188
  91.0 1.9 copy-start.15
  91.0 1.9 copy-start.17
  91.0 4.5 %copy-start.13 = (bf16[512,768]{1,0:T(8,128)(2,1)}, bf16[512,768]{1,0:T(8,128)(2,1)S(1)}, u32[]{:S(2)}) copy-start(bf16[512,768]{1,0:T(8,128)(2,1)S(1)} %get-tuple-element.22) | copy-start | bytes 2359300
  91.0 2.7 %copy-start.11 = (bf16[1,768,2048]{2,1,0:T(8,128)(2,1)S(1)}, bf16[1,768,2048]{2,1,0:T(8,128)(2,1)}, u32[]{:S(2)}) copy-start(bf16[1,768,2048]{2,1,0:T(8,128)(2,1)} %param.14) | copy-start | bytes 9437188
  107.1 7.3 %copy-start.18 = (bf16[512,768]{1,0:T(8,128)(2,1)S(1)}, bf16[512,768]{1,0:T(8,128)(2,1)}, u32[]{:S(2)}) copy-start(bf16[512,768]{1,0:T(8,128)(2,1)} %copy-done.17) | copy-start | bytes 2359300
  107.1 58.4 %all-to-all-start.1 = ((bf16[128,4,4096]{2,1,0:T(4,128)(2,1)}), bf16[128,4,4096]{2,1,0:T(4,128)(2,1)}, u32[]{:S(2)}, u32[]{:S(2)}) async-start(bf16[128,4,4096]{2,1,0:T(4,128)(2,1)} %reshape.101), calls=%async_computation.1 | async-start | bytes 8388608 | tf_op jit(solution)/shard_map/all_to_all | solution.py:10
  114.4 5.3 %copy-start.8 = (bf16[512,4096]{1,0:T(8,128)(2,1)S(1)}, bf16[512,4096]{1,0:T(8,128)(2,1)}, u32[]{:S(2)}) copy-start(bf16[512,4096]{1,0:T(8,128)(2,1)} %reshape.100) | copy-start | bytes 12582916
  114.4 5.3 %copy-start.16 = (bf16[512,768]{1,0:T(8,128)(2,1)S(1)}, bf16[512,768]{1,0:T(8,128)(2,1)}, u32[]{:S(2)}) copy-start(bf16[512,768]{1,0:T(8,128)(2,1)} %copy-done.15) | copy-start | bytes 2359300
  119.6 3.6 %copy-start.14 = (bf16[512,768]{1,0:T(8,128)(2,1)S(1)}, bf16[512,768]{1,0:T(8,128)(2,1)}, u32[]{:S(2)}) copy-start(bf16[512,768]{1,0:T(8,128)(2,1)} %copy-done.13) | copy-start | bytes 2359300
  172.3 3.4 %copy-start.2 = (bf16[512,4096]{1,0:T(8,128)(2,1)S(1)}, bf16[512,4096]{1,0:T(8,128)(2,1)}, u32[]{:S(2)}) copy-start(bf16[512,4096]{1,0:T(8,128)(2,1)} %reshape.102) | copy-start | bytes 12582916
  175.8 1.3 copy-start.3
  175.8 1.4 copy-start.5
  175.8 2.0 copy-start.6
  177.7 1.3 copy-start.4
  179.1 3.7 %collective-permute-start = (f32[2048]{0:T(1024)S(1)}, f32[2048]{0:T(1024)S(1)}, u32[]{:S(2)}, u32[]{:S(2)}) collective-permute-start(f32[2048]{0:T(1024)S(1)} %get-tuple-element.16), channel_id=1, source_target_pairs={{0,1},{1,0},{2,3},{3,2},{4,5},{5,4},{6,7},{7,6},{8,9},{9,8},{10,11... | collective-permute-start | bytes 24584 | tf_op jit(solution)/shard_map/ppermute | solution.py:26
  179.9 3.7 %collective-permute-start.1 = (f32[2048]{0:T(1024)S(1)}, f32[2048]{0:T(1024)S(1)}, u32[]{:S(2)}, u32[]{:S(2)}) collective-permute-start(f32[2048]{0:T(1024)S(1)} %get-tuple-element.16), channel_id=1, source_target_pairs={{0,2},{1,3},{2,0},{3,1},{4,6},{5,7},{6,4},{7,5},{8,10},{9,11},{10,... | collective-permute-start | bytes 24584 | tf_op jit(solution)/shard_map/ppermute | solution.py:26
  180.8 4.5 %collective-permute-start.2 = (f32[2048]{0:T(1024)S(1)}, f32[2048]{0:T(1024)S(1)}, u32[]{:S(2)}, u32[]{:S(2)}) collective-permute-start(f32[2048]{0:T(1024)S(1)} %get-tuple-element.16), channel_id=1, source_target_pairs={{0,3},{1,2},{2,1},{3,0},{4,7},{5,6},{6,5},{7,4},{8,11},{9,10},{10,... | collective-permute-start | bytes 24584 | tf_op jit(solution)/shard_map/ppermute | solution.py:26
  185.4 5.2 %collective-permute-start.3 = (f32[2048]{0:T(1024)S(1)}, f32[2048]{0:T(1024)S(1)}, u32[]{:S(2)}, u32[]{:S(2)}) collective-permute-start(f32[2048]{0:T(1024)S(1)} %add_add_fusion.2), channel_id=1, source_target_pairs={{0,4},{1,5},{2,6},{3,7},{4,0},{5,1},{6,2},{7,3},{8,12},{9,13},{10,... | collective-permute-start | bytes 24584 | tf_op jit(solution)/shard_map/ppermute | solution.py:26
  187.4 3.2 %collective-permute-start.4 = (f32[2048]{0:T(1024)S(1)}, f32[2048]{0:T(1024)S(1)}, u32[]{:S(2)}, u32[]{:S(2)}) collective-permute-start(f32[2048]{0:T(1024)S(1)} %add_add_fusion.2), channel_id=1, source_target_pairs={{0,8},{1,9},{2,10},{3,11},{4,12},{5,13},{6,14},{7,15},{8,0},{9,1},... | collective-permute-start | bytes 24584 | tf_op jit(solution)/shard_map/ppermute | solution.py:26
  187.4 4.6 %collective-permute-start.5 = (f32[2048]{0:T(1024)S(1)}, f32[2048]{0:T(1024)S(1)}, u32[]{:S(2)}, u32[]{:S(2)}) collective-permute-start(f32[2048]{0:T(1024)S(1)} %add_add_fusion.2), channel_id=1, source_target_pairs={{0,12},{1,13},{2,14},{3,15},{4,8},{5,9},{6,10},{7,11},{8,4},{9,5},... | collective-permute-start | bytes 24584 | tf_op jit(solution)/shard_map/ppermute | solution.py:26
  192.0 8.8 %collective-permute-start.6 = (f32[2048]{0:T(1024)S(1)}, f32[2048]{0:T(1024)S(1)}, u32[]{:S(2)}, u32[]{:S(2)}) collective-permute-start(f32[2048]{0:T(1024)S(1)} %add_add_fusion.1), channel_id=1, source_target_pairs={{0,16},{1,17},{2,18},{3,19},{4,20},{5,21},{6,22},{7,23},{8,24},{9,... | collective-permute-start | bytes 24584 | tf_op jit(solution)/shard_map/ppermute | solution.py:26
  192.6 8.3 %collective-permute-start.7 = (f32[2048]{0:T(1024)S(1)}, f32[2048]{0:T(1024)S(1)}, u32[]{:S(2)}, u32[]{:S(2)}) collective-permute-start(f32[2048]{0:T(1024)S(1)} %add_add_fusion.1), channel_id=1, source_target_pairs={{0,32},{1,33},{2,34},{3,35},{4,36},{5,37},{6,38},{7,39},{8,40},{9,... | collective-permute-start | bytes 24584 | tf_op jit(solution)/shard_map/ppermute | solution.py:26
  195.3 5.5 %collective-permute-start.8 = (f32[2048]{0:T(1024)S(1)}, f32[2048]{0:T(1024)S(1)}, u32[]{:S(2)}, u32[]{:S(2)}) collective-permute-start(f32[2048]{0:T(1024)S(1)} %add_add_fusion.1), channel_id=1, source_target_pairs={{0,48},{1,49},{2,50},{3,51},{4,52},{5,53},{6,54},{7,55},{8,56},{9,... | collective-permute-start | bytes 24584 | tf_op jit(solution)/shard_map/ppermute | solution.py:26
  196.8 9.9 %copy-start.1 = (bf16[1,2048,768]{2,1,0:T(8,128)(2,1)S(1)}, bf16[1,2048,768]{2,1,0:T(8,128)(2,1)}, u32[]{:S(2)}) copy-start(bf16[1,2048,768]{2,1,0:T(8,128)(2,1)} %param.13) | copy-start | bytes 9437188
  200.9 5.2 %collective-permute-start.9 = (f32[2048]{0:T(1024)S(1)}, f32[2048]{0:T(1024)S(1)}, u32[]{:S(2)}, u32[]{:S(2)}) collective-permute-start(f32[2048]{0:T(1024)S(1)} %add_add_fusion), channel_id=1, source_target_pairs={{0,64},{1,65},{2,66},{3,67},{4,68},{5,69},{6,70},{7,71},{8,72},{9,... | collective-permute-start | bytes 24584 | tf_op jit(solution)/shard_map/ppermute | solution.py:26

commit v2 on v1

--- a/solution.py
+++ b/solution.py
@@ -96,26 +96,22 @@
     expert_out, grad_back, grad_gate, grad_up, grad_down = expert_pass(
         arrived, arrived_grad, w_gate[0], w_up[0], w_down[0]
     )
-    back = jnp.concatenate([expert_out, grad_back], axis=1).reshape(
-        devices_all, capacity, 2 * width
+    returned_grad, grad_gate, grad_up, grad_down = lax.optimization_barrier(
+        (exchange(grad_back.reshape(devices_all, capacity, width)), grad_gate, grad_up, grad_down)
     )
-    returned, grad_gate, grad_up, grad_down = lax.optimization_barrier(
-        (exchange(back), grad_gate, grad_up, grad_down)
-    )
-    returned = returned.reshape(slots, 2 * width)
-    picked = [
-        contract(select_tk[:, k, :], returned, 1, 0) for k in range(top_count)
-    ]
-    outs = [p[:, :width] for p in picked]
-    backs = [p[:, width:] for p in picked]
+    returned_grad = returned_grad.reshape(slots, width)
+    returned_grad, expert_out = lax.optimization_barrier((returned_grad, expert_out))
+    returned = exchange(expert_out.reshape(devices_all, capacity, width)).reshape(slots, width)
+    backs = [contract(select_tk[:, k, :], returned_grad, 1, 0) for k in range(top_count)]
+    outs = [contract(select_tk[:, k, :], returned, 1, 0) for k in range(top_count)]
+    grad_normed = backs[0]
+    for k in range(1, top_count):
+        grad_normed = grad_normed + backs[k]
     combined = gate_probs[:, 0:1] * outs[0]
     for k in range(1, top_count):
         combined = combined + gate_probs[:, k : k + 1] * outs[k]
     mixed = (inputs + combined).astype(jnp.bfloat16)
     grad_probs = jnp.stack([jnp.sum(grad_in * o, axis=1) for o in outs], axis=1)
-    grad_normed = backs[0]
-    for k in range(1, top_count):
-        grad_normed = grad_normed + backs[k]
     gain_part = jnp.sum(grad_normed * normed, axis=0)
     grad_gain = all_sum(gain_part, devices_all)
     grad_scaled = grad_normed * norm_gain

time: 208 us -> 207 us (level)
  starting transfers between devices: 21.2 us -> 30.6 us
  waiting for transfers between devices: 47 us -> 39 us
  other arithmetic: 12.5 us -> 5.57 us
  matrix products: 32.8 us -> 38.9 us
    all_to_all x1 -> x2, waiting for transfers between devices: 38.7 us -> 13.2 us  [exchange(): return lax.all_to_all(rows, AXES, split_axis=0, concat_axis=0, tiled=True)]
    ppermute x10, waiting for transfers between devices: 8.31 us -> 25.8 us  [all_sum(): lax.ppermute(total, AXES, [(i, i ^ x * step) for i in range(devices_all)])]
    all_to_all x1 -> x2, starting transfers between devices: 7.13 us -> 13.1 us  [exchange(): return lax.all_to_all(rows, AXES, split_axis=0, concat_axis=0, tiled=True)]
    convert_element_type x1 -> x0, other arithmetic: 4.06 us -> none  [on_device(): grad_tokens = (grad_in + inverse_rms * (grad_scaled - normed * jnp.mean(g...]
    ppermute x10, starting transfers between devices: 14 us -> 17.5 us  [all_sum(): lax.ppermute(total, AXES, [(i, i ^ x * step) for i in range(devices_all)])]
    dot_general x1, matrix products: 1.82 us -> 4.45 us  [expert_pass(): pre_gate = jnp.dot(arrived, gate_matrix, preferred_element_type=jnp.float32)]
    concatenate x1 -> x0, other arithmetic: 2.48 us -> none  [on_device(): jnp.concatenate([expert_out, grad_back], axis=1)]
    dot_general x8 -> x10, matrix products: 24.3 us -> 25.2 us  [contract(): lax.dot_general(left, right, (((left_dim,), (right_dim,)), ((), ())), pre...]
  transfers between devices with their start and end apart: 11 -> 12, of which waited for: 7 -> 8; matrix products, arithmetic and copies ran while one was open for 8% -> 9% of each run, Pallas kernels for 0% -> 0%
where the time goes in v2:
time: 207 us; the launch traced here: 206 us
  blocking collectives  63 us (30%)
  waiting for transfers between devices  39 us (19%)
  matrix products  38.9 us (19%)
  starting transfers between devices  30.6 us (15%)
  local copies, waits for them, and re-layouts  28.3 us (14%)
  other arithmetic  5.57 us (3%)
    all_to_all x1, blocking collectives, exchange(): return lax.all_to_all(rows, AXES, split_axis=0, concat_axis=0, tiled=True)  63 us
    ppermute x10, waiting for transfers between devices, all_sum(): lax.ppermute(total, AXES, [(i, i ^ x * step) for i in range(devices_all)])  25.8 us
    dot_general x10, matrix products, contract(): lax.dot_general(left, right, (((left_dim,), (right_dim,)), ((), ())), pre...  25.2 us
    ppermute x10, starting transfers between devices, all_sum(): lax.ppermute(total, AXES, [(i, i ^ x * step) for i in range(devices_all)])  17.5 us
    all_to_all x2, waiting for transfers between devices, exchange(): return lax.all_to_all(rows, AXES, split_axis=0, concat_axis=0, tiled=True)  13.2 us
    all_to_all x2, starting transfers between devices, exchange(): return lax.all_to_all(rows, AXES, split_axis=0, concat_axis=0, tiled=True)  13.1 us
    reshape x1, local copies, waits for them, and re-layouts, on_device(): arrived_all = exchange(sent).reshape(slots, 2 * width)  6.91 us
    dot_general x1, matrix products, expert_pass(): pre_gate = jnp.dot(arrived, gate_matrix, preferred_element_type=jnp.float32)  4.45 us
  transfers between devices with their start and end apart: 12, of which 8 were waited for; matrix products, arithmetic and copies ran while one was open for 9% of the time, Pallas kernels for 0%

profile of v2, /device:TPU:0, one launch (start us, length us, event | category | flops | bytes accessed | tf_op | source)
XLA Modules:
  0.0 206.4 jit_solution(4408299161992975956)
XLA Ops:
  0.6 0.0 copy-start
  0.7 0.9 copy.37
  1.6 0.1 eq.62
  1.8 0.1 eq.58
  1.9 2.1 %convert_element_type.67 = f32[128,2048]{1,0:T(8,128)} convert(bf16[128,2048]{1,0:T(8,128)(2,1)} %param.15) | non-fusion elementwise | flops 262144 | bytes 1572864 | tf_op jit(solution)/shard_map/convert_element_type | solution.py:84
  4.0 0.1 copy.39
  4.1 0.2 fusion.51
  4.4 0.2 fusion.53
  4.6 0.1 reduce_sum.69
  4.8 0.1 copy.41
  4.8 1.3 fusion.35
  6.1 0.1 convert_reduce_fusion
  6.2 0.1 copy.42
  6.4 2.1 %bitcast_convert_fusion = bf16[128,4,2048]{2,0,1:T(8,128)(2,1)S(1)} fusion(f32[128,2048]{1,0:T(8,128)} %convert_element_type.67, f32[128,2]{0,1:T(2,128)S(1)} %copy-done.12, s32[128,4]{0,1:T(4,128)S(1)} %multiply_add_fusion, s32[128,2]{0,1:T(2,128)S(1)} %multiply_add_fusion.1), kind=kOutput, calls=%fused_computation.1 | convolution fusion | flops 539099136 | bytes 3149824 | tf_op jit(solution)/shard_map/dot_general | solution.py:89
  8.5 0.8 convolution_convert_fusion.3
  9.3 0.3 pad_maximum_fusion
  9.6 3.2 %copy.44 = bf16[128,4,4096]{2,1,0:T(4,128)(2,1)S(1)} copy(bf16[128,4,4096]{2,0,1:T(8,128)(2,1)S(1)} %pad_maximum_fusion) | data formatting | bytes 8388608 | tf_op jit(solution)/shard_map/concatenate | solution.py:92
  12.8 63.0 %all_to_all.15 = bf16[128,4,4096]{2,1,0:T(4,128)(2,1)} all-to-all(bf16[128,4,4096]{2,1,0:T(4,128)(2,1)S(1)} %copy.44), channel_id=1, replica_groups=mesh['expert'=16,'dp'=8] {'expert','dp'}, dimensions={0} | all-to-all | bytes 8388608 | tf_op jit(solution)/shard_map/all_to_all | solution.py:10
  75.8 6.9 %reshape.106 = bf16[512,4096]{1,0:T(8,128)(2,1)} reshape(bf16[128,4,4096]{2,1,0:T(4,128)(2,1)} %all_to_all.15) | data formatting | bytes 8388608 | tf_op jit(solution)/shard_map/reshape | solution.py:93
  82.7 4.5 %fusion.2 = f32[512,768]{1,0:T(8,128)S(1)} fusion(bf16[1,2048,768]{2,1,0:T(8,128)(2,1)} %param.12, bf16[512,4096]{1,0:T(8,128)(2,1)} %reshape.106), kind=kOutput, calls=%fused_computation.8 | convolution fusion | flops 1610612736 | bytes 6815744 | tf_op jit(solution)/shard_map/dot_general | solution.py:40
  87.2 0.3 copy-done.14
  87.4 1.8 fusion.10
  89.3 3.2 %multiply_convert_fusion.1 = (bf16[512,768]{1,0:T(8,128)(2,1)}, bf16[512,768]{1,0:T(8,128)(2,1)S(1)}, bf16[512,768]{1,0:T(8,128)(2,1)S(1)}) fusion(f32[512,768]{1,0:T(8,128)S(1)} %fusion.2, f32[512,768]{1,0:T(8,128)S(1)} %fusion.10, bf16[1,2048,768]{2,1,0:T(8,128)(2,1)S(1)} %copy-done, bf16[512,4096]{1,0:T(8,128)(2,1)S(1)} %copy-done.6), kind=kOutput, calls=%fused_computation.24 | convolution fusion | flops 1616510976 | bytes 10747904 | tf_op jit(solution)/shard_map/dot_general | solution.py:41
  92.5 1.8 fusion
  94.4 3.2 %add_convert_fusion = bf16[512,2048]{1,0:T(8,128)(2,1)} fusion(f32[512,2048]{1,0:T(8,128)S(1)} %fusion, bf16[512,768]{1,0:T(8,128)(2,1)S(1)} %get-tuple-element.25, bf16[1,2048,768]{2,1,0:T(8,128)(2,1)S(1)} %copy-done), kind=kOutput, calls=%fused_computation.2 | convolution fusion | flops 1612709888 | bytes 10223616 | tf_op jit(solution)/shard_map/dot_general | solution.py:14
  97.6 4.1 %reshape.107 = bf16[128,4,2048]{2,1,0:T(4,128)(2,1)} reshape(bf16[512,2048]{1,0:T(8,128)(2,1)} %add_convert_fusion) | data formatting | bytes 4194304 | tf_op jit(solution)/shard_map/reshape | solution.py:100
  101.7 7.1 %all-to-all-start.1 = ((bf16[128,4,2048]{2,1,0:T(4,128)(2,1)}), bf16[128,4,2048]{2,1,0:T(4,128)(2,1)}, u32[]{:S(2)}, u32[]{:S(2)}) async-start(bf16[128,4,2048]{2,1,0:T(4,128)(2,1)} %reshape.107), calls=%async_computation.1 | async-start | bytes 4194304 | tf_op jit(solution)/shard_map/all_to_all | solution.py:10
  108.9 5.2 %convolution_convert_fusion = bf16[768,2048]{1,0:T(8,128)(2,1)} fusion(bf16[512,768]{1,0:T(8,128)(2,1)S(1)} %copy-done.20, bf16[512,4096]{1,0:T(8,128)(2,1)} %reshape.106), kind=kOutput, calls=%fused_computation.3 | convolution fusion | flops 1612185600 | bytes 6029312 | tf_op jit(solution)/shard_map/dot_general | solution.py:14
  114.1 3.5 %convolution_convert_fusion.2 = bf16[2048,768]{1,0:T(8,128)(2,1)} fusion(bf16[512,768]{1,0:T(8,128)(2,1)S(1)} %copy-done.19, bf16[512,4096]{1,0:T(8,128)(2,1)S(1)} %copy-done.7), kind=kOutput, calls=%fused_computation.5 | convolution fusion | flops 1612185600 | bytes 6029312 | tf_op jit(solution)/shard_map/dot_general | solution.py:14
  117.6 3.5 %convolution_convert_fusion.1 = bf16[2048,768]{1,0:T(8,128)(2,1)} fusion(bf16[512,768]{1,0:T(8,128)(2,1)S(1)} %copy-done.17, bf16[512,4096]{1,0:T(8,128)(2,1)S(1)} %copy-done.7), kind=kOutput, calls=%fused_computation.4 | convolution fusion | flops 1612185600 | bytes 6029312 | tf_op jit(solution)/shard_map/dot_general | solution.py:14
  121.2 3.1 %fusion.12 = bf16[512,2048]{1,0:T(8,128)(2,1)} fusion(bf16[512,768]{1,0:T(8,128)(2,1)S(1)} %copy-done.21, bf16[1,768,2048]{2,1,0:T(8,128)(2,1)S(1)} %copy-done.15), kind=kOutput, calls=%fused_computation.19 | convolution fusion | flops 1611661312 | bytes 6029312 | tf_op jit(solution)/shard_map/dot_general | solution.py:45
  124.3 13.2 %all-to-all-done.1 = bf16[128,4,2048]{2,1,0:T(4,128)(2,1)} async-done(((bf16[128,4,2048]{2,1,0:T(4,128)(2,1)}), bf16[128,4,2048]{2,1,0:T(4,128)(2,1)}, u32[]{:S(2)}, u32[]{:S(2)}) %all-to-all-start.1) | async-done | bytes 2097184 | tf_op jit(solution)/shard_map/all_to_all | solution.py:10
  137.6 2.5 %reshape.108 = bf16[512,2048]{1,0:T(8,128)(2,1)S(1)} reshape(bf16[128,4,2048]{2,1,0:T(4,128)(2,1)} %all-to-all-done.1) | data formatting | bytes 4194304 | tf_op jit(solution)/shard_map/reshape | solution.py:102
  140.1 4.1 %reshape.109 = bf16[128,4,2048]{2,1,0:T(4,128)(2,1)} reshape(bf16[512,2048]{1,0:T(8,128)(2,1)} %fusion.12) | data formatting | bytes 4194304 | tf_op jit(solution)/shard_map/reshape | solution.py:104
  144.2 6.0 %all-to-all-start.2 = ((bf16[128,4,2048]{2,1,0:T(4,128)(2,1)}), bf16[128,4,2048]{2,1,0:T(4,128)(2,1)}, u32[]{:S(2)}, u32[]{:S(2)}) async-start(bf16[128,4,2048]{2,1,0:T(4,128)(2,1)} %reshape.109), calls=%async_computation.2 | async-start | bytes 4194304 | tf_op jit(solution)/shard_map/all_to_all | solution.py:10
  150.3 0.1 iota_compare_fusion
  150.4 0.4 fusion.48
  150.9 0.4 copy-done.4
  151.3 1.6 fusion.30
  152.9 0.9 collective-permute-start.1
  153.7 1.6 collective-permute-start.2
  155.3 1.0 collective-permute-start
  156.3 10.8 %collective-permute-done.1 = f32[2048]{0:T(1024)S(1)} collective-permute-done((f32[2048]{0:T(1024)S(1)}, f32[2048]{0:T(1024)S(1)}, u32[]{:S(2)}, u32[]{:S(2)}) %collective-permute-start.1) | collective-permute-done | bytes 8224 | tf_op jit(solution)/shard_map/ppermute | solution.py:26
  167.2 3.9 %collective-permute-done.2 = f32[2048]{0:T(1024)S(1)} collective-permute-done((f32[2048]{0:T(1024)S(1)}, f32[2048]{0:T(1024)S(1)}, u32[]{:S(2)}, u32[]{:S(2)}) %collective-permute-start.2) | collective-permute-done | bytes 8224 | tf_op jit(solution)/shard_map/ppermute | solution.py:26
  171.1 0.1 collective-permute-start.4
  171.2 3.8 %collective-permute-start.5 = (f32[2048]{0:T(1024)S(1)}, f32[2048]{0:T(1024)S(1)}, u32[]{:S(2)}, u32[]{:S(2)}) collective-permute-start(f32[2048]{0:T(1024)S(1)} %add_add_fusion.2), channel_id=1, source_target_pairs={{0,12},{1,13},{2,14},{3,15},{4,8},{5,9},{6,10},{7,11},{8,4},{9,5},... | collective-permute-start | bytes 24584 | tf_op jit(solution)/shard_map/ppermute | solution.py:26
  174.9 0.1 collective-permute-start.3
  175.0 1.3 collective-permute-done.5
  176.3 3.8 %collective-permute-done.3 = f32[2048]{0:T(1024)S(1)} collective-permute-done((f32[2048]{0:T(1024)S(1)}, f32[2048]{0:T(1024)S(1)}, u32[]{:S(2)}, u32[]{:S(2)}) %collective-permute-start.3) | collective-permute-done | bytes 8224 | tf_op jit(solution)/shard_map/ppermute | solution.py:26
  180.1 6.0 %collective-permute-start.7 = (f32[2048]{0:T(1024)S(1)}, f32[2048]{0:T(1024)S(1)}, u32[]{:S(2)}, u32[]{:S(2)}) collective-permute-start(f32[2048]{0:T(1024)S(1)} %add_add_fusion.1), channel_id=1, source_target_pairs={{0,32},{1,33},{2,34},{3,35},{4,36},{5,37},{6,38},{7,39},{8,40},{9,... | collective-permute-start | bytes 24584 | tf_op jit(solution)/shard_map/ppermute | solution.py:26
  186.1 0.8 collective-permute-start.8
  186.9 0.8 collective-permute-done.7
  187.7 3.2 %collective-permute-done.8 = f32[2048]{0:T(1024)S(1)} collective-permute-done((f32[2048]{0:T(1024)S(1)}, f32[2048]{0:T(1024)S(1)}, u32[]{:S(2)}, u32[]{:S(2)}) %collective-permute-start.8) | collective-permute-done | bytes 8224 | tf_op jit(solution)/shard_map/ppermute | solution.py:26
  191.0 3.3 %collective-permute-start.9 = (f32[2048]{0:T(1024)S(1)}, f32[2048]{0:T(1024)S(1)}, u32[]{:S(2)}, u32[]{:S(2)}) collective-permute-start(f32[2048]{0:T(1024)S(1)} %add_add_fusion), channel_id=1, source_target_pairs={{0,64},{1,65},{2,66},{3,67},{4,68},{5,69},{6,70},{7,71},{8,72},{9,... | collective-permute-start | bytes 24584 | tf_op jit(solution)/shard_map/ppermute | solution.py:26
  194.3 1.9 collective-permute-done.9
  196.2 0.6 select_add_fusion
  196.8 2.5 %reshape.110 = bf16[512,2048]{1,0:T(8,128)(2,1)S(1)} reshape(bf16[128,4,2048]{2,1,0:T(4,128)(2,1)} %all-to-all-done.2) | data formatting | bytes 4194304 | tf_op jit(solution)/shard_map/reshape | solution.py:104
  199.3 1.3 copy-done.2
  200.7 0.4 fusion.50
  201.1 0.6 copy-done.5
  201.7 0.3 copy-done.8
  202.1 0.1 copy-done.9
  202.2 3.6 %multiply_reduce_fusion.1 = (f32[128]{0:T(128)S(1)}, f32[128]{0:T(128)S(1)}, bf16[128,2048]{1,0:T(8,128)(2,1)}, bf16[128,2048]{1,0:T(8,128)(2,1)}) fusion(bf16[128,2048]{1,0:T(8,128)(2,1)S(1)} %copy-done.9, f32[128,2048]{1,0:T(8,128)S(1)} %fusion.50, f32[128]{0:T(128)S(1)} %get-tuple-element.29, f32[128]{0:T(128)S(1)} %get-tuple-element.28, ...), kind=kOutput, calls=%fused_computation.51 | convolution fusion | flops 273153792 | bytes 6368256 | tf_op jit(solution)/shard_map/dot_general | solution.py:14
  205.8 0.6 pad_maximum_fusion.1
  (56 shorter events, 0.2 us)
Async XLA Ops:
  0.6 88.7 %copy-start = (bf16[1,2048,768]{2,1,0:T(8,128)(2,1)S(1)}, bf16[1,2048,768]{2,1,0:T(8,128)(2,1)}, u32[]{:S(2)}) copy-start(bf16[1,2048,768]{2,1,0:T(8,128)(2,1)} %param.13) | copy-start | bytes 9437188
  0.6 4.2 %copy-start.11 = (s32[128,2]{0,1:T(2,128)S(1)}, s32[128,2]{0,1:T(2,128)}, u32[]{:S(2)}) copy-start(s32[128,2]{0,1:T(2,128)} %param.9) | copy-start | bytes 3076
  0.7 5.7 %copy-start.12 = (f32[128,2]{0,1:T(2,128)S(1)}, f32[128,2]{0,1:T(2,128)}, u32[]{:S(2)}) copy-start(f32[128,2]{0,1:T(2,128)} %param.10) | copy-start | bytes 3076
  4.6 3.8 %copy-start.10 = (f32[2048]{0:T(1024)S(1)}, f32[2048]{0:T(1024)}, u32[]{:S(2)}) copy-start(f32[2048]{0:T(1024)} %param.11) | copy-start | bytes 24580
  6.4 2.1 %copy-start.3 = (bf16[128,2048]{1,0:T(8,128)(2,1)S(1)}, bf16[128,2048]{1,0:T(8,128)(2,1)}, u32[]{:S(2)}) copy-start(bf16[128,2048]{1,0:T(8,128)(2,1)} %param.8) | copy-start | bytes 1572868
  82.7 4.5 %copy-start.6 = (bf16[512,4096]{1,0:T(8,128)(2,1)S(1)}, bf16[512,4096]{1,0:T(8,128)(2,1)}, u32[]{:S(2)}) copy-start(bf16[512,4096]{1,0:T(8,128)(2,1)} %reshape.106) | copy-start | bytes 12582916
  82.7 4.7 %copy-start.14 = (bf16[1,768,2048]{2,1,0:T(8,128)(2,1)S(1)}, bf16[1,768,2048]{2,1,0:T(8,128)(2,1)}, u32[]{:S(2)}) copy-start(bf16[1,768,2048]{2,1,0:T(8,128)(2,1)} %param.14) | copy-start | bytes 9437188
  89.3 3.2 %copy-start.13 = (bf16[1,2048,768]{2,1,0:T(8,128)(2,1)S(1)}, bf16[1,2048,768]{2,1,0:T(8,128)(2,1)}, u32[]{:S(2)}) copy-start(bf16[1,2048,768]{2,1,0:T(8,128)(2,1)} %param.12) | copy-start | bytes 9437188
  92.5 1.8 copy-start.18
  92.5 1.8 copy-start.16
  101.7 7.1 %copy-start.20 = (bf16[512,768]{1,0:T(8,128)(2,1)S(1)}, bf16[512,768]{1,0:T(8,128)(2,1)}, u32[]{:S(2)}) copy-start(bf16[512,768]{1,0:T(8,128)(2,1)} %get-tuple-element.23) | copy-start | bytes 2359300
  101.7 35.9 %all-to-all-start.1 = ((bf16[128,4,2048]{2,1,0:T(4,128)(2,1)}), bf16[128,4,2048]{2,1,0:T(4,128)(2,1)}, u32[]{:S(2)}, u32[]{:S(2)}) async-start(bf16[128,4,2048]{2,1,0:T(4,128)(2,1)} %reshape.107), calls=%async_computation.1 | async-start | bytes 4194304 | tf_op jit(solution)/shard_map/all_to_all | solution.py:10
  108.8 5.3 %copy-start.7 = (bf16[512,4096]{1,0:T(8,128)(2,1)S(1)}, bf16[512,4096]{1,0:T(8,128)(2,1)}, u32[]{:S(2)}) copy-start(bf16[512,4096]{1,0:T(8,128)(2,1)} %reshape.106) | copy-start | bytes 12582916
  108.8 5.3 %copy-start.19 = (bf16[512,768]{1,0:T(8,128)(2,1)S(1)}, bf16[512,768]{1,0:T(8,128)(2,1)}, u32[]{:S(2)}) copy-start(bf16[512,768]{1,0:T(8,128)(2,1)} %copy-done.18) | copy-start | bytes 2359300
  114.1 3.5 %copy-start.17 = (bf16[512,768]{1,0:T(8,128)(2,1)S(1)}, bf16[512,768]{1,0:T(8,128)(2,1)}, u32[]{:S(2)}) copy-start(bf16[512,768]{1,0:T(8,128)(2,1)} %copy-done.16) | copy-start | bytes 2359300
  117.6 3.5 %copy-start.15 = (bf16[1,768,2048]{2,1,0:T(8,128)(2,1)S(1)}, bf16[1,768,2048]{2,1,0:T(8,128)(2,1)}, u32[]{:S(2)}) copy-start(bf16[1,768,2048]{2,1,0:T(8,128)(2,1)} %param.14) | copy-start | bytes 9437188
  117.6 3.5 %copy-start.21 = (bf16[512,768]{1,0:T(8,128)(2,1)S(1)}, bf16[512,768]{1,0:T(8,128)(2,1)}, u32[]{:S(2)}) copy-start(bf16[512,768]{1,0:T(8,128)(2,1)} %get-tuple-element.23) | copy-start | bytes 2359300
  144.2 52.6 %all-to-all-start.2 = ((bf16[128,4,2048]{2,1,0:T(4,128)(2,1)}), bf16[128,4,2048]{2,1,0:T(4,128)(2,1)}, u32[]{:S(2)}, u32[]{:S(2)}) async-start(bf16[128,4,2048]{2,1,0:T(4,128)(2,1)} %reshape.109), calls=%async_computation.2 | async-start | bytes 4194304 | tf_op jit(solution)/shard_map/all_to_all | solution.py:10
  150.2 1.0 copy-start.4
  152.9 14.3 %collective-permute-start.1 = (f32[2048]{0:T(1024)S(1)}, f32[2048]{0:T(1024)S(1)}, u32[]{:S(2)}, u32[]{:S(2)}) collective-permute-start(f32[2048]{0:T(1024)S(1)} %get-tuple-element.20), channel_id=1, source_target_pairs={{0,2},{1,3},{2,0},{3,1},{4,6},{5,7},{6,4},{7,5},{8,10},{9,11},{10,... | collective-permute-start | bytes 24584 | tf_op jit(solution)/shard_map/ppermute | solution.py:26
  153.7 17.3 %collective-permute-start.2 = (f32[2048]{0:T(1024)S(1)}, f32[2048]{0:T(1024)S(1)}, u32[]{:S(2)}, u32[]{:S(2)}) collective-permute-start(f32[2048]{0:T(1024)S(1)} %get-tuple-element.20), channel_id=1, source_target_pairs={{0,3},{1,2},{2,1},{3,0},{4,7},{5,6},{6,5},{7,4},{8,11},{9,10},{10,... | collective-permute-start | bytes 24584 | tf_op jit(solution)/shard_map/ppermute | solution.py:26
  155.3 15.7 %collective-permute-start = (f32[2048]{0:T(1024)S(1)}, f32[2048]{0:T(1024)S(1)}, u32[]{:S(2)}, u32[]{:S(2)}) collective-permute-start(f32[2048]{0:T(1024)S(1)} %get-tuple-element.20), channel_id=1, source_target_pairs={{0,1},{1,0},{2,3},{3,2},{4,5},{5,4},{6,7},{7,6},{8,9},{9,8},{10,11... | collective-permute-start | bytes 24584 | tf_op jit(solution)/shard_map/ppermute | solution.py:26
  171.1 3.9 %collective-permute-start.4 = (f32[2048]{0:T(1024)S(1)}, f32[2048]{0:T(1024)S(1)}, u32[]{:S(2)}, u32[]{:S(2)}) collective-permute-start(f32[2048]{0:T(1024)S(1)} %add_add_fusion.2), channel_id=1, source_target_pairs={{0,8},{1,9},{2,10},{3,11},{4,12},{5,13},{6,14},{7,15},{8,0},{9,1},... | collective-permute-start | bytes 24584 | tf_op jit(solution)/shard_map/ppermute | solution.py:26
  171.2 5.1 %collective-permute-start.5 = (f32[2048]{0:T(1024)S(1)}, f32[2048]{0:T(1024)S(1)}, u32[]{:S(2)}, u32[]{:S(2)}) collective-permute-start(f32[2048]{0:T(1024)S(1)} %add_add_fusion.2), channel_id=1, source_target_pairs={{0,12},{1,13},{2,14},{3,15},{4,8},{5,9},{6,10},{7,11},{8,4},{9,5},... | collective-permute-start | bytes 24584 | tf_op jit(solution)/shard_map/ppermute | solution.py:26
  174.9 5.2 %collective-permute-start.3 = (f32[2048]{0:T(1024)S(1)}, f32[2048]{0:T(1024)S(1)}, u32[]{:S(2)}, u32[]{:S(2)}) collective-permute-start(f32[2048]{0:T(1024)S(1)} %add_add_fusion.2), channel_id=1, source_target_pairs={{0,4},{1,5},{2,6},{3,7},{4,0},{5,1},{6,2},{7,3},{8,12},{9,13},{10,... | collective-permute-start | bytes 24584 | tf_op jit(solution)/shard_map/ppermute | solution.py:26
  180.1 7.6 %collective-permute-start.7 = (f32[2048]{0:T(1024)S(1)}, f32[2048]{0:T(1024)S(1)}, u32[]{:S(2)}, u32[]{:S(2)}) collective-permute-start(f32[2048]{0:T(1024)S(1)} %add_add_fusion.1), channel_id=1, source_target_pairs={{0,32},{1,33},{2,34},{3,35},{4,36},{5,37},{6,38},{7,39},{8,40},{9,... | collective-permute-start | bytes 24584 | tf_op jit(solution)/shard_map/ppermute | solution.py:26
  186.1 4.9 %collective-permute-start.8 = (f32[2048]{0:T(1024)S(1)}, f32[2048]{0:T(1024)S(1)}, u32[]{:S(2)}, u32[]{:S(2)}) collective-permute-start(f32[2048]{0:T(1024)S(1)} %add_add_fusion.1), channel_id=1, source_target_pairs={{0,48},{1,49},{2,50},{3,51},{4,52},{5,53},{6,54},{7,55},{8,56},{9,... | collective-permute-start | bytes 24584 | tf_op jit(solution)/shard_map/ppermute | solution.py:26
  186.9 4.0 %collective-permute-start.6 = (f32[2048]{0:T(1024)S(1)}, f32[2048]{0:T(1024)S(1)}, u32[]{:S(2)}, u32[]{:S(2)}) collective-permute-start(f32[2048]{0:T(1024)S(1)} %add_add_fusion.1), channel_id=1, source_target_pairs={{0,16},{1,17},{2,18},{3,19},{4,20},{5,21},{6,22},{7,23},{8,24},{9,... | collective-permute-start | bytes 24584 | tf_op jit(solution)/shard_map/ppermute | solution.py:26
  191.0 5.2 %collective-permute-start.9 = (f32[2048]{0:T(1024)S(1)}, f32[2048]{0:T(1024)S(1)}, u32[]{:S(2)}, u32[]{:S(2)}) collective-permute-start(f32[2048]{0:T(1024)S(1)} %add_add_fusion), channel_id=1, source_target_pairs={{0,64},{1,65},{2,66},{3,67},{4,68},{5,69},{6,70},{7,71},{8,72},{9,... | collective-permute-start | bytes 24584 | tf_op jit(solution)/shard_map/ppermute | solution.py:26
  199.3 1.3 copy-start.2
  200.7 1.0 copy-start.5
  200.7 1.4 copy-start.8
  200.7 1.5 copy-start.9
  201.1 5.2 %copy-start.1 = (bf16[1,2048,768]{2,1,0:T(8,128)(2,1)S(1)}, bf16[1,2048,768]{2,1,0:T(8,128)(2,1)}, u32[]{:S(2)}) copy-start(bf16[1,2048,768]{2,1,0:T(8,128)(2,1)} %param.13) | copy-start | bytes 9437188

commit v3 on v1

--- a/solution.py
+++ b/solution.py
@@ -69,7 +69,6 @@
     inputs = tokens.astype(jnp.float32)
     inverse_rms = lax.rsqrt(jnp.mean(inputs * inputs, axis=1, keepdims=True) + 1e-06)
     normed = inputs * inverse_rms
-    scaled = (normed * norm_gain).astype(jnp.bfloat16)
     flat_ids = routes.reshape(assigned)
     onehot = (flat_ids[:, None] == jnp.arange(devices_all, dtype=jnp.int32)[None, :]).astype(
         jnp.int32
@@ -85,16 +84,24 @@
     grad_rows = (gate_probs[:, :, None] * grad_in[:, None, :]).astype(jnp.bfloat16)
     sel_tok3 = select_tok.reshape(tok_rows, devices_all, capacity)
     sel_tk3 = select_tk.reshape(tok_rows, top_count, devices_all, capacity)
-    send_scaled = lax.dot_general(sel_tok3, scaled, (((0,), (0,)), ((), ())), preferred_element_type=jnp.float32).astype(jnp.bfloat16)
+    send_scaled = lax.dot_general(sel_tok3, tokens, (((0,), (0,)), ((), ())), preferred_element_type=jnp.float32).astype(jnp.bfloat16)
     send_grad = lax.dot_general(
         sel_tk3, grad_rows, (((0, 1), (0, 1)), ((), ())), preferred_element_type=jnp.float32
     ).astype(jnp.bfloat16)
     sent = jnp.concatenate([send_scaled, send_grad], axis=2)
     arrived_all = exchange(sent).reshape(slots, 2 * width)
-    arrived = arrived_all[:, :width]
+    arrived_inputs = arrived_all[:, :width].astype(jnp.float32)
+    arrived_rms = lax.rsqrt(
+        jnp.mean(arrived_inputs * arrived_inputs, axis=1, keepdims=True) + 1e-06
+    )
+    arrived_normed = arrived_inputs * arrived_rms
+    arrived = (arrived_normed * norm_gain).astype(jnp.bfloat16)
     arrived_grad = arrived_all[:, width:]
     expert_out, grad_back, grad_gate, grad_up, grad_down = expert_pass(
         arrived, arrived_grad, w_gate[0], w_up[0], w_down[0]
+    )
+    grad_gain = all_sum(
+        jnp.sum(grad_back.astype(jnp.float32) * arrived_normed, axis=0), devices_all
     )
     back = jnp.concatenate([expert_out, grad_back], axis=1).reshape(
         devices_all, capacity, 2 * width
@@ -116,8 +123,6 @@
     grad_normed = backs[0]
     for k in range(1, top_count):
         grad_normed = grad_normed + backs[k]
-    gain_part = jnp.sum(grad_normed * normed, axis=0)
-    grad_gain = all_sum(gain_part, devices_all)
     grad_scaled = grad_normed * norm_gain
     grad_tokens = (
         grad_in

time: 208 us -> 206 us (level)
    all_to_all x1, waiting for transfers between devices: 38.7 us -> 0.01 us  [exchange(): return lax.all_to_all(rows, AXES, split_axis=0, concat_axis=0, tiled=True)]
    ppermute x10, waiting for transfers between devices: 8.31 us -> 45.5 us  [all_sum(): lax.ppermute(total, AXES, [(i, i ^ x * step) for i in range(devices_all)])]
    convert_element_type x1, other arithmetic: 4.06 us -> 1.45 us  [on_device(): grad_tokens = (grad_in + inverse_rms * (grad_scaled - normed * jnp.mean(g...]
  transfers between devices with their start and end apart: 11 -> 11, of which waited for: 7 -> 3; matrix products, arithmetic and copies ran while one was open for 8% -> 7% of each run, Pallas kernels for 0% -> 0%
where the time goes in v3:
time: 206 us; the launch traced here: 205 us
  blocking collectives  63 us (31%)
  waiting for transfers between devices  45.5 us (22%)
  matrix products  33.2 us (16%)
  local copies, waits for them, and re-layouts  28.5 us (14%)
  starting transfers between devices  22.3 us (11%)
  other arithmetic  11.8 us (6%)
    all_to_all x1, blocking collectives, exchange(): return lax.all_to_all(rows, AXES, split_axis=0, concat_axis=0, tiled=True)  63 us
    ppermute x10, waiting for transfers between devices, all_sum(): lax.ppermute(total, AXES, [(i, i ^ x * step) for i in range(devices_all)])  45.5 us
    dot_general x8, matrix products, contract(): lax.dot_general(left, right, (((left_dim,), (right_dim,)), ((), ())), pre...  24.5 us
    ppermute x10, starting transfers between devices, all_sum(): lax.ppermute(total, AXES, [(i, i ^ x * step) for i in range(devices_all)])  15.4 us
    reshape x1, local copies, waits for them, and re-layouts, on_device(): jnp.concatenate([expert_out, grad_back], axis=1)  7.21 us
    all_to_all x1, starting transfers between devices, exchange(): return lax.all_to_all(rows, AXES, split_axis=0, concat_axis=0, tiled=True)  6.91 us
    reshape x1, local copies, waits for them, and re-layouts, on_device(): returned = returned.reshape(slots, 2 * width)  6.89 us
    reshape x1, local copies, waits for them, and re-layouts, on_device(): arrived_all = exchange(sent).reshape(slots, 2 * width)  6.89 us
  transfers between devices with their start and end apart: 11, of which 3 were waited for; matrix products, arithmetic and copies ran while one was open for 7% of the time, Pallas kernels for 0%

profile of v3, /device:TPU:0, one launch (start us, length us, event | category | flops | bytes accessed | tf_op | source)
XLA Modules:
  0.0 205.3 jit_solution(14004332367087498022)
XLA Ops:
  0.6 0.0 copy-start
  0.7 0.9 copy.37
  1.6 0.1 eq.62
  1.7 0.1 eq.58
  1.9 0.1 copy.39
  2.0 0.2 fusion.45
  2.3 0.2 fusion.47
  2.5 0.1 reduce_sum.78
  2.6 0.1 copy.41
  2.7 0.7 multiply_add_fusion.1
  3.4 2.1 %convert_element_type.72 = f32[128,2048]{1,0:T(8,128)} convert(bf16[128,2048]{1,0:T(8,128)(2,1)} %param.15) | non-fusion elementwise | flops 262144 | bytes 1572864 | tf_op jit(solution)/shard_map/convert_element_type | solution.py:83
  5.5 0.1 convert_reduce_fusion
  5.6 0.1 copy.42
  5.8 0.0 copy-start.8
  5.8 1.8 convolution_convert_fusion.3
  7.6 0.8 bitcast_convert_fusion
  8.4 0.3 pad_maximum_fusion
  8.7 3.2 %copy.44 = bf16[128,4,4096]{2,1,0:T(4,128)(2,1)S(1)} copy(bf16[128,4,4096]{2,0,1:T(8,128)(2,1)S(1)} %pad_maximum_fusion) | data formatting | bytes 8388608 | tf_op jit(solution)/shard_map/concatenate | solution.py:91
  12.0 63.0 %all_to_all.10 = bf16[128,4,4096]{2,1,0:T(4,128)(2,1)} all-to-all(bf16[128,4,4096]{2,1,0:T(4,128)(2,1)S(1)} %copy.44), channel_id=1, replica_groups=mesh['expert'=16,'dp'=8] {'expert','dp'}, dimensions={0} | all-to-all | bytes 8388608 | tf_op jit(solution)/shard_map/all_to_all | solution.py:10
  74.9 6.9 %reshape.108 = bf16[512,4096]{1,0:T(8,128)(2,1)} reshape(bf16[128,4,4096]{2,1,0:T(4,128)(2,1)} %all_to_all.10) | data formatting | bytes 8388608 | tf_op jit(solution)/shard_map/reshape | solution.py:92
  81.8 2.1 %fusion.4 = f32[512]{0:T(512)S(1)} fusion(bf16[512,4096]{1,0:T(8,128)(2,1)} %reshape.108), kind=kLoop, calls=%fused_computation.6 | loop fusion | flops 3145216 | bytes 2099200 | tf_op jit(solution)/shard_map/reduce_sum | solution.py:95
  83.9 0.0 copy-start.9
  83.9 0.0 copy-start.12
  84.0 4.5 %fusion.5 = f32[512,768]{1,0:T(8,128)S(1)} fusion(bf16[1,768,2048]{2,1,0:T(8,128)(2,1)} %param.14, bf16[512,4096]{1,0:T(8,128)(2,1)} %reshape.108), kind=kOutput, calls=%fused_computation.14 | convolution fusion | flops 1610612736 | bytes 6815744 | tf_op jit(solution)/shard_map/dot_general | solution.py:14
  88.5 0.2 copy-done.12
  88.7 1.9 fusion.15
  90.6 2.4 %multiply_convert_fusion.3 = (bf16[512,768]{1,0:T(8,128)(2,1)S(1)}, bf16[512,768]{1,0:T(8,128)(2,1)S(1)}, bf16[512,768]{1,0:T(8,128)(2,1)S(1)}) fusion(f32[512,768]{1,0:T(8,128)S(1)} %fusion.15, f32[512,768]{1,0:T(8,128)S(1)} %fusion.5, bf16[1,2048,768]{2,1,0:T(8,128)(2,1)S(1)} %copy-done, f32[2048]{0:T(1024)S(1)} %copy-done.9, f32[512]{0:T(512)S(1)} %add_rsqrt_fusion, ...), kind=kOutput, calls=%fused_computation.33 | convolution fusion | flops 1620705280 | bytes 10758144 | tf_op jit(solution)/shard_map/dot_general | solution.py:41
  93.0 0.0 copy-start.13
  93.0 0.0 copy-start.11
  93.0 1.8 fusion.9
  94.9 0.9 copy-done.11
  95.7 1.8 fusion.17
  97.6 2.0 fusion.3
  99.5 2.5 %pad_maximum_fusion.1 = bf16[512,4096]{1,0:T(8,128)(2,1)} fusion(bf16[512,2048]{1,0:T(8,128)(2,1)S(1)} %get-tuple-element.26, bf16[512,2048]{1,0:T(8,128)(2,1)S(1)} %fusion.17), kind=kLoop, calls=%fused_computation.8 | loop fusion | flops 8388608 | bytes 8388608 | tf_op jit(solution)/shard_map/concatenate | solution.py:106
  102.0 7.2 %reshape.109 = bf16[128,4,4096]{2,1,0:T(4,128)(2,1)} reshape(bf16[512,4096]{1,0:T(8,128)(2,1)} %pad_maximum_fusion.1) | data formatting | bytes 8388608 | tf_op jit(solution)/shard_map/reshape | solution.py:106
  109.2 6.9 %all-to-all-start.1 = ((bf16[128,4,4096]{2,1,0:T(4,128)(2,1)}), bf16[128,4,4096]{2,1,0:T(4,128)(2,1)}, u32[]{:S(2)}, u32[]{:S(2)}) async-start(bf16[128,4,4096]{2,1,0:T(4,128)(2,1)} %reshape.109), calls=%async_computation.1 | async-start | bytes 8388608 | tf_op jit(solution)/shard_map/all_to_all | solution.py:10
  116.2 0.2 fusion.33
  116.3 0.1 iota_compare_fusion
  116.5 1.1 collective-permute-start
  117.6 1.5 collective-permute-start.1
  119.1 1.0 collective-permute-start.2
  120.1 3.7 %collective-permute-done = f32[2048]{0:T(1024)S(1)} collective-permute-done((f32[2048]{0:T(1024)S(1)}, f32[2048]{0:T(1024)S(1)}, u32[]{:S(2)}, u32[]{:S(2)}) %collective-permute-start) | collective-permute-done | bytes 8224 | tf_op jit(solution)/shard_map/ppermute | solution.py:26
  123.7 33.3 %collective-permute-done.1 = f32[2048]{0:T(1024)S(1)} collective-permute-done((f32[2048]{0:T(1024)S(1)}, f32[2048]{0:T(1024)S(1)}, u32[]{:S(2)}, u32[]{:S(2)}) %collective-permute-start.1) | collective-permute-done | bytes 8224 | tf_op jit(solution)/shard_map/ppermute | solution.py:26
  157.0 8.5 %collective-permute-done.2 = f32[2048]{0:T(1024)S(1)} collective-permute-done((f32[2048]{0:T(1024)S(1)}, f32[2048]{0:T(1024)S(1)}, u32[]{:S(2)}, u32[]{:S(2)}) %collective-permute-start.2) | collective-permute-done | bytes 8224 | tf_op jit(solution)/shard_map/ppermute | solution.py:26
  165.5 0.0 copy-start.14
  165.5 0.7 collective-permute-start.3
  166.2 3.0 %collective-permute-start.5 = (f32[2048]{0:T(1024)S(1)}, f32[2048]{0:T(1024)S(1)}, u32[]{:S(2)}, u32[]{:S(2)}) collective-permute-start(f32[2048]{0:T(1024)S(1)} %add_add_fusion.2), channel_id=1, source_target_pairs={{0,12},{1,13},{2,14},{3,15},{4,8},{5,9},{6,10},{7,11},{8,4},{9,5},... | collective-permute-start | bytes 24584 | tf_op jit(solution)/shard_map/ppermute | solution.py:26
  169.3 5.2 %convolution_convert_fusion.1 = bf16[2048,768]{1,0:T(8,128)(2,1)} fusion(bf16[512,768]{1,0:T(8,128)(2,1)S(1)} %copy-done.16, f32[2048]{0:T(1024)S(1)} %copy-done.9, f32[512]{0:T(512)S(1)} %add_rsqrt_fusion, bf16[512,4096]{1,0:T(8,128)(2,1)} %reshape.108), kind=kOutput, calls=%fused_computation.12 | convolution fusion | flops 1616379904 | bytes 6039552 | tf_op jit(solution)/shard_map/dot_general | solution.py:14
  174.6 0.6 collective-permute-start.6
  175.1 2.3 %collective-permute-start.7 = (f32[2048]{0:T(1024)S(1)}, f32[2048]{0:T(1024)S(1)}, u32[]{:S(2)}, u32[]{:S(2)}) collective-permute-start(f32[2048]{0:T(1024)S(1)} %add_add_fusion.1), channel_id=1, source_target_pairs={{0,32},{1,33},{2,34},{3,35},{4,36},{5,37},{6,38},{7,39},{8,40},{9,... | collective-permute-start | bytes 24584 | tf_op jit(solution)/shard_map/ppermute | solution.py:26
  177.5 1.8 collective-permute-start.8
  179.3 3.7 %convolution_convert_fusion.2 = bf16[2048,768]{1,0:T(8,128)(2,1)} fusion(bf16[512,768]{1,0:T(8,128)(2,1)S(1)} %copy-done.14, f32[2048]{0:T(1024)S(1)} %copy-done.9, f32[512]{0:T(512)S(1)} %add_rsqrt_fusion, bf16[512,4096]{1,0:T(8,128)(2,1)S(1)} %copy-done.4), kind=kOutput, calls=%fused_computation.13 | convolution fusion | flops 1616379904 | bytes 6039552 | tf_op jit(solution)/shard_map/dot_general | solution.py:14
  183.1 3.3 %collective-permute-start.9 = (f32[2048]{0:T(1024)S(1)}, f32[2048]{0:T(1024)S(1)}, u32[]{:S(2)}, u32[]{:S(2)}) collective-permute-start(f32[2048]{0:T(1024)S(1)} %add_add_fusion), channel_id=1, source_target_pairs={{0,64},{1,65},{2,66},{3,67},{4,68},{5,69},{6,70},{7,71},{8,72},{9,... | collective-permute-start | bytes 24584 | tf_op jit(solution)/shard_map/ppermute | solution.py:26
  186.3 3.5 %convolution_convert_fusion = bf16[768,2048]{1,0:T(8,128)(2,1)} fusion(bf16[512,768]{1,0:T(8,128)(2,1)S(1)} %copy-done.18, bf16[512,4096]{1,0:T(8,128)(2,1)S(1)} %copy-done.4), kind=kOutput, calls=%fused_computation.11 | convolution fusion | flops 1612185600 | bytes 6029312 | tf_op jit(solution)/shard_map/dot_general | solution.py:14
  189.9 0.6 select_add_fusion
  190.5 6.9 %reshape.110 = bf16[512,4096]{1,0:T(8,128)(2,1)} reshape(bf16[128,4,4096]{2,1,0:T(4,128)(2,1)} %all-to-all-done.1) | data formatting | bytes 8388608 | tf_op jit(solution)/shard_map/reshape | solution.py:112
  197.4 3.1 %fusion.44 = f32[128,4096]{1,0:T(8,128)S(1)} fusion(bf16[512,4096]{1,0:T(8,128)(2,1)} %reshape.110, pred[128,2,512]{2,0,1:T(32,128)(4,1)S(1)} %iota_compare_fusion), kind=kOutput, calls=%fused_computation.64 | convolution fusion | flops 536870912 | bytes 6356992 | tf_op jit(solution)/shard_map/dot_general | solution.py:14
  200.4 0.4 copy-done.2
  200.8 0.7 fusion.43
  201.6 0.3 copy-done.7
  201.9 0.6 fusion.27
  202.5 0.6 pad_maximum_fusion.2
  203.0 1.4 fusion.31
  204.5 0.8 copy-done.1
  (49 shorter events, 0.2 us)
Async XLA Ops:
  0.6 89.9 %copy-start = (bf16[1,2048,768]{2,1,0:T(8,128)(2,1)S(1)}, bf16[1,2048,768]{2,1,0:T(8,128)(2,1)}, u32[]{:S(2)}) copy-start(bf16[1,2048,768]{2,1,0:T(8,128)(2,1)} %param.13) | copy-start | bytes 9437188
  0.6 7.0 %copy-start.10 = (f32[128,2]{0,1:T(2,128)S(1)}, f32[128,2]{0,1:T(2,128)}, u32[]{:S(2)}) copy-start(f32[128,2]{0,1:T(2,128)} %param.10) | copy-start | bytes 3076
  5.8 1.9 copy-start.8
  83.9 4.5 %copy-start.3 = (bf16[512,4096]{1,0:T(8,128)(2,1)S(1)}, bf16[512,4096]{1,0:T(8,128)(2,1)}, u32[]{:S(2)}) copy-start(bf16[512,4096]{1,0:T(8,128)(2,1)} %reshape.108) | copy-start | bytes 12582916
  83.9 4.5 %copy-start.9 = (f32[2048]{0:T(1024)S(1)}, f32[2048]{0:T(1024)}, u32[]{:S(2)}) copy-start(f32[2048]{0:T(1024)} %param.11) | copy-start | bytes 24580
  83.9 4.7 %copy-start.12 = (bf16[1,2048,768]{2,1,0:T(8,128)(2,1)S(1)}, bf16[1,2048,768]{2,1,0:T(8,128)(2,1)}, u32[]{:S(2)}) copy-start(bf16[1,2048,768]{2,1,0:T(8,128)(2,1)} %param.12) | copy-start | bytes 9437188
  93.0 1.9 copy-start.15
  93.0 1.9 copy-start.17
  93.0 4.6 %copy-start.13 = (bf16[512,768]{1,0:T(8,128)(2,1)}, bf16[512,768]{1,0:T(8,128)(2,1)S(1)}, u32[]{:S(2)}) copy-start(bf16[512,768]{1,0:T(8,128)(2,1)S(1)} %get-tuple-element.21) | copy-start | bytes 2359300
  93.0 2.7 %copy-start.11 = (bf16[1,768,2048]{2,1,0:T(8,128)(2,1)S(1)}, bf16[1,768,2048]{2,1,0:T(8,128)(2,1)}, u32[]{:S(2)}) copy-start(bf16[1,768,2048]{2,1,0:T(8,128)(2,1)} %param.14) | copy-start | bytes 9437188
  109.2 6.9 %copy-start.5 = (bf16[128,2048]{1,0:T(8,128)(2,1)S(1)}, bf16[128,2048]{1,0:T(8,128)(2,1)}, u32[]{:S(2)}) copy-start(bf16[128,2048]{1,0:T(8,128)(2,1)} %param.8) | copy-start | bytes 1572868
  109.2 60.0 %copy-start.16 = (bf16[512,768]{1,0:T(8,128)(2,1)S(1)}, bf16[512,768]{1,0:T(8,128)(2,1)}, u32[]{:S(2)}) copy-start(bf16[512,768]{1,0:T(8,128)(2,1)} %copy-done.15) | copy-start | bytes 2359300
  109.2 81.2 %all-to-all-start.1 = ((bf16[128,4,4096]{2,1,0:T(4,128)(2,1)}), bf16[128,4,4096]{2,1,0:T(4,128)(2,1)}, u32[]{:S(2)}, u32[]{:S(2)}) async-start(bf16[128,4,4096]{2,1,0:T(4,128)(2,1)} %reshape.109), calls=%async_computation.1 | async-start | bytes 8388608 | tf_op jit(solution)/shard_map/all_to_all | solution.py:10
  116.5 7.2 %collective-permute-start = (f32[2048]{0:T(1024)S(1)}, f32[2048]{0:T(1024)S(1)}, u32[]{:S(2)}, u32[]{:S(2)}) collective-permute-start(f32[2048]{0:T(1024)S(1)} %get-tuple-element.25), channel_id=1, source_target_pairs={{0,1},{1,0},{2,3},{3,2},{4,5},{5,4},{6,7},{7,6},{8,9},{9,8},{10,11... | collective-permute-start | bytes 24584 | tf_op jit(solution)/shard_map/ppermute | solution.py:26
  117.6 39.4 %collective-permute-start.1 = (f32[2048]{0:T(1024)S(1)}, f32[2048]{0:T(1024)S(1)}, u32[]{:S(2)}, u32[]{:S(2)}) collective-permute-start(f32[2048]{0:T(1024)S(1)} %get-tuple-element.25), channel_id=1, source_target_pairs={{0,2},{1,3},{2,0},{3,1},{4,6},{5,7},{6,4},{7,5},{8,10},{9,11},{10,... | collective-permute-start | bytes 24584 | tf_op jit(solution)/shard_map/ppermute | solution.py:26
  119.1 46.4 %collective-permute-start.2 = (f32[2048]{0:T(1024)S(1)}, f32[2048]{0:T(1024)S(1)}, u32[]{:S(2)}, u32[]{:S(2)}) collective-permute-start(f32[2048]{0:T(1024)S(1)} %get-tuple-element.25), channel_id=1, source_target_pairs={{0,3},{1,2},{2,1},{3,0},{4,7},{5,6},{6,5},{7,4},{8,11},{9,10},{10,... | collective-permute-start | bytes 24584 | tf_op jit(solution)/shard_map/ppermute | solution.py:26
  165.5 13.8 %copy-start.4 = (bf16[512,4096]{1,0:T(8,128)(2,1)S(1)}, bf16[512,4096]{1,0:T(8,128)(2,1)}, u32[]{:S(2)}) copy-start(bf16[512,4096]{1,0:T(8,128)(2,1)} %reshape.108) | copy-start | bytes 12582916
  165.5 13.8 %copy-start.14 = (bf16[512,768]{1,0:T(8,128)(2,1)S(1)}, bf16[512,768]{1,0:T(8,128)(2,1)}, u32[]{:S(2)}) copy-start(bf16[512,768]{1,0:T(8,128)(2,1)} %copy-done.13) | copy-start | bytes 2359300
  165.5 9.0 %collective-permute-start.3 = (f32[2048]{0:T(1024)S(1)}, f32[2048]{0:T(1024)S(1)}, u32[]{:S(2)}, u32[]{:S(2)}) collective-permute-start(f32[2048]{0:T(1024)S(1)} %add_add_fusion.2), channel_id=1, source_target_pairs={{0,4},{1,5},{2,6},{3,7},{4,0},{5,1},{6,2},{7,3},{8,12},{9,13},{10,... | collective-permute-start | bytes 24584 | tf_op jit(solution)/shard_map/ppermute | solution.py:26
  166.2 8.3 %collective-permute-start.4 = (f32[2048]{0:T(1024)S(1)}, f32[2048]{0:T(1024)S(1)}, u32[]{:S(2)}, u32[]{:S(2)}) collective-permute-start(f32[2048]{0:T(1024)S(1)} %add_add_fusion.2), channel_id=1, source_target_pairs={{0,8},{1,9},{2,10},{3,11},{4,12},{5,13},{6,14},{7,15},{8,0},{9,1},... | collective-permute-start | bytes 24584 | tf_op jit(solution)/shard_map/ppermute | solution.py:26
  166.2 8.3 %collective-permute-start.5 = (f32[2048]{0:T(1024)S(1)}, f32[2048]{0:T(1024)S(1)}, u32[]{:S(2)}, u32[]{:S(2)}) collective-permute-start(f32[2048]{0:T(1024)S(1)} %add_add_fusion.2), channel_id=1, source_target_pairs={{0,12},{1,13},{2,14},{3,15},{4,8},{5,9},{6,10},{7,11},{8,4},{9,5},... | collective-permute-start | bytes 24584 | tf_op jit(solution)/shard_map/ppermute | solution.py:26
  174.5 11.8 %copy-start.18 = (bf16[512,768]{1,0:T(8,128)(2,1)S(1)}, bf16[512,768]{1,0:T(8,128)(2,1)}, u32[]{:S(2)}) copy-start(bf16[512,768]{1,0:T(8,128)(2,1)} %copy-done.17) | copy-start | bytes 2359300
  174.6 8.5 %collective-permute-start.6 = (f32[2048]{0:T(1024)S(1)}, f32[2048]{0:T(1024)S(1)}, u32[]{:S(2)}, u32[]{:S(2)}) collective-permute-start(f32[2048]{0:T(1024)S(1)} %add_add_fusion.1), channel_id=1, source_target_pairs={{0,16},{1,17},{2,18},{3,19},{4,20},{5,21},{6,22},{7,23},{8,24},{9,... | collective-permute-start | bytes 24584 | tf_op jit(solution)/shard_map/ppermute | solution.py:26
  175.1 7.9 %collective-permute-start.7 = (f32[2048]{0:T(1024)S(1)}, f32[2048]{0:T(1024)S(1)}, u32[]{:S(2)}, u32[]{:S(2)}) collective-permute-start(f32[2048]{0:T(1024)S(1)} %add_add_fusion.1), channel_id=1, source_target_pairs={{0,32},{1,33},{2,34},{3,35},{4,36},{5,37},{6,38},{7,39},{8,40},{9,... | collective-permute-start | bytes 24584 | tf_op jit(solution)/shard_map/ppermute | solution.py:26
  177.5 5.5 %collective-permute-start.8 = (f32[2048]{0:T(1024)S(1)}, f32[2048]{0:T(1024)S(1)}, u32[]{:S(2)}, u32[]{:S(2)}) collective-permute-start(f32[2048]{0:T(1024)S(1)} %add_add_fusion.1), channel_id=1, source_target_pairs={{0,48},{1,49},{2,50},{3,51},{4,52},{5,53},{6,54},{7,55},{8,56},{9,... | collective-permute-start | bytes 24584 | tf_op jit(solution)/shard_map/ppermute | solution.py:26
  183.1 6.8 %collective-permute-start.9 = (f32[2048]{0:T(1024)S(1)}, f32[2048]{0:T(1024)S(1)}, u32[]{:S(2)}, u32[]{:S(2)}) collective-permute-start(f32[2048]{0:T(1024)S(1)} %add_add_fusion), channel_id=1, source_target_pairs={{0,64},{1,65},{2,66},{3,67},{4,68},{5,69},{6,70},{7,71},{8,72},{9,... | collective-permute-start | bytes 24584 | tf_op jit(solution)/shard_map/ppermute | solution.py:26
  197.4 3.4 %copy-start.2 = (bf16[512,4096]{1,0:T(8,128)(2,1)S(1)}, bf16[512,4096]{1,0:T(8,128)(2,1)}, u32[]{:S(2)}) copy-start(bf16[512,4096]{1,0:T(8,128)(2,1)} %reshape.110) | copy-start | bytes 12582916
  200.8 1.0 copy-start.7
  201.9 1.2 copy-start.6
  203.0 2.3 %copy-start.1 = (bf16[1,2048,768]{2,1,0:T(8,128)(2,1)S(1)}, bf16[1,2048,768]{2,1,0:T(8,128)(2,1)}, u32[]{:S(2)}) copy-start(bf16[1,2048,768]{2,1,0:T(8,128)(2,1)} %param.13) | copy-start | bytes 9437188

commit v4 on v3

--- a/solution.py
+++ b/solution.py
@@ -75,46 +75,42 @@
     )
     earlier = jnp.cumsum(onehot, axis=0) - onehot
     slot_index = flat_ids * capacity + jnp.sum(earlier * onehot, axis=1)
-    select = (slot_index[:, None] == jnp.arange(slots, dtype=jnp.int32)[None, :]).astype(
-        jnp.bfloat16
-    )
-    select_tk = select.reshape(tok_rows, top_count, slots)
-    select_tok = jnp.sum(select_tk, axis=1)
     grad_in = out_grad.astype(jnp.float32)
     grad_rows = (gate_probs[:, :, None] * grad_in[:, None, :]).astype(jnp.bfloat16)
-    sel_tok3 = select_tok.reshape(tok_rows, devices_all, capacity)
-    sel_tk3 = select_tk.reshape(tok_rows, top_count, devices_all, capacity)
-    send_scaled = lax.dot_general(sel_tok3, tokens, (((0,), (0,)), ((), ())), preferred_element_type=jnp.float32).astype(jnp.bfloat16)
-    send_grad = lax.dot_general(
-        sel_tk3, grad_rows, (((0, 1), (0, 1)), ((), ())), preferred_element_type=jnp.float32
-    ).astype(jnp.bfloat16)
-    sent = jnp.concatenate([send_scaled, send_grad], axis=2)
-    arrived_all = exchange(sent).reshape(slots, 2 * width)
-    arrived_inputs = arrived_all[:, :width].astype(jnp.float32)
+    lanes = jnp.arange(2 * slots, dtype=jnp.int32)[None, :]
+    pair_slot = slot_index.reshape(tok_rows, top_count)
+    token_pick = pair_slot[:, 0:1] * 2 == lanes
+    for k in range(1, top_count):
+        token_pick = token_pick | (pair_slot[:, k : k + 1] * 2 == lanes)
+    grad_pick = slot_index[:, None] * 2 + 1 == lanes
+    pick_send = jnp.concatenate([token_pick, grad_pick], axis=0).astype(jnp.bfloat16)
+    source_rows = jnp.concatenate([tokens, grad_rows.reshape(assigned, width)], axis=0)
+    sent = contract(pick_send, source_rows, 0, 0).astype(jnp.bfloat16)
+    arrived_all = exchange(sent.reshape(devices_all, 2 * capacity, width)).reshape(2 * slots, width)
+    arrived_inputs = arrived_all[0::2].astype(jnp.float32)
     arrived_rms = lax.rsqrt(
         jnp.mean(arrived_inputs * arrived_inputs, axis=1, keepdims=True) + 1e-06
     )
     arrived_normed = arrived_inputs * arrived_rms
     arrived = (arrived_normed * norm_gain).astype(jnp.bfloat16)
-    arrived_grad = arrived_all[:, width:]
+    arrived_grad = arrived_all[1::2]
     expert_out, grad_back, grad_gate, grad_up, grad_down = expert_pass(
         arrived, arrived_grad, w_gate[0], w_up[0], w_down[0]
     )
     grad_gain = all_sum(
         jnp.sum(grad_back.astype(jnp.float32) * arrived_normed, axis=0), devices_all
     )
-    back = jnp.concatenate([expert_out, grad_back], axis=1).reshape(
-        devices_all, capacity, 2 * width
+    zero = jnp.zeros((), jnp.bfloat16)
+    back = lax.pad(expert_out, zero, ((0, 1, 1), (0, 0, 0))) + lax.pad(
+        grad_back, zero, ((1, 0, 1), (0, 0, 0))
     )
-    returned, grad_gate, grad_up, grad_down = lax.optimization_barrier(
-        (exchange(back), grad_gate, grad_up, grad_down)
-    )
-    returned = returned.reshape(slots, 2 * width)
-    picked = [
-        contract(select_tk[:, k, :], returned, 1, 0) for k in range(top_count)
-    ]
-    outs = [p[:, :width] for p in picked]
-    backs = [p[:, width:] for p in picked]
+    back, grad_gain = lax.optimization_barrier((back, grad_gain))
+    returned = exchange(back.reshape(devices_all, 2 * capacity, width)).reshape(2 * slots, width)
+    order = slot_index.reshape(tok_rows, top_count).T.reshape(assigned)
+    pick_back = jnp.concatenate([order * 2, order * 2 + 1])[:, None] == lanes
+    picked = contract(pick_back.astype(jnp.bfloat16), returned, 1, 0)
+    outs = [picked[k * tok_rows : (k + 1) * tok_rows] for k in range(top_count)]
+    backs = [picked[(top_count + k) * tok_rows : (top_count + k + 1) * tok_rows] for k in range(top_count)]
     combined = gate_probs[:, 0:1] * outs[0]
     for k in range(1, top_count):
         combined = combined + gate_probs[:, k : k + 1] * outs[k]

time: 206 us -> 280 us (1.36)
  local copies, waits for them, and re-layouts: 28.5 us -> 89.7 us
  matrix products: 33.2 us -> 40 us
  other arithmetic: 11.8 us -> 16.6 us
    pad x0 -> x2, local copies, waits for them, and re-layouts: none -> 43.9 us  [the longest x1 29.2 us: on_device(): lax.pad(expert_out, zero, ((0, 1, 1), (0, 0, 0)))]
    all_to_all x1, waiting for transfers between devices: 0.01 us -> 38.2 us  [exchange(): return lax.all_to_all(rows, AXES, split_axis=0, concat_axis=0, tiled=True)]
    ppermute x10, waiting for transfers between devices: 45.5 us -> 9.09 us  [all_sum(): lax.ppermute(total, AXES, [(i, i ^ x * step) for i in range(devices_all)])]
    slice x0 -> x2, local copies, waits for them, and re-layouts: none -> 36 us  [the longest x1 18 us: on_device(): arrived_inputs = arrived_all[0::2].astype(jnp.float32)]
    reshape x3 -> x0, local copies, waits for them, and re-layouts: 21 us -> none  [the longest x1 7.21 us: on_device(): jnp.concatenate([expert_out, grad_back], axis=1)]
    mul x0 -> x3, local copies, waits for them, and re-layouts: none -> 7.2 us  [on_device(): gate_probs[:, :, None] * grad_in[:, None, :]]
    add x1 -> x3, other arithmetic: 0.71 us -> 7.74 us  [the longest x1 7.73 us: on_device(): lax.pad(expert_out, zero, ((0, 1, 1), (0, 0, 0)))]
    dot_general x8, matrix products: 24.5 us -> 29.4 us  [contract(): lax.dot_general(left, right, (((left_dim,), (right_dim,)), ((), ())), pre...]
  transfers between devices with their start and end apart: 11 -> 11, of which waited for: 3 -> 8; matrix products, arithmetic and copies ran while one was open for 7% -> 25% of each run, Pallas kernels for 0% -> 0%
where the time goes in v4:
time: 280 us; the launch traced here: 279 us
  local copies, waits for them, and re-layouts  89.7 us (32%)
  blocking collectives  63 us (22%)
  waiting for transfers between devices  47.3 us (17%)
  matrix products  40 us (14%)
  starting transfers between devices  21.1 us (8%)
  other arithmetic  16.6 us (6%)
    all_to_all x1, blocking collectives, exchange(): return lax.all_to_all(rows, AXES, split_axis=0, concat_axis=0, tiled=True)  63 us
    all_to_all x1, waiting for transfers between devices, exchange(): return lax.all_to_all(rows, AXES, split_axis=0, concat_axis=0, tiled=True)  38.2 us
    dot_general x8, matrix products, contract(): lax.dot_general(left, right, (((left_dim,), (right_dim,)), ((), ())), pre...  29.4 us
    pad x1, local copies, waits for them, and re-layouts, on_device(): lax.pad(expert_out, zero, ((0, 1, 1), (0, 0, 0)))  29.2 us
    slice x1, local copies, waits for them, and re-layouts, on_device(): arrived_inputs = arrived_all[0::2].astype(jnp.float32)  18 us
    slice x1, local copies, waits for them, and re-layouts, on_device(): arrived_grad = arrived_all[1::2]  18 us
    pad x1, local copies, waits for them, and re-layouts, on_device(): lax.pad(grad_back, zero, ((1, 0, 1), (0, 0, 0)))  14.7 us
    ppermute x10, starting transfers between devices, all_sum(): lax.ppermute(total, AXES, [(i, i ^ x * step) for i in range(devices_all)])  13.8 us
  transfers between devices with their start and end apart: 11, of which 8 were waited for; matrix products, arithmetic and copies ran while one was open for 25% of the time, Pallas kernels for 0%

profile of v4, /device:TPU:0, one launch (start us, length us, event | category | flops | bytes accessed | tf_op | source)
XLA Modules:
  0.0 278.5 jit_solution(4722438858336015043)
XLA Ops:
  0.6 0.0 copy-start
  0.6 0.9 copy.30
  1.6 0.1 eq.90
  1.7 0.1 eq.86
  1.9 0.1 copy.32
  2.0 0.2 fusion.46
  2.3 0.2 fusion.48
  2.5 0.1 reduce_sum.66
  2.6 0.1 copy.34
  2.7 0.7 multiply_bitcast_fusion
  3.4 0.2 iota_compare_fusion.2
  3.6 3.4 %mul.184 = f32[128,2,2048]{2,1,0:T(2,128)} broadcast(bf16[128,2048]{1,0:T(8,128)(2,1)} %param.15), dimensions={0,2} | broadcast | bytes 2621440 | tf_op jit(solution)/shard_map/mul | solution.py:79
  7.1 3.6 %mul.185 = f32[256,2048]{1,0:T(8,128)} reshape(f32[128,2,2048]{2,1,0:T(2,128)} %mul.184) | data formatting | bytes 4194304 | tf_op jit(solution)/shard_map/mul | solution.py:79
  10.7 0.1 copy.35
  10.8 0.1 mul.182
  11.0 0.0 copy-start.6
  11.0 0.2 fusion.45
  11.1 1.8 multiply_convert_fusion
  12.9 2.4 convert_bitcast_fusion
  15.3 63.0 %all_to_all.10 = bf16[128,8,2048]{2,1,0:T(8,128)(2,1)} all-to-all(bf16[128,8,2048]{2,1,0:T(8,128)(2,1)S(1)} %convert_bitcast_fusion), channel_id=1, replica_groups=mesh['expert'=16,'dp'=8] {'expert','dp'}, dimensions={0} | all-to-all | bytes 8388608 | tf_op jit(solution)/shard_map/all_to_all | solution.py:10
  78.3 18.0 %slice.41 = bf16[512,2048]{1,0:T(8,128)(2,1)} slice(bf16[1024,2048]{1,0:T(8,128)(2,1)} %bitcast.74), slice={[0:1024:2], [0:2048:1]} | slice | bytes 4194304 | tf_op jit(solution)/shard_map/slice | solution.py:90
  96.3 18.0 %slice.42 = bf16[512,2048]{1,0:T(8,128)(2,1)} slice(bf16[1024,2048]{1,0:T(8,128)(2,1)} %bitcast.75), slice={[1:1024:2], [0:2048:1]} | slice | bytes 4194304 | tf_op jit(solution)/shard_map/slice | solution.py:96
  114.3 2.1 fusion.4
  116.5 0.0 copy-start.12
  116.5 4.5 %fusion.7 = f32[512,768]{1,0:T(8,128)S(1)} fusion(bf16[512,2048]{1,0:T(8,128)(2,1)} %slice.42, bf16[1,768,2048]{2,1,0:T(8,128)(2,1)} %param.14), kind=kOutput, calls=%fused_computation.14 | convolution fusion | flops 1610612736 | bytes 6815744 | tf_op jit(solution)/shard_map/dot_general | solution.py:14
  121.0 1.9 fusion.13
  122.9 3.3 %multiply_convert_fusion.2 = (bf16[512,768]{1,0:T(8,128)(2,1)S(1)}, bf16[512,768]{1,0:T(8,128)(2,1)S(1)}, bf16[512,768]{1,0:T(8,128)(2,1)}) fusion(f32[512,768]{1,0:T(8,128)S(1)} %fusion.7, f32[512,768]{1,0:T(8,128)S(1)} %fusion.13, bf16[1,2048,768]{2,1,0:T(8,128)(2,1)S(1)} %copy-done, bf16[512,2048]{1,0:T(8,128)(2,1)S(1)} %copy-done.2, ...), kind=kOutput, calls=%fused_computation.36 | convolution fusion | flops 1620705280 | bytes 10758144 | tf_op jit(solution)/shard_map/dot_general | solution.py:40
  126.2 1.8 fusion.11
  128.1 3.3 %fusion.3 = (f32[2048]{0:T(1024)S(1)}, bf16[512,2048]{1,0:T(8,128)(2,1)}) fusion(bf16[512,2048]{1,0:T(8,128)(2,1)S(1)} %copy-done.2, f32[512]{0:T(512)S(1)} %add_rsqrt_fusion, f32[512,2048]{1,0:T(8,128)S(1)} %fusion.11, bf16[512,768]{1,0:T(8,128)(2,1)S(1)} %get-tuple-element.18, bf16[1,2048,768]{2,1,0:T(8,128)(2,1)S(1)} %copy-done), kind=kOutput, calls=%fused_computation.5 | convolution fusion | flops 1617950720 | bytes 12331008 | tf_op jit(solution)/shard_map/dot_general | solution.py:14
  131.4 0.8 collective-permute-start
  132.3 0.9 collective-permute-start.1
  133.2 1.8 collective-permute-start.2
  134.9 0.2 collective-permute-done
  135.1 0.8 collective-permute-done.1
  135.9 1.8 collective-permute-done.2
  137.7 2.1 collective-permute-start.3
  139.8 1.7 collective-permute-start.5
  141.4 1.5 collective-permute-done.3
  143.0 1.4 collective-permute-done.5
  144.4 0.5 collective-permute-start.6
  144.9 2.8 collective-permute-start.7
  147.7 1.5 collective-permute-start.8
  149.2 0.9 collective-permute-done.7
  150.1 2.5 collective-permute-done.8
  152.6 1.8 collective-permute-start.9
  154.4 5.4 %fusion.19 = bf16[512,2048]{1,0:T(8,128)(2,1)} fusion(bf16[512,768]{1,0:T(8,128)(2,1)} %get-tuple-element.20, bf16[1,768,2048]{2,1,0:T(8,128)(2,1)} %param.14), kind=kOutput, calls=%fused_computation.26 | convolution fusion | flops 1611661312 | bytes 6029312 | tf_op jit(solution)/shard_map/dot_general | solution.py:45
  159.8 14.7 %pad.7 = bf16[1024,2048]{1,0:T(8,128)(2,1)} pad(bf16[512,2048]{1,0:T(8,128)(2,1)S(1)} %copy-done.9, bf16[]{:T(256)} %constant.100.clone.1), padding=1_0_1x0_0_0 | pad | bytes 6291458 | tf_op jit(solution)/shard_map/pad | solution.py:104
  174.4 29.2 %pad.6 = bf16[1024,2048]{1,0:T(8,128)(2,1)} pad(bf16[512,2048]{1,0:T(8,128)(2,1)} %fusion.19, bf16[]{:T(256)} %constant.100.clone.1), padding=0_1_1x0_0_0 | pad | bytes 6291458 | tf_op jit(solution)/shard_map/pad | solution.py:104
  203.7 7.7 %add.135 = bf16[1024,2048]{1,0:T(8,128)(2,1)} add(bf16[1024,2048]{1,0:T(8,128)(2,1)} %pad.6, bf16[1024,2048]{1,0:T(8,128)(2,1)} %pad.7) | non-fusion elementwise | flops 2097152 | bytes 12582912 | tf_op jit(solution)/shard_map/add | solution.py:104
  211.4 0.6 select_add_fusion
  212.0 7.2 %all-to-all-start.1 = ((bf16[128,8,2048]{2,1,0:T(8,128)(2,1)}), bf16[128,8,2048]{2,1,0:T(8,128)(2,1)}, u32[]{:S(2)}, u32[]{:S(2)}) async-start(bf16[128,8,2048]{2,1,0:T(8,128)(2,1)} %bitcast.73), calls=%async_computation.1 | async-start | bytes 8388608 | tf_op jit(solution)/shard_map/all_to_all | solution.py:10
  219.3 0.2 fusion.42
  219.5 0.0 copy-start.3
  219.5 5.5 %fusion.24 = bf16[1,768,2048]{2,1,0:T(8,128)(2,1)} fusion(bf16[512,768]{1,0:T(8,128)(2,1)} %get-tuple-element.20, bf16[512,2048]{1,0:T(8,128)(2,1)} %slice.42), kind=kOutput, calls=%fused_computation.29 | convolution fusion | flops 1612185600 | bytes 6029312 | tf_op jit(solution)/shard_map/dot_general | solution.py:14
  225.0 3.6 %fusion.22 = bf16[1,2048,768]{2,1,0:T(8,128)(2,1)} fusion(bf16[512,768]{1,0:T(8,128)(2,1)S(1)} %copy-done.14, bf16[512,2048]{1,0:T(8,128)(2,1)S(1)} %copy-done.3, f32[2048]{0:T(1024)S(1)} %copy-done.10, f32[512]{0:T(512)S(1)} %add_rsqrt_fusion), kind=kOutput, calls=%fused_computation.27 | convolution fusion | flops 1616379904 | bytes 6039552 | tf_op jit(solution)/shard_map/dot_general | solution.py:14
  228.7 3.6 %fusion.23 = bf16[1,2048,768]{2,1,0:T(8,128)(2,1)} fusion(bf16[512,768]{1,0:T(8,128)(2,1)S(1)} %copy-done.16, bf16[512,2048]{1,0:T(8,128)(2,1)S(1)} %copy-done.3, f32[2048]{0:T(1024)S(1)} %copy-done.10, f32[512]{0:T(512)S(1)} %add_rsqrt_fusion), kind=kOutput, calls=%fused_computation.28 | convolution fusion | flops 1616379904 | bytes 6039552 | tf_op jit(solution)/shard_map/dot_general | solution.py:14
  232.3 38.2 %all-to-all-done.1 = bf16[128,8,2048]{2,1,0:T(8,128)(2,1)} async-done(((bf16[128,8,2048]{2,1,0:T(8,128)(2,1)}), bf16[128,8,2048]{2,1,0:T(8,128)(2,1)}, u32[]{:S(2)}, u32[]{:S(2)}) %all-to-all-start.1) | async-done | bytes 4194336 | tf_op jit(solution)/shard_map/all_to_all | solution.py:10
  270.5 4.6 %fusion.5 = f32[512,2048]{1,0:T(8,128)S(1)} fusion(bf16[128,8,2048]{2,1,0:T(8,128)(2,1)} %all-to-all-done.1, s32[512]{0:T(512)S(1)} %pad_add_fusion), kind=kOutput, calls=%fused_computation.7 | convolution fusion | flops 2148007936 | bytes 8390656 | tf_op jit(solution)/shard_map/dot_general | solution.py:14
  275.1 0.0 copy-start.5
  275.1 0.6 multiply_reduce_fusion.1
  275.7 0.6 pad_maximum_fusion
  276.3 0.0 copy-done.8
  276.3 1.4 fusion.40
  277.7 0.8 copy-done.1
  (48 shorter events, 0.2 us)
Async XLA Ops:
  0.6 122.3 %copy-start = (bf16[1,2048,768]{2,1,0:T(8,128)(2,1)S(1)}, bf16[1,2048,768]{2,1,0:T(8,128)(2,1)}, u32[]{:S(2)}) copy-start(bf16[1,2048,768]{2,1,0:T(8,128)(2,1)} %param.12) | copy-start | bytes 9437188
  3.6 7.1 %copy-start.11 = (f32[128,2]{0,1:T(2,128)S(1)}, f32[128,2]{0,1:T(2,128)}, u32[]{:S(2)}) copy-start(f32[128,2]{0,1:T(2,128)} %param.10) | copy-start | bytes 3076
  11.0 2.0 copy-start.6
  116.4 4.5 %copy-start.2 = (bf16[512,2048]{1,0:T(8,128)(2,1)S(1)}, bf16[512,2048]{1,0:T(8,128)(2,1)}, u32[]{:S(2)}) copy-start(bf16[512,2048]{1,0:T(8,128)(2,1)} %slice.41) | copy-start | bytes 6291460
  116.4 4.5 %copy-start.10 = (f32[2048]{0:T(1024)S(1)}, f32[2048]{0:T(1024)}, u32[]{:S(2)}) copy-start(f32[2048]{0:T(1024)} %param.11) | copy-start | bytes 24580
  116.5 4.5 %copy-start.12 = (bf16[1,2048,768]{2,1,0:T(8,128)(2,1)S(1)}, bf16[1,2048,768]{2,1,0:T(8,128)(2,1)}, u32[]{:S(2)}) copy-start(bf16[1,2048,768]{2,1,0:T(8,128)(2,1)} %param.13) | copy-start | bytes 9437188
  126.2 1.8 copy-start.15
  126.2 1.8 copy-start.13
  131.4 3.7 %collective-permute-start = (f32[2048]{0:T(1024)S(1)}, f32[2048]{0:T(1024)S(1)}, u32[]{:S(2)}, u32[]{:S(2)}) collective-permute-start(f32[2048]{0:T(1024)S(1)} %get-tuple-element.25), channel_id=1, source_target_pairs={{0,1},{1,0},{2,3},{3,2},{4,5},{5,4},{6,7},{7,6},{8,9},{9,8},{10,11... | collective-permute-start | bytes 24584 | tf_op jit(solution)/shard_map/ppermute | solution.py:26
  132.3 3.7 %collective-permute-start.1 = (f32[2048]{0:T(1024)S(1)}, f32[2048]{0:T(1024)S(1)}, u32[]{:S(2)}, u32[]{:S(2)}) collective-permute-start(f32[2048]{0:T(1024)S(1)} %get-tuple-element.25), channel_id=1, source_target_pairs={{0,2},{1,3},{2,0},{3,1},{4,6},{5,7},{6,4},{7,5},{8,10},{9,11},{10,... | collective-permute-start | bytes 24584 | tf_op jit(solution)/shard_map/ppermute | solution.py:26
  133.2 4.5 %collective-permute-start.2 = (f32[2048]{0:T(1024)S(1)}, f32[2048]{0:T(1024)S(1)}, u32[]{:S(2)}, u32[]{:S(2)}) collective-permute-start(f32[2048]{0:T(1024)S(1)} %get-tuple-element.25), channel_id=1, source_target_pairs={{0,3},{1,2},{2,1},{3,0},{4,7},{5,6},{6,5},{7,4},{8,11},{9,10},{10,... | collective-permute-start | bytes 24584 | tf_op jit(solution)/shard_map/ppermute | solution.py:26
  137.7 5.2 %collective-permute-start.3 = (f32[2048]{0:T(1024)S(1)}, f32[2048]{0:T(1024)S(1)}, u32[]{:S(2)}, u32[]{:S(2)}) collective-permute-start(f32[2048]{0:T(1024)S(1)} %add_add_fusion.2), channel_id=1, source_target_pairs={{0,4},{1,5},{2,6},{3,7},{4,0},{5,1},{6,2},{7,3},{8,12},{9,13},{10,... | collective-permute-start | bytes 24584 | tf_op jit(solution)/shard_map/ppermute | solution.py:26
  139.8 3.2 %collective-permute-start.4 = (f32[2048]{0:T(1024)S(1)}, f32[2048]{0:T(1024)S(1)}, u32[]{:S(2)}, u32[]{:S(2)}) collective-permute-start(f32[2048]{0:T(1024)S(1)} %add_add_fusion.2), channel_id=1, source_target_pairs={{0,8},{1,9},{2,10},{3,11},{4,12},{5,13},{6,14},{7,15},{8,0},{9,1},... | collective-permute-start | bytes 24584 | tf_op jit(solution)/shard_map/ppermute | solution.py:26
  139.8 4.6 %collective-permute-start.5 = (f32[2048]{0:T(1024)S(1)}, f32[2048]{0:T(1024)S(1)}, u32[]{:S(2)}, u32[]{:S(2)}) collective-permute-start(f32[2048]{0:T(1024)S(1)} %add_add_fusion.2), channel_id=1, source_target_pairs={{0,12},{1,13},{2,14},{3,15},{4,8},{5,9},{6,10},{7,11},{8,4},{9,5},... | collective-permute-start | bytes 24584 | tf_op jit(solution)/shard_map/ppermute | solution.py:26
  144.4 4.8 %collective-permute-start.6 = (f32[2048]{0:T(1024)S(1)}, f32[2048]{0:T(1024)S(1)}, u32[]{:S(2)}, u32[]{:S(2)}) collective-permute-start(f32[2048]{0:T(1024)S(1)} %add_add_fusion.1), channel_id=1, source_target_pairs={{0,16},{1,17},{2,18},{3,19},{4,20},{5,21},{6,22},{7,23},{8,24},{9,... | collective-permute-start | bytes 24584 | tf_op jit(solution)/shard_map/ppermute | solution.py:26
  144.9 5.2 %collective-permute-start.7 = (f32[2048]{0:T(1024)S(1)}, f32[2048]{0:T(1024)S(1)}, u32[]{:S(2)}, u32[]{:S(2)}) collective-permute-start(f32[2048]{0:T(1024)S(1)} %add_add_fusion.1), channel_id=1, source_target_pairs={{0,32},{1,33},{2,34},{3,35},{4,36},{5,37},{6,38},{7,39},{8,40},{9,... | collective-permute-start | bytes 24584 | tf_op jit(solution)/shard_map/ppermute | solution.py:26
  147.7 4.9 %collective-permute-start.8 = (f32[2048]{0:T(1024)S(1)}, f32[2048]{0:T(1024)S(1)}, u32[]{:S(2)}, u32[]{:S(2)}) collective-permute-start(f32[2048]{0:T(1024)S(1)} %add_add_fusion.1), channel_id=1, source_target_pairs={{0,48},{1,49},{2,50},{3,51},{4,52},{5,53},{6,54},{7,55},{8,56},{9,... | collective-permute-start | bytes 24584 | tf_op jit(solution)/shard_map/ppermute | solution.py:26
  152.6 58.9 %collective-permute-start.9 = (f32[2048]{0:T(1024)S(1)}, f32[2048]{0:T(1024)S(1)}, u32[]{:S(2)}, u32[]{:S(2)}) collective-permute-start(f32[2048]{0:T(1024)S(1)} %add_add_fusion), channel_id=1, source_target_pairs={{0,64},{1,65},{2,66},{3,67},{4,68},{5,69},{6,70},{7,71},{8,72},{9,... | collective-permute-start | bytes 24584 | tf_op jit(solution)/shard_map/ppermute | solution.py:26
  154.4 5.4 %copy-start.9 = (bf16[512,2048]{1,0:T(8,128)(2,1)S(1)}, bf16[512,2048]{1,0:T(8,128)(2,1)}, u32[]{:S(2)}) copy-start(bf16[512,2048]{1,0:T(8,128)(2,1)} %get-tuple-element.26) | copy-start | bytes 6291460
  212.0 7.3 %copy-start.7 = (bf16[128,2048]{1,0:T(8,128)(2,1)S(1)}, bf16[128,2048]{1,0:T(8,128)(2,1)}, u32[]{:S(2)}) copy-start(bf16[128,2048]{1,0:T(8,128)(2,1)} %param.8) | copy-start | bytes 1572868
  212.0 58.5 %all-to-all-start.1 = ((bf16[128,8,2048]{2,1,0:T(8,128)(2,1)}), bf16[128,8,2048]{2,1,0:T(8,128)(2,1)}, u32[]{:S(2)}, u32[]{:S(2)}) async-start(bf16[128,8,2048]{2,1,0:T(8,128)(2,1)} %bitcast.73), calls=%async_computation.1 | async-start | bytes 8388608 | tf_op jit(solution)/shard_map/all_to_all | solution.py:10
  219.5 5.5 %copy-start.3 = (bf16[512,2048]{1,0:T(8,128)(2,1)S(1)}, bf16[512,2048]{1,0:T(8,128)(2,1)}, u32[]{:S(2)}) copy-start(bf16[512,2048]{1,0:T(8,128)(2,1)} %slice.41) | copy-start | bytes 6291460
  219.5 5.5 %copy-start.14 = (bf16[512,768]{1,0:T(8,128)(2,1)S(1)}, bf16[512,768]{1,0:T(8,128)(2,1)}, u32[]{:S(2)}) copy-start(bf16[512,768]{1,0:T(8,128)(2,1)} %copy-done.13) | copy-start | bytes 2359300
  225.0 3.7 %copy-start.16 = (bf16[512,768]{1,0:T(8,128)(2,1)S(1)}, bf16[512,768]{1,0:T(8,128)(2,1)}, u32[]{:S(2)}) copy-start(bf16[512,768]{1,0:T(8,128)(2,1)} %copy-done.15) | copy-start | bytes 2359300
  232.3 42.7 %copy-start.4 = (bf16[128,2048]{1,0:T(8,128)(2,1)S(1)}, bf16[128,2048]{1,0:T(8,128)(2,1)}, u32[]{:S(2)}) copy-start(bf16[128,2048]{1,0:T(8,128)(2,1)} %param.15) | copy-start | bytes 1572868
  275.1 1.2 copy-start.5
  275.1 1.2 copy-start.8
  276.2 2.3 copy-start.1

commit v5 on v3

--- a/solution.py
+++ b/solution.py
@@ -106,6 +106,7 @@
     back = jnp.concatenate([expert_out, grad_back], axis=1).reshape(
         devices_all, capacity, 2 * width
     )
+    back, grad_gain = lax.optimization_barrier((back, grad_gain))
     returned, grad_gate, grad_up, grad_down = lax.optimization_barrier(
         (exchange(back), grad_gate, grad_up, grad_down)
     )

time: 206 us -> 205 us (level)
  matrix products: 33.2 us -> 36.1 us
    ppermute x10, waiting for transfers between devices: 45.5 us -> 5.71 us  [all_sum(): lax.ppermute(total, AXES, [(i, i ^ x * step) for i in range(devices_all)])]
    all_to_all x1, waiting for transfers between devices: 0.01 us -> 38.5 us  [exchange(): return lax.all_to_all(rows, AXES, split_axis=0, concat_axis=0, tiled=True)]
  transfers between devices with their start and end apart: 11 -> 11, of which waited for: 3 -> 6; matrix products, arithmetic and copies ran while one was open for 7% -> 13% of each run, Pallas kernels for 0% -> 0%
where the time goes in v5:
time: 205 us; the launch traced here: 204 us
  blocking collectives  63 us (31%)
  waiting for transfers between devices  44.2 us (22%)
  matrix products  36.1 us (18%)
  local copies, waits for them, and re-layouts  27.6 us (13%)
  starting transfers between devices  20.5 us (10%)
  other arithmetic  11.8 us (6%)
    all_to_all x1, blocking collectives, exchange(): return lax.all_to_all(rows, AXES, split_axis=0, concat_axis=0, tiled=True)  63 us
    all_to_all x1, waiting for transfers between devices, exchange(): return lax.all_to_all(rows, AXES, split_axis=0, concat_axis=0, tiled=True)  38.5 us
    dot_general x8, matrix products, contract(): lax.dot_general(left, right, (((left_dim,), (right_dim,)), ((), ())), pre...  24.7 us
    ppermute x10, starting transfers between devices, all_sum(): lax.ppermute(total, AXES, [(i, i ^ x * step) for i in range(devices_all)])  14.3 us
    reshape x1, local copies, waits for them, and re-layouts, on_device(): jnp.concatenate([expert_out, grad_back], axis=1)  7.17 us
    reshape x1, local copies, waits for them, and re-layouts, on_device(): arrived_all = exchange(sent).reshape(slots, 2 * width)  6.89 us
    reshape x1, local copies, waits for them, and re-layouts, on_device(): returned = returned.reshape(slots, 2 * width)  6.89 us
    all_to_all x1, starting transfers between devices, exchange(): return lax.all_to_all(rows, AXES, split_axis=0, concat_axis=0, tiled=True)  6.19 us
  transfers between devices with their start and end apart: 11, of which 6 were waited for; matrix products, arithmetic and copies ran while one was open for 13% of the time, Pallas kernels for 0%

profile of v5, /device:TPU:0, one launch (start us, length us, event | category | flops | bytes accessed | tf_op | source)
XLA Modules:
  0.0 204.2 jit_solution(13853192287675233910)
XLA Ops:
  0.6 0.0 copy-start
  0.7 0.9 copy.37
  1.6 0.1 eq.62
  1.7 0.1 eq.58
  1.9 0.1 copy.39
  2.0 0.2 fusion.45
  2.3 0.2 fusion.47
  2.5 0.1 reduce_sum.78
  2.6 0.1 copy.41
  2.7 0.7 multiply_add_fusion.1
  3.4 2.1 %convert_element_type.72 = f32[128,2048]{1,0:T(8,128)} convert(bf16[128,2048]{1,0:T(8,128)(2,1)} %param.15) | non-fusion elementwise | flops 262144 | bytes 1572864 | tf_op jit(solution)/shard_map/convert_element_type | solution.py:83
  5.5 0.1 convert_reduce_fusion
  5.6 0.1 copy.42
  5.8 0.0 copy-start.8
  5.8 1.8 convolution_convert_fusion.3
  7.6 0.8 bitcast_convert_fusion
  8.4 0.3 pad_maximum_fusion
  8.7 3.2 %copy.44 = bf16[128,4,4096]{2,1,0:T(4,128)(2,1)S(1)} copy(bf16[128,4,4096]{2,0,1:T(8,128)(2,1)S(1)} %pad_maximum_fusion) | data formatting | bytes 8388608 | tf_op jit(solution)/shard_map/concatenate | solution.py:91
  12.0 63.0 %all_to_all.10 = bf16[128,4,4096]{2,1,0:T(4,128)(2,1)} all-to-all(bf16[128,4,4096]{2,1,0:T(4,128)(2,1)S(1)} %copy.44), channel_id=1, replica_groups=mesh['expert'=16,'dp'=8] {'expert','dp'}, dimensions={0} | all-to-all | bytes 8388608 | tf_op jit(solution)/shard_map/all_to_all | solution.py:10
  74.9 6.9 %reshape.108 = bf16[512,4096]{1,0:T(8,128)(2,1)} reshape(bf16[128,4,4096]{2,1,0:T(4,128)(2,1)} %all_to_all.10) | data formatting | bytes 8388608 | tf_op jit(solution)/shard_map/reshape | solution.py:92
  81.8 2.1 %fusion.4 = f32[512]{0:T(512)S(1)} fusion(bf16[512,4096]{1,0:T(8,128)(2,1)} %reshape.108), kind=kLoop, calls=%fused_computation.6 | loop fusion | flops 3145216 | bytes 2099200 | tf_op jit(solution)/shard_map/reduce_sum | solution.py:95
  83.9 0.0 copy-start.9
  83.9 0.0 copy-start.11
  84.0 4.5 %fusion.5 = f32[512,768]{1,0:T(8,128)S(1)} fusion(bf16[1,768,2048]{2,1,0:T(8,128)(2,1)} %param.14, bf16[512,4096]{1,0:T(8,128)(2,1)} %reshape.108), kind=kOutput, calls=%fused_computation.14 | convolution fusion | flops 1610612736 | bytes 6815744 | tf_op jit(solution)/shard_map/dot_general | solution.py:14
  88.5 0.2 copy-done.11
  88.7 1.9 fusion.15
  90.6 3.2 %multiply_convert_fusion.3 = (bf16[512,768]{1,0:T(8,128)(2,1)}, bf16[512,768]{1,0:T(8,128)(2,1)S(1)}, bf16[512,768]{1,0:T(8,128)(2,1)S(1)}) fusion(f32[512,768]{1,0:T(8,128)S(1)} %fusion.15, f32[512,768]{1,0:T(8,128)S(1)} %fusion.5, bf16[1,2048,768]{2,1,0:T(8,128)(2,1)S(1)} %copy-done, f32[2048]{0:T(1024)S(1)} %copy-done.9, f32[512]{0:T(512)S(1)} %add_rsqrt_fusion, ...), kind=kOutput, calls=%fused_computation.33 | convolution fusion | flops 1620705280 | bytes 10758144 | tf_op jit(solution)/shard_map/dot_general | solution.py:41
  93.8 1.8 fusion.9
  95.6 0.0 copy-start.16
  95.6 2.0 fusion.3
  97.6 0.9 collective-permute-start
  98.6 0.9 collective-permute-start.1
  99.4 1.8 collective-permute-start.2
  101.2 0.2 collective-permute-done
  101.4 0.8 collective-permute-done.1
  102.2 1.8 collective-permute-done.2
  104.0 2.0 %collective-permute-start.3 = (f32[2048]{0:T(1024)S(1)}, f32[2048]{0:T(1024)S(1)}, u32[]{:S(2)}, u32[]{:S(2)}) collective-permute-start(f32[2048]{0:T(1024)S(1)} %add_add_fusion.2), channel_id=1, source_target_pairs={{0,4},{1,5},{2,6},{3,7},{4,0},{5,1},{6,2},{7,3},{8,12},{9,13},{10,... | collective-permute-start | bytes 24584 | tf_op jit(solution)/shard_map/ppermute | solution.py:26
  106.1 1.7 collective-permute-start.5
  107.7 1.5 collective-permute-done.3
  109.3 1.4 collective-permute-done.5
  110.7 0.6 collective-permute-start.6
  111.3 2.7 %collective-permute-start.7 = (f32[2048]{0:T(1024)S(1)}, f32[2048]{0:T(1024)S(1)}, u32[]{:S(2)}, u32[]{:S(2)}) collective-permute-start(f32[2048]{0:T(1024)S(1)} %add_add_fusion.1), channel_id=1, source_target_pairs={{0,32},{1,33},{2,34},{3,35},{4,36},{5,37},{6,38},{7,39},{8,40},{9,... | collective-permute-start | bytes 24584 | tf_op jit(solution)/shard_map/ppermute | solution.py:26
  114.0 1.5 collective-permute-start.8
  115.4 3.7 %fusion.17 = bf16[512,2048]{1,0:T(8,128)(2,1)S(1)} fusion(bf16[512,768]{1,0:T(8,128)(2,1)S(1)} %copy-done.16, bf16[1,768,2048]{2,1,0:T(8,128)(2,1)} %param.14), kind=kOutput, calls=%fused_computation.27 | convolution fusion | flops 1611661312 | bytes 6029312 | tf_op jit(solution)/shard_map/dot_general | solution.py:45
  119.2 2.3 %collective-permute-start.9 = (f32[2048]{0:T(1024)S(1)}, f32[2048]{0:T(1024)S(1)}, u32[]{:S(2)}, u32[]{:S(2)}) collective-permute-start(f32[2048]{0:T(1024)S(1)} %add_add_fusion), channel_id=1, source_target_pairs={{0,64},{1,65},{2,66},{3,67},{4,68},{5,69},{6,70},{7,71},{8,72},{9,... | collective-permute-start | bytes 24584 | tf_op jit(solution)/shard_map/ppermute | solution.py:26
  121.5 2.5 %pad_maximum_fusion.1 = bf16[512,4096]{1,0:T(8,128)(2,1)} fusion(bf16[512,2048]{1,0:T(8,128)(2,1)S(1)} %get-tuple-element.30, bf16[512,2048]{1,0:T(8,128)(2,1)S(1)} %fusion.17), kind=kLoop, calls=%fused_computation.8 | loop fusion | flops 8388608 | bytes 8388608 | tf_op jit(solution)/shard_map/concatenate | solution.py:106
  123.9 7.2 %reshape.109 = bf16[128,4,4096]{2,1,0:T(4,128)(2,1)} reshape(bf16[512,4096]{1,0:T(8,128)(2,1)} %pad_maximum_fusion.1) | data formatting | bytes 8388608 | tf_op jit(solution)/shard_map/reshape | solution.py:106
  131.1 0.6 select_add_fusion
  131.7 6.2 %all-to-all-start.1 = ((bf16[128,4,4096]{2,1,0:T(4,128)(2,1)}), bf16[128,4,4096]{2,1,0:T(4,128)(2,1)}, u32[]{:S(2)}, u32[]{:S(2)}) async-start(bf16[128,4,4096]{2,1,0:T(4,128)(2,1)} %reshape.109), calls=%async_computation.1 | async-start | bytes 8388608 | tf_op jit(solution)/shard_map/all_to_all | solution.py:10
  137.9 0.2 fusion.33
  138.1 0.1 iota_compare_fusion
  138.3 5.2 %convolution_convert_fusion = bf16[768,2048]{1,0:T(8,128)(2,1)} fusion(bf16[512,768]{1,0:T(8,128)(2,1)S(1)} %copy-done.16, bf16[512,4096]{1,0:T(8,128)(2,1)} %reshape.108), kind=kOutput, calls=%fused_computation.11 | convolution fusion | flops 1612185600 | bytes 6029312 | tf_op jit(solution)/shard_map/dot_general | solution.py:14
  143.5 3.7 %convolution_convert_fusion.1 = bf16[2048,768]{1,0:T(8,128)(2,1)} fusion(bf16[512,768]{1,0:T(8,128)(2,1)S(1)} %copy-done.15, f32[2048]{0:T(1024)S(1)} %copy-done.9, f32[512]{0:T(512)S(1)} %add_rsqrt_fusion, bf16[512,4096]{1,0:T(8,128)(2,1)S(1)} %copy-done.4), kind=kOutput, calls=%fused_computation.12 | convolution fusion | flops 1616379904 | bytes 6039552 | tf_op jit(solution)/shard_map/dot_general | solution.py:14
  147.2 3.7 %convolution_convert_fusion.2 = bf16[2048,768]{1,0:T(8,128)(2,1)} fusion(bf16[512,768]{1,0:T(8,128)(2,1)S(1)} %copy-done.13, f32[2048]{0:T(1024)S(1)} %copy-done.9, f32[512]{0:T(512)S(1)} %add_rsqrt_fusion, bf16[512,4096]{1,0:T(8,128)(2,1)S(1)} %copy-done.4), kind=kOutput, calls=%fused_computation.13 | convolution fusion | flops 1616379904 | bytes 6039552 | tf_op jit(solution)/shard_map/dot_general | solution.py:14
  150.9 38.5 %all-to-all-done.1 = bf16[128,4,4096]{2,1,0:T(4,128)(2,1)} async-done(((bf16[128,4,4096]{2,1,0:T(4,128)(2,1)}), bf16[128,4,4096]{2,1,0:T(4,128)(2,1)}, u32[]{:S(2)}, u32[]{:S(2)}) %all-to-all-start.1) | async-done | bytes 4194336 | tf_op jit(solution)/shard_map/all_to_all | solution.py:10
  189.4 6.9 %reshape.110 = bf16[512,4096]{1,0:T(8,128)(2,1)} reshape(bf16[128,4,4096]{2,1,0:T(4,128)(2,1)} %all-to-all-done.1) | data formatting | bytes 8388608 | tf_op jit(solution)/shard_map/reshape | solution.py:113
  196.3 3.1 %fusion.44 = f32[128,4096]{1,0:T(8,128)S(1)} fusion(bf16[512,4096]{1,0:T(8,128)(2,1)} %reshape.110, pred[128,2,512]{2,0,1:T(32,128)(4,1)S(1)} %iota_compare_fusion), kind=kOutput, calls=%fused_computation.64 | convolution fusion | flops 536870912 | bytes 6356992 | tf_op jit(solution)/shard_map/dot_general | solution.py:14
  199.3 0.4 copy-done.2
  199.7 0.7 fusion.43
  200.5 0.3 copy-done.7
  200.8 0.6 fusion.27
  201.4 0.6 pad_maximum_fusion.2
  201.9 1.4 fusion.31
  203.4 0.8 copy-done.1
  (45 shorter events, 0.2 us)
Async XLA Ops:
  0.6 89.9 %copy-start = (bf16[1,2048,768]{2,1,0:T(8,128)(2,1)S(1)}, bf16[1,2048,768]{2,1,0:T(8,128)(2,1)}, u32[]{:S(2)}) copy-start(bf16[1,2048,768]{2,1,0:T(8,128)(2,1)} %param.13) | copy-start | bytes 9437188
  0.6 7.0 %copy-start.10 = (f32[128,2]{0,1:T(2,128)S(1)}, f32[128,2]{0,1:T(2,128)}, u32[]{:S(2)}) copy-start(f32[128,2]{0,1:T(2,128)} %param.10) | copy-start | bytes 3076
  5.8 1.9 copy-start.8
  83.9 4.5 %copy-start.3 = (bf16[512,4096]{1,0:T(8,128)(2,1)S(1)}, bf16[512,4096]{1,0:T(8,128)(2,1)}, u32[]{:S(2)}) copy-start(bf16[512,4096]{1,0:T(8,128)(2,1)} %reshape.108) | copy-start | bytes 12582916
  83.9 4.5 %copy-start.9 = (f32[2048]{0:T(1024)S(1)}, f32[2048]{0:T(1024)}, u32[]{:S(2)}) copy-start(f32[2048]{0:T(1024)} %param.11) | copy-start | bytes 24580
  83.9 4.7 %copy-start.11 = (bf16[1,2048,768]{2,1,0:T(8,128)(2,1)S(1)}, bf16[1,2048,768]{2,1,0:T(8,128)(2,1)}, u32[]{:S(2)}) copy-start(bf16[1,2048,768]{2,1,0:T(8,128)(2,1)} %param.12) | copy-start | bytes 9437188
  93.8 1.8 copy-start.14
  93.8 1.8 copy-start.12
  95.6 19.8 %copy-start.16 = (bf16[512,768]{1,0:T(8,128)(2,1)S(1)}, bf16[512,768]{1,0:T(8,128)(2,1)}, u32[]{:S(2)}) copy-start(bf16[512,768]{1,0:T(8,128)(2,1)} %get-tuple-element.24) | copy-start | bytes 2359300
  97.6 3.7 %collective-permute-start = (f32[2048]{0:T(1024)S(1)}, f32[2048]{0:T(1024)S(1)}, u32[]{:S(2)}, u32[]{:S(2)}) collective-permute-start(f32[2048]{0:T(1024)S(1)} %get-tuple-element.29), channel_id=1, source_target_pairs={{0,1},{1,0},{2,3},{3,2},{4,5},{5,4},{6,7},{7,6},{8,9},{9,8},{10,11... | collective-permute-start | bytes 24584 | tf_op jit(solution)/shard_map/ppermute | solution.py:26
  98.6 3.7 %collective-permute-start.1 = (f32[2048]{0:T(1024)S(1)}, f32[2048]{0:T(1024)S(1)}, u32[]{:S(2)}, u32[]{:S(2)}) collective-permute-start(f32[2048]{0:T(1024)S(1)} %get-tuple-element.29), channel_id=1, source_target_pairs={{0,2},{1,3},{2,0},{3,1},{4,6},{5,7},{6,4},{7,5},{8,10},{9,11},{10,... | collective-permute-start | bytes 24584 | tf_op jit(solution)/shard_map/ppermute | solution.py:26
  99.4 4.5 %collective-permute-start.2 = (f32[2048]{0:T(1024)S(1)}, f32[2048]{0:T(1024)S(1)}, u32[]{:S(2)}, u32[]{:S(2)}) collective-permute-start(f32[2048]{0:T(1024)S(1)} %get-tuple-element.29), channel_id=1, source_target_pairs={{0,3},{1,2},{2,1},{3,0},{4,7},{5,6},{6,5},{7,4},{8,11},{9,10},{10,... | collective-permute-start | bytes 24584 | tf_op jit(solution)/shard_map/ppermute | solution.py:26
  104.0 5.2 %collective-permute-start.3 = (f32[2048]{0:T(1024)S(1)}, f32[2048]{0:T(1024)S(1)}, u32[]{:S(2)}, u32[]{:S(2)}) collective-permute-start(f32[2048]{0:T(1024)S(1)} %add_add_fusion.2), channel_id=1, source_target_pairs={{0,4},{1,5},{2,6},{3,7},{4,0},{5,1},{6,2},{7,3},{8,12},{9,13},{10,... | collective-permute-start | bytes 24584 | tf_op jit(solution)/shard_map/ppermute | solution.py:26
  106.1 3.2 %collective-permute-start.4 = (f32[2048]{0:T(1024)S(1)}, f32[2048]{0:T(1024)S(1)}, u32[]{:S(2)}, u32[]{:S(2)}) collective-permute-start(f32[2048]{0:T(1024)S(1)} %add_add_fusion.2), channel_id=1, source_target_pairs={{0,8},{1,9},{2,10},{3,11},{4,12},{5,13},{6,14},{7,15},{8,0},{9,1},... | collective-permute-start | bytes 24584 | tf_op jit(solution)/shard_map/ppermute | solution.py:26
  106.1 4.6 %collective-permute-start.5 = (f32[2048]{0:T(1024)S(1)}, f32[2048]{0:T(1024)S(1)}, u32[]{:S(2)}, u32[]{:S(2)}) collective-permute-start(f32[2048]{0:T(1024)S(1)} %add_add_fusion.2), channel_id=1, source_target_pairs={{0,12},{1,13},{2,14},{3,15},{4,8},{5,9},{6,10},{7,11},{8,4},{9,5},... | collective-permute-start | bytes 24584 | tf_op jit(solution)/shard_map/ppermute | solution.py:26
  110.7 8.5 %collective-permute-start.6 = (f32[2048]{0:T(1024)S(1)}, f32[2048]{0:T(1024)S(1)}, u32[]{:S(2)}, u32[]{:S(2)}) collective-permute-start(f32[2048]{0:T(1024)S(1)} %add_add_fusion.1), channel_id=1, source_target_pairs={{0,16},{1,17},{2,18},{3,19},{4,20},{5,21},{6,22},{7,23},{8,24},{9,... | collective-permute-start | bytes 24584 | tf_op jit(solution)/shard_map/ppermute | solution.py:26
  111.3 7.9 %collective-permute-start.7 = (f32[2048]{0:T(1024)S(1)}, f32[2048]{0:T(1024)S(1)}, u32[]{:S(2)}, u32[]{:S(2)}) collective-permute-start(f32[2048]{0:T(1024)S(1)} %add_add_fusion.1), channel_id=1, source_target_pairs={{0,32},{1,33},{2,34},{3,35},{4,36},{5,37},{6,38},{7,39},{8,40},{9,... | collective-permute-start | bytes 24584 | tf_op jit(solution)/shard_map/ppermute | solution.py:26
  114.0 5.2 %collective-permute-start.8 = (f32[2048]{0:T(1024)S(1)}, f32[2048]{0:T(1024)S(1)}, u32[]{:S(2)}, u32[]{:S(2)}) collective-permute-start(f32[2048]{0:T(1024)S(1)} %add_add_fusion.1), channel_id=1, source_target_pairs={{0,48},{1,49},{2,50},{3,51},{4,52},{5,53},{6,54},{7,55},{8,56},{9,... | collective-permute-start | bytes 24584 | tf_op jit(solution)/shard_map/ppermute | solution.py:26
  119.2 11.9 %collective-permute-start.9 = (f32[2048]{0:T(1024)S(1)}, f32[2048]{0:T(1024)S(1)}, u32[]{:S(2)}, u32[]{:S(2)}) collective-permute-start(f32[2048]{0:T(1024)S(1)} %add_add_fusion), channel_id=1, source_target_pairs={{0,64},{1,65},{2,66},{3,67},{4,68},{5,69},{6,70},{7,71},{8,72},{9,... | collective-permute-start | bytes 24584 | tf_op jit(solution)/shard_map/ppermute | solution.py:26
  131.7 6.2 %copy-start.5 = (bf16[128,2048]{1,0:T(8,128)(2,1)S(1)}, bf16[128,2048]{1,0:T(8,128)(2,1)}, u32[]{:S(2)}) copy-start(bf16[128,2048]{1,0:T(8,128)(2,1)} %param.8) | copy-start | bytes 1572868
  131.7 57.7 %all-to-all-start.1 = ((bf16[128,4,4096]{2,1,0:T(4,128)(2,1)}), bf16[128,4,4096]{2,1,0:T(4,128)(2,1)}, u32[]{:S(2)}, u32[]{:S(2)}) async-start(bf16[128,4,4096]{2,1,0:T(4,128)(2,1)} %reshape.109), calls=%async_computation.1 | async-start | bytes 8388608 | tf_op jit(solution)/shard_map/all_to_all | solution.py:10
  138.3 5.3 %copy-start.4 = (bf16[512,4096]{1,0:T(8,128)(2,1)S(1)}, bf16[512,4096]{1,0:T(8,128)(2,1)}, u32[]{:S(2)}) copy-start(bf16[512,4096]{1,0:T(8,128)(2,1)} %reshape.108) | copy-start | bytes 12582916
  138.3 5.3 %copy-start.15 = (bf16[512,768]{1,0:T(8,128)(2,1)S(1)}, bf16[512,768]{1,0:T(8,128)(2,1)}, u32[]{:S(2)}) copy-start(bf16[512,768]{1,0:T(8,128)(2,1)} %copy-done.14) | copy-start | bytes 2359300
  143.5 3.7 %copy-start.13 = (bf16[512,768]{1,0:T(8,128)(2,1)S(1)}, bf16[512,768]{1,0:T(8,128)(2,1)}, u32[]{:S(2)}) copy-start(bf16[512,768]{1,0:T(8,128)(2,1)} %copy-done.12) | copy-start | bytes 2359300
  196.3 3.4 %copy-start.2 = (bf16[512,4096]{1,0:T(8,128)(2,1)S(1)}, bf16[512,4096]{1,0:T(8,128)(2,1)}, u32[]{:S(2)}) copy-start(bf16[512,4096]{1,0:T(8,128)(2,1)} %reshape.110) | copy-start | bytes 12582916
  199.7 1.0 copy-start.7
  200.7 1.2 copy-start.6
  201.9 2.3 %copy-start.1 = (bf16[1,2048,768]{2,1,0:T(8,128)(2,1)S(1)}, bf16[1,2048,768]{2,1,0:T(8,128)(2,1)}, u32[]{:S(2)}) copy-start(bf16[1,2048,768]{2,1,0:T(8,128)(2,1)} %param.13) | copy-start | bytes 9437188

commit v6 on v3

--- a/solution.py
+++ b/solution.py
@@ -100,15 +100,14 @@
     expert_out, grad_back, grad_gate, grad_up, grad_down = expert_pass(
         arrived, arrived_grad, w_gate[0], w_up[0], w_down[0]
     )
-    grad_gain = all_sum(
-        jnp.sum(grad_back.astype(jnp.float32) * arrived_normed, axis=0), devices_all
-    )
+    gain_part = jnp.sum(grad_back.astype(jnp.float32) * arrived_normed, axis=0)
     back = jnp.concatenate([expert_out, grad_back], axis=1).reshape(
         devices_all, capacity, 2 * width
     )
-    returned, grad_gate, grad_up, grad_down = lax.optimization_barrier(
-        (exchange(back), grad_gate, grad_up, grad_down)
+    returned, grad_gate, grad_up, grad_down, gain_part = lax.optimization_barrier(
+        (exchange(back), grad_gate, grad_up, grad_down, gain_part)
     )
+    grad_gain = all_sum(gain_part, devices_all)
     returned = returned.reshape(slots, 2 * width)
     picked = [
         contract(select_tk[:, k, :], returned, 1, 0) for k in range(top_count)

time: 206 us -> 203 us (0.985)
    ppermute x10, waiting for transfers between devices: 45.5 us -> 6.36 us  [all_sum(): lax.ppermute(total, AXES, [(i, i ^ x * step) for i in range(devices_all)])]
    all_to_all x1, waiting for transfers between devices: 0.01 us -> 38.1 us  [exchange(): return lax.all_to_all(rows, AXES, split_axis=0, concat_axis=0, tiled=True)]
  transfers between devices with their start and end apart: 11 -> 11, of which waited for: 3 -> 5; matrix products, arithmetic and copies ran while one was open for 7% -> 13% of each run, Pallas kernels for 0% -> 0%
where the time goes in v6:
time: 203 us
  blocking collectives  63 us (31%)
  waiting for transfers between devices  44.5 us (22%)
  matrix products  33.4 us (16%)
  local copies, waits for them, and re-layouts  27.7 us (14%)
  starting transfers between devices  21.1 us (10%)
  other arithmetic  11.8 us (6%)
    all_to_all x1, blocking collectives, exchange(): return lax.all_to_all(rows, AXES, split_axis=0, concat_axis=0, tiled=True)  63 us
    all_to_all x1, waiting for transfers between devices, exchange(): return lax.all_to_all(rows, AXES, split_axis=0, concat_axis=0, tiled=True)  38.1 us
    dot_general x8, matrix products, contract(): lax.dot_general(left, right, (((left_dim,), (right_dim,)), ((), ())), pre...  24.7 us
    ppermute x10, starting transfers between devices, all_sum(): lax.ppermute(total, AXES, [(i, i ^ x * step) for i in range(devices_all)])  13.9 us
    reshape x1, local copies, waits for them, and re-layouts, on_device(): jnp.concatenate([expert_out, grad_back], axis=1)  7.21 us
    all_to_all x1, starting transfers between devices, exchange(): return lax.all_to_all(rows, AXES, split_axis=0, concat_axis=0, tiled=True)  7.13 us
    reshape x1, local copies, waits for them, and re-layouts, on_device(): arrived_all = exchange(sent).reshape(slots, 2 * width)  6.89 us
    reshape x1, local copies, waits for them, and re-layouts, on_device(): returned = returned.reshape(slots, 2 * width)  6.88 us
  transfers between devices with their start and end apart: 11, of which 5 were waited for; matrix products, arithmetic and copies ran while one was open for 13% of the time, Pallas kernels for 0%

profile of v6, /device:TPU:0, one launch (start us, length us, event | category | flops | bytes accessed | tf_op | source)
XLA Modules:
  0.0 202.6 jit_solution(11039934840000253612)
XLA Ops:
  0.6 0.0 copy-start
  0.7 0.9 copy.37
  1.6 0.1 eq.62
  1.7 0.1 eq.58
  1.9 0.1 copy.39
  2.0 0.2 fusion.45
  2.3 0.2 fusion.47
  2.5 0.1 reduce_sum.78
  2.6 0.1 copy.41
  2.7 0.7 multiply_add_fusion.1
  3.4 2.1 %convert_element_type.72 = f32[128,2048]{1,0:T(8,128)} convert(bf16[128,2048]{1,0:T(8,128)(2,1)} %param.15) | non-fusion elementwise | flops 262144 | bytes 1572864 | tf_op jit(solution)/shard_map/convert_element_type | solution.py:83
  5.5 0.1 convert_reduce_fusion
  5.6 0.1 copy.42
  5.8 0.0 copy-start.8
  5.8 1.8 convolution_convert_fusion.3
  7.6 0.8 bitcast_convert_fusion
  8.4 0.3 pad_maximum_fusion
  8.7 3.2 %copy.44 = bf16[128,4,4096]{2,1,0:T(4,128)(2,1)S(1)} copy(bf16[128,4,4096]{2,0,1:T(8,128)(2,1)S(1)} %pad_maximum_fusion) | data formatting | bytes 8388608 | tf_op jit(solution)/shard_map/concatenate | solution.py:91
  12.0 63.0 %all_to_all.10 = bf16[128,4,4096]{2,1,0:T(4,128)(2,1)} all-to-all(bf16[128,4,4096]{2,1,0:T(4,128)(2,1)S(1)} %copy.44), channel_id=1, replica_groups=mesh['expert'=16,'dp'=8] {'expert','dp'}, dimensions={0} | all-to-all | bytes 8388608 | tf_op jit(solution)/shard_map/all_to_all | solution.py:10
  74.9 6.9 %reshape.108 = bf16[512,4096]{1,0:T(8,128)(2,1)} reshape(bf16[128,4,4096]{2,1,0:T(4,128)(2,1)} %all_to_all.10) | data formatting | bytes 8388608 | tf_op jit(solution)/shard_map/reshape | solution.py:92
  81.8 2.1 %fusion.4 = f32[512]{0:T(512)S(1)} fusion(bf16[512,4096]{1,0:T(8,128)(2,1)} %reshape.108), kind=kLoop, calls=%fused_computation.6 | loop fusion | flops 3145216 | bytes 2099200 | tf_op jit(solution)/shard_map/reduce_sum | solution.py:95
  83.9 0.0 copy-start.9
  83.9 0.0 copy-start.12
  84.0 4.5 %fusion.5 = f32[512,768]{1,0:T(8,128)S(1)} fusion(bf16[1,768,2048]{2,1,0:T(8,128)(2,1)} %param.14, bf16[512,4096]{1,0:T(8,128)(2,1)} %reshape.108), kind=kOutput, calls=%fused_computation.14 | convolution fusion | flops 1610612736 | bytes 6815744 | tf_op jit(solution)/shard_map/dot_general | solution.py:14
  88.5 0.2 copy-done.12
  88.7 1.9 fusion.15
  90.6 2.4 %multiply_convert_fusion.3 = (bf16[512,768]{1,0:T(8,128)(2,1)S(1)}, bf16[512,768]{1,0:T(8,128)(2,1)S(1)}, bf16[512,768]{1,0:T(8,128)(2,1)S(1)}) fusion(f32[512,768]{1,0:T(8,128)S(1)} %fusion.15, f32[512,768]{1,0:T(8,128)S(1)} %fusion.5, bf16[1,2048,768]{2,1,0:T(8,128)(2,1)S(1)} %copy-done, f32[2048]{0:T(1024)S(1)} %copy-done.9, f32[512]{0:T(512)S(1)} %add_rsqrt_fusion, ...), kind=kOutput, calls=%fused_computation.33 | convolution fusion | flops 1620705280 | bytes 10758144 | tf_op jit(solution)/shard_map/dot_general | solution.py:41
  93.0 0.0 copy-start.17
  93.0 0.0 copy-start.13
  93.0 1.8 fusion.9
  94.9 0.9 copy-done.11
  95.7 1.8 fusion.17
  97.6 2.0 fusion.3
  99.5 2.5 %pad_maximum_fusion.1 = bf16[512,4096]{1,0:T(8,128)(2,1)} fusion(bf16[512,2048]{1,0:T(8,128)(2,1)S(1)} %get-tuple-element.28, bf16[512,2048]{1,0:T(8,128)(2,1)S(1)} %fusion.17), kind=kLoop, calls=%fused_computation.8 | loop fusion | flops 8388608 | bytes 8388608 | tf_op jit(solution)/shard_map/concatenate | solution.py:104
  102.0 7.2 %reshape.109 = bf16[128,4,4096]{2,1,0:T(4,128)(2,1)} reshape(bf16[512,4096]{1,0:T(8,128)(2,1)} %pad_maximum_fusion.1) | data formatting | bytes 8388608 | tf_op jit(solution)/shard_map/reshape | solution.py:104
  109.2 7.1 %all-to-all-start.1 = ((bf16[128,4,4096]{2,1,0:T(4,128)(2,1)}), bf16[128,4,4096]{2,1,0:T(4,128)(2,1)}, u32[]{:S(2)}, u32[]{:S(2)}) async-start(bf16[128,4,4096]{2,1,0:T(4,128)(2,1)} %reshape.109), calls=%async_computation.1 | async-start | bytes 8388608 | tf_op jit(solution)/shard_map/all_to_all | solution.py:10
  116.5 0.2 fusion.33
  116.7 0.1 iota_compare_fusion
  116.9 5.2 %convolution_convert_fusion = bf16[768,2048]{1,0:T(8,128)(2,1)} fusion(bf16[512,768]{1,0:T(8,128)(2,1)S(1)} %copy-done.18, bf16[512,4096]{1,0:T(8,128)(2,1)} %reshape.108), kind=kOutput, calls=%fused_computation.11 | convolution fusion | flops 1612185600 | bytes 6029312 | tf_op jit(solution)/shard_map/dot_general | solution.py:14
  122.2 3.7 %convolution_convert_fusion.1 = bf16[2048,768]{1,0:T(8,128)(2,1)} fusion(bf16[512,768]{1,0:T(8,128)(2,1)S(1)} %copy-done.16, f32[2048]{0:T(1024)S(1)} %copy-done.9, f32[512]{0:T(512)S(1)} %add_rsqrt_fusion, bf16[512,4096]{1,0:T(8,128)(2,1)S(1)} %copy-done.4), kind=kOutput, calls=%fused_computation.12 | convolution fusion | flops 1616379904 | bytes 6039552 | tf_op jit(solution)/shard_map/dot_general | solution.py:14
  125.8 3.7 %convolution_convert_fusion.2 = bf16[2048,768]{1,0:T(8,128)(2,1)} fusion(bf16[512,768]{1,0:T(8,128)(2,1)S(1)} %copy-done.14, f32[2048]{0:T(1024)S(1)} %copy-done.9, f32[512]{0:T(512)S(1)} %add_rsqrt_fusion, bf16[512,4096]{1,0:T(8,128)(2,1)S(1)} %copy-done.4), kind=kOutput, calls=%fused_computation.13 | convolution fusion | flops 1616379904 | bytes 6039552 | tf_op jit(solution)/shard_map/dot_general | solution.py:14
  129.5 38.1 %all-to-all-done.1 = bf16[128,4,4096]{2,1,0:T(4,128)(2,1)} async-done(((bf16[128,4,4096]{2,1,0:T(4,128)(2,1)}), bf16[128,4,4096]{2,1,0:T(4,128)(2,1)}, u32[]{:S(2)}, u32[]{:S(2)}) %all-to-all-start.1) | async-done | bytes 4194336 | tf_op jit(solution)/shard_map/all_to_all | solution.py:10
  167.6 0.8 collective-permute-start
  168.4 0.9 collective-permute-start.1
  169.3 1.8 collective-permute-start.2
  171.1 6.9 %reshape.110 = bf16[512,4096]{1,0:T(8,128)(2,1)} reshape(bf16[128,4,4096]{2,1,0:T(4,128)(2,1)} %all-to-all-done.1) | data formatting | bytes 8388608 | tf_op jit(solution)/shard_map/reshape | solution.py:111
  178.0 3.1 %fusion.44 = f32[128,4096]{1,0:T(8,128)S(1)} fusion(bf16[512,4096]{1,0:T(8,128)(2,1)} %reshape.110, pred[128,2,512]{2,0,1:T(32,128)(4,1)S(1)} %iota_compare_fusion), kind=kOutput, calls=%fused_computation.64 | convolution fusion | flops 536870912 | bytes 6356992 | tf_op jit(solution)/shard_map/dot_general | solution.py:14
  181.1 0.4 copy-done.2
  181.4 0.7 fusion.43
  182.2 0.3 copy-done.7
  182.5 0.6 fusion.27
  183.1 2.1 %collective-permute-start.3 = (f32[2048]{0:T(1024)S(1)}, f32[2048]{0:T(1024)S(1)}, u32[]{:S(2)}, u32[]{:S(2)}) collective-permute-start(f32[2048]{0:T(1024)S(1)} %add_add_fusion.2), channel_id=1, source_target_pairs={{0,4},{1,5},{2,6},{3,7},{4,0},{5,1},{6,2},{7,3},{8,12},{9,13},{10,... | collective-permute-start | bytes 24584 | tf_op jit(solution)/shard_map/ppermute | solution.py:26
  185.3 1.6 collective-permute-start.5
  186.9 1.5 collective-permute-done.3
  188.4 1.5 collective-permute-done.5
  189.9 0.3 collective-permute-start.6
  190.1 1.7 collective-permute-start.7
  191.9 2.8 %collective-permute-start.8 = (f32[2048]{0:T(1024)S(1)}, f32[2048]{0:T(1024)S(1)}, u32[]{:S(2)}, u32[]{:S(2)}) collective-permute-start(f32[2048]{0:T(1024)S(1)} %add_add_fusion.1), channel_id=1, source_target_pairs={{0,48},{1,49},{2,50},{3,51},{4,52},{5,53},{6,54},{7,55},{8,56},{9,... | collective-permute-start | bytes 24584 | tf_op jit(solution)/shard_map/ppermute | solution.py:26
  194.6 1.4 fusion.31
  196.1 0.6 collective-permute-done.8
  196.8 1.9 collective-permute-start.9
  198.7 0.6 pad_maximum_fusion.2
  199.3 2.7 %collective-permute-done.9 = f32[2048]{0:T(1024)S(1)} collective-permute-done((f32[2048]{0:T(1024)S(1)}, f32[2048]{0:T(1024)S(1)}, u32[]{:S(2)}, u32[]{:S(2)}) %collective-permute-start.9) | collective-permute-done | bytes 8224 | tf_op jit(solution)/shard_map/ppermute | solution.py:26
  202.0 0.6 select_add_fusion
  (49 shorter events, 0.2 us)
Async XLA Ops:
  0.6 89.9 %copy-start = (bf16[1,2048,768]{2,1,0:T(8,128)(2,1)S(1)}, bf16[1,2048,768]{2,1,0:T(8,128)(2,1)}, u32[]{:S(2)}) copy-start(bf16[1,2048,768]{2,1,0:T(8,128)(2,1)} %param.13) | copy-start | bytes 9437188
  0.6 7.0 %copy-start.10 = (f32[128,2]{0,1:T(2,128)S(1)}, f32[128,2]{0,1:T(2,128)}, u32[]{:S(2)}) copy-start(f32[128,2]{0,1:T(2,128)} %param.10) | copy-start | bytes 3076
  5.8 1.9 copy-start.8
  83.9 4.5 %copy-start.3 = (bf16[512,4096]{1,0:T(8,128)(2,1)S(1)}, bf16[512,4096]{1,0:T(8,128)(2,1)}, u32[]{:S(2)}) copy-start(bf16[512,4096]{1,0:T(8,128)(2,1)} %reshape.108) | copy-start | bytes 12582916
  83.9 4.5 %copy-start.9 = (f32[2048]{0:T(1024)S(1)}, f32[2048]{0:T(1024)}, u32[]{:S(2)}) copy-start(f32[2048]{0:T(1024)} %param.11) | copy-start | bytes 24580
  83.9 4.7 %copy-start.12 = (bf16[1,2048,768]{2,1,0:T(8,128)(2,1)S(1)}, bf16[1,2048,768]{2,1,0:T(8,128)(2,1)}, u32[]{:S(2)}) copy-start(bf16[1,2048,768]{2,1,0:T(8,128)(2,1)} %param.12) | copy-start | bytes 9437188
  93.0 1.9 copy-start.15
  93.0 1.9 copy-start.17
  93.0 4.6 %copy-start.13 = (bf16[512,768]{1,0:T(8,128)(2,1)}, bf16[512,768]{1,0:T(8,128)(2,1)S(1)}, u32[]{:S(2)}) copy-start(bf16[512,768]{1,0:T(8,128)(2,1)S(1)} %get-tuple-element.23) | copy-start | bytes 2359300
  93.0 2.7 %copy-start.11 = (bf16[1,768,2048]{2,1,0:T(8,128)(2,1)S(1)}, bf16[1,768,2048]{2,1,0:T(8,128)(2,1)}, u32[]{:S(2)}) copy-start(bf16[1,768,2048]{2,1,0:T(8,128)(2,1)} %param.14) | copy-start | bytes 9437188
  109.2 7.3 %copy-start.5 = (bf16[128,2048]{1,0:T(8,128)(2,1)S(1)}, bf16[128,2048]{1,0:T(8,128)(2,1)}, u32[]{:S(2)}) copy-start(bf16[128,2048]{1,0:T(8,128)(2,1)} %param.8) | copy-start | bytes 1572868
  109.2 7.7 %copy-start.18 = (bf16[512,768]{1,0:T(8,128)(2,1)S(1)}, bf16[512,768]{1,0:T(8,128)(2,1)}, u32[]{:S(2)}) copy-start(bf16[512,768]{1,0:T(8,128)(2,1)} %copy-done.17) | copy-start | bytes 2359300
  109.2 58.4 %all-to-all-start.1 = ((bf16[128,4,4096]{2,1,0:T(4,128)(2,1)}), bf16[128,4,4096]{2,1,0:T(4,128)(2,1)}, u32[]{:S(2)}, u32[]{:S(2)}) async-start(bf16[128,4,4096]{2,1,0:T(4,128)(2,1)} %reshape.109), calls=%async_computation.1 | async-start | bytes 8388608 | tf_op jit(solution)/shard_map/all_to_all | solution.py:10
  116.9 5.3 %copy-start.4 = (bf16[512,4096]{1,0:T(8,128)(2,1)S(1)}, bf16[512,4096]{1,0:T(8,128)(2,1)}, u32[]{:S(2)}) copy-start(bf16[512,4096]{1,0:T(8,128)(2,1)} %reshape.108) | copy-start | bytes 12582916
  116.9 5.3 %copy-start.16 = (bf16[512,768]{1,0:T(8,128)(2,1)S(1)}, bf16[512,768]{1,0:T(8,128)(2,1)}, u32[]{:S(2)}) copy-start(bf16[512,768]{1,0:T(8,128)(2,1)} %copy-done.15) | copy-start | bytes 2359300
  122.2 3.7 %copy-start.14 = (bf16[512,768]{1,0:T(8,128)(2,1)S(1)}, bf16[512,768]{1,0:T(8,128)(2,1)}, u32[]{:S(2)}) copy-start(bf16[512,768]{1,0:T(8,128)(2,1)} %copy-done.13) | copy-start | bytes 2359300
  167.6 15.5 %collective-permute-start = (f32[2048]{0:T(1024)S(1)}, f32[2048]{0:T(1024)S(1)}, u32[]{:S(2)}, u32[]{:S(2)}) collective-permute-start(f32[2048]{0:T(1024)S(1)} %get-tuple-element.13), channel_id=1, source_target_pairs={{0,1},{1,0},{2,3},{3,2},{4,5},{5,4},{6,7},{7,6},{8,9},{9,8},{10,11... | collective-permute-start | bytes 24584 | tf_op jit(solution)/shard_map/ppermute | solution.py:26
  168.4 14.7 %collective-permute-start.1 = (f32[2048]{0:T(1024)S(1)}, f32[2048]{0:T(1024)S(1)}, u32[]{:S(2)}, u32[]{:S(2)}) collective-permute-start(f32[2048]{0:T(1024)S(1)} %get-tuple-element.13), channel_id=1, source_target_pairs={{0,2},{1,3},{2,0},{3,1},{4,6},{5,7},{6,4},{7,5},{8,10},{9,11},{10,... | collective-permute-start | bytes 24584 | tf_op jit(solution)/shard_map/ppermute | solution.py:26
  169.3 13.8 %collective-permute-start.2 = (f32[2048]{0:T(1024)S(1)}, f32[2048]{0:T(1024)S(1)}, u32[]{:S(2)}, u32[]{:S(2)}) collective-permute-start(f32[2048]{0:T(1024)S(1)} %get-tuple-element.13), channel_id=1, source_target_pairs={{0,3},{1,2},{2,1},{3,0},{4,7},{5,6},{6,5},{7,4},{8,11},{9,10},{10,... | collective-permute-start | bytes 24584 | tf_op jit(solution)/shard_map/ppermute | solution.py:26
  178.0 3.4 %copy-start.2 = (bf16[512,4096]{1,0:T(8,128)(2,1)S(1)}, bf16[512,4096]{1,0:T(8,128)(2,1)}, u32[]{:S(2)}) copy-start(bf16[512,4096]{1,0:T(8,128)(2,1)} %reshape.110) | copy-start | bytes 12582916
  181.4 1.0 copy-start.7
  182.5 12.2 %copy-start.6 = (bf16[128,2048]{1,0:T(8,128)(2,1)S(1)}, bf16[128,2048]{1,0:T(8,128)(2,1)}, u32[]{:S(2)}) copy-start(bf16[128,2048]{1,0:T(8,128)(2,1)} %param.8) | copy-start | bytes 1572868
  183.1 5.2 %collective-permute-start.3 = (f32[2048]{0:T(1024)S(1)}, f32[2048]{0:T(1024)S(1)}, u32[]{:S(2)}, u32[]{:S(2)}) collective-permute-start(f32[2048]{0:T(1024)S(1)} %add_add_fusion.2), channel_id=1, source_target_pairs={{0,4},{1,5},{2,6},{3,7},{4,0},{5,1},{6,2},{7,3},{8,12},{9,13},{10,... | collective-permute-start | bytes 24584 | tf_op jit(solution)/shard_map/ppermute | solution.py:26
  185.3 3.1 %collective-permute-start.4 = (f32[2048]{0:T(1024)S(1)}, f32[2048]{0:T(1024)S(1)}, u32[]{:S(2)}, u32[]{:S(2)}) collective-permute-start(f32[2048]{0:T(1024)S(1)} %add_add_fusion.2), channel_id=1, source_target_pairs={{0,8},{1,9},{2,10},{3,11},{4,12},{5,13},{6,14},{7,15},{8,0},{9,1},... | collective-permute-start | bytes 24584 | tf_op jit(solution)/shard_map/ppermute | solution.py:26
  185.3 4.6 %collective-permute-start.5 = (f32[2048]{0:T(1024)S(1)}, f32[2048]{0:T(1024)S(1)}, u32[]{:S(2)}, u32[]{:S(2)}) collective-permute-start(f32[2048]{0:T(1024)S(1)} %add_add_fusion.2), channel_id=1, source_target_pairs={{0,12},{1,13},{2,14},{3,15},{4,8},{5,9},{6,10},{7,11},{8,4},{9,5},... | collective-permute-start | bytes 24584 | tf_op jit(solution)/shard_map/ppermute | solution.py:26
  189.9 6.2 %collective-permute-start.6 = (f32[2048]{0:T(1024)S(1)}, f32[2048]{0:T(1024)S(1)}, u32[]{:S(2)}, u32[]{:S(2)}) collective-permute-start(f32[2048]{0:T(1024)S(1)} %add_add_fusion.1), channel_id=1, source_target_pairs={{0,16},{1,17},{2,18},{3,19},{4,20},{5,21},{6,22},{7,23},{8,24},{9,... | collective-permute-start | bytes 24584 | tf_op jit(solution)/shard_map/ppermute | solution.py:26
  190.1 6.0 %collective-permute-start.7 = (f32[2048]{0:T(1024)S(1)}, f32[2048]{0:T(1024)S(1)}, u32[]{:S(2)}, u32[]{:S(2)}) collective-permute-start(f32[2048]{0:T(1024)S(1)} %add_add_fusion.1), channel_id=1, source_target_pairs={{0,32},{1,33},{2,34},{3,35},{4,36},{5,37},{6,38},{7,39},{8,40},{9,... | collective-permute-start | bytes 24584 | tf_op jit(solution)/shard_map/ppermute | solution.py:26
  191.9 4.9 %collective-permute-start.8 = (f32[2048]{0:T(1024)S(1)}, f32[2048]{0:T(1024)S(1)}, u32[]{:S(2)}, u32[]{:S(2)}) collective-permute-start(f32[2048]{0:T(1024)S(1)} %add_add_fusion.1), channel_id=1, source_target_pairs={{0,48},{1,49},{2,50},{3,51},{4,52},{5,53},{6,54},{7,55},{8,56},{9,... | collective-permute-start | bytes 24584 | tf_op jit(solution)/shard_map/ppermute | solution.py:26
  194.6 7.9 %copy-start.1 = (bf16[1,2048,768]{2,1,0:T(8,128)(2,1)S(1)}, bf16[1,2048,768]{2,1,0:T(8,128)(2,1)}, u32[]{:S(2)}) copy-start(bf16[1,2048,768]{2,1,0:T(8,128)(2,1)} %param.13) | copy-start | bytes 9437188
  196.8 5.2 %collective-permute-start.9 = (f32[2048]{0:T(1024)S(1)}, f32[2048]{0:T(1024)S(1)}, u32[]{:S(2)}, u32[]{:S(2)}) collective-permute-start(f32[2048]{0:T(1024)S(1)} %add_add_fusion), channel_id=1, source_target_pairs={{0,64},{1,65},{2,66},{3,67},{4,68},{5,69},{6,70},{7,71},{8,72},{9,... | collective-permute-start | bytes 24584 | tf_op jit(solution)/shard_map/ppermute | solution.py:26

commit v7 on v6

--- a/solution.py
+++ b/solution.py
@@ -108,9 +108,10 @@
         (exchange(back), grad_gate, grad_up, grad_down, gain_part)
     )
     grad_gain = all_sum(gain_part, devices_all)
-    returned = returned.reshape(slots, 2 * width)
+    pair_slot = slot_index.reshape(tok_rows, top_count)
     picked = [
-        contract(select_tk[:, k, :], returned, 1, 0) for k in range(top_count)
+        returned[pair_slot[:, k] // capacity, pair_slot[:, k] % capacity].astype(jnp.float32)
+        for k in range(top_count)
     ]
     outs = [p[:, :width] for p in picked]
     backs = [p[:, width:] for p in picked]

time: 203 us -> 206 us (1.015)
  other arithmetic: 11.8 us -> 16.4 us
  matrix products: 33.4 us -> 29.6 us
    gather x0 -> x2, local copies, waits for them, and re-layouts: none -> 9.48 us  [on_device(): returned[pair_slot[:, k] // capacity, pair_slot[:, k] % capacity]]
    reshape x1 -> x0, local copies, waits for them, and re-layouts: 6.88 us -> none  [on_device(): returned = returned.reshape(slots, 2 * width)]
    dot_general x8 -> x6, matrix products: 24.7 us -> 20.9 us  [contract(): lax.dot_general(left, right, (((left_dim,), (right_dim,)), ((), ())), pre...]
    convert_element_type x0 -> x2, other arithmetic: none -> 2.91 us  [on_device(): returned[pair_slot[:, k] // capacity, pair_slot[:, k] % capacity]]
  transfers between devices with their start and end apart: 11 -> 11, of which waited for: 5 -> 4; matrix products, arithmetic and copies ran while one was open for 13% -> 14% of each run, Pallas kernels for 0% -> 0%
where the time goes in v7:
time: 206 us; the launch traced here: 205 us
  blocking collectives  63 us (31%)
  waiting for transfers between devices  45.1 us (22%)
  local copies, waits for them, and re-layouts  29.7 us (14%)
  matrix products  29.6 us (14%)
  starting transfers between devices  19.9 us (10%)
  other arithmetic  16.4 us (8%)
    all_to_all x1, blocking collectives, exchange(): return lax.all_to_all(rows, AXES, split_axis=0, concat_axis=0, tiled=True)  63 us
    all_to_all x1, waiting for transfers between devices, exchange(): return lax.all_to_all(rows, AXES, split_axis=0, concat_axis=0, tiled=True)  38.2 us
    dot_general x6, matrix products, contract(): lax.dot_general(left, right, (((left_dim,), (right_dim,)), ((), ())), pre...  20.9 us
    ppermute x10, starting transfers between devices, all_sum(): lax.ppermute(total, AXES, [(i, i ^ x * step) for i in range(devices_all)])  12.8 us
    gather x2, local copies, waits for them, and re-layouts, on_device(): returned[pair_slot[:, k] // capacity, pair_slot[:, k] % capacity]  9.48 us
    reshape x1, local copies, waits for them, and re-layouts, on_device(): jnp.concatenate([expert_out, grad_back], axis=1)  7.2 us
    all_to_all x1, starting transfers between devices, exchange(): return lax.all_to_all(rows, AXES, split_axis=0, concat_axis=0, tiled=True)  7.12 us
    reshape x1, local copies, waits for them, and re-layouts, on_device(): arrived_all = exchange(sent).reshape(slots, 2 * width)  6.94 us
  transfers between devices with their start and end apart: 11, of which 4 were waited for; matrix products, arithmetic and copies ran while one was open for 14% of the time, Pallas kernels for 0%

profile of v7, /device:TPU:0, one launch (start us, length us, event | category | flops | bytes accessed | tf_op | source)
XLA Modules:
  0.0 204.9 jit_solution(11667800711288605446)
XLA Ops:
  0.6 0.0 copy-start
  0.7 0.9 copy.54
  1.6 0.1 eq.64
  1.7 0.1 eq.60
  1.9 0.1 copy.56
  2.0 0.2 fusion.45
  2.3 0.2 fusion.47
  2.5 0.1 reduce_sum.78
  2.6 0.1 copy.58
  2.7 0.7 multiply_add_fusion.1
  3.4 2.1 %convert_element_type.78 = f32[128,2048]{1,0:T(8,128)} convert(bf16[128,2048]{1,0:T(8,128)(2,1)} %param.15) | non-fusion elementwise | flops 262144 | bytes 1572864 | tf_op jit(solution)/shard_map/convert_element_type | solution.py:83
  5.5 0.1 fusion.42
  5.6 0.1 copy.59
  5.8 0.0 copy-start.8
  5.8 1.8 convolution_convert_fusion.3
  7.6 0.8 bitcast_convert_fusion
  8.4 0.3 pad_maximum_fusion
  8.7 3.2 %copy.61 = bf16[128,4,4096]{2,1,0:T(4,128)(2,1)S(1)} copy(bf16[128,4,4096]{2,0,1:T(8,128)(2,1)S(1)} %pad_maximum_fusion) | data formatting | bytes 8388608 | tf_op jit(solution)/shard_map/concatenate | solution.py:91
  12.0 63.0 %all_to_all.10 = bf16[128,4,4096]{2,1,0:T(4,128)(2,1)} all-to-all(bf16[128,4,4096]{2,1,0:T(4,128)(2,1)S(1)} %copy.61), channel_id=1, replica_groups=mesh['expert'=16,'dp'=8] {'expert','dp'}, dimensions={0} | all-to-all | bytes 8388608 | tf_op jit(solution)/shard_map/all_to_all | solution.py:10
  74.9 6.9 %reshape.99 = bf16[512,4096]{1,0:T(8,128)(2,1)} reshape(bf16[128,4,4096]{2,1,0:T(4,128)(2,1)} %all_to_all.10) | data formatting | bytes 8388608 | tf_op jit(solution)/shard_map/reshape | solution.py:92
  81.9 2.1 %fusion.4 = f32[512]{0:T(512)S(1)} fusion(bf16[512,4096]{1,0:T(8,128)(2,1)} %reshape.99), kind=kLoop, calls=%fused_computation.8 | loop fusion | flops 3145216 | bytes 2099200 | tf_op jit(solution)/shard_map/reduce_sum | solution.py:95
  84.0 0.0 copy-start.9
  84.0 0.0 copy-start.12
  84.0 4.5 %fusion.5 = f32[512,768]{1,0:T(8,128)S(1)} fusion(bf16[1,768,2048]{2,1,0:T(8,128)(2,1)} %param.14, bf16[512,4096]{1,0:T(8,128)(2,1)} %reshape.99), kind=kOutput, calls=%fused_computation.16 | convolution fusion | flops 1610612736 | bytes 6815744 | tf_op jit(solution)/shard_map/dot_general | solution.py:14
  88.5 0.2 copy-done.12
  88.7 1.9 fusion.15
  90.6 2.4 %multiply_convert_fusion.3 = (bf16[512,768]{1,0:T(8,128)(2,1)S(1)}, bf16[512,768]{1,0:T(8,128)(2,1)S(1)}, bf16[512,768]{1,0:T(8,128)(2,1)S(1)}) fusion(f32[512,768]{1,0:T(8,128)S(1)} %fusion.15, f32[512,768]{1,0:T(8,128)S(1)} %fusion.5, bf16[1,2048,768]{2,1,0:T(8,128)(2,1)S(1)} %copy-done, f32[2048]{0:T(1024)S(1)} %copy-done.9, f32[512]{0:T(512)S(1)} %add_rsqrt_fusion, ...), kind=kOutput, calls=%fused_computation.35 | convolution fusion | flops 1620705280 | bytes 10758144 | tf_op jit(solution)/shard_map/dot_general | solution.py:41
  93.0 0.0 copy-start.15
  93.0 0.0 copy-start.17
  93.0 0.0 copy-start.13
  93.1 0.0 copy-start.11
  93.1 1.8 fusion.9
  94.9 0.9 copy-done.11
  95.8 1.8 fusion.17
  97.6 2.0 fusion.3
  99.6 2.4 %pad_maximum_fusion.1 = bf16[512,4096]{1,0:T(8,128)(2,1)} fusion(bf16[512,2048]{1,0:T(8,128)(2,1)S(1)} %get-tuple-element.30, bf16[512,2048]{1,0:T(8,128)(2,1)S(1)} %fusion.17), kind=kLoop, calls=%fused_computation.10 | loop fusion | flops 8388608 | bytes 8388608 | tf_op jit(solution)/shard_map/concatenate | solution.py:104
  102.0 7.2 %reshape.100 = bf16[128,4,4096]{2,1,0:T(4,128)(2,1)} reshape(bf16[512,4096]{1,0:T(8,128)(2,1)} %pad_maximum_fusion.1) | data formatting | bytes 8388608 | tf_op jit(solution)/shard_map/reshape | solution.py:104
  109.2 7.1 %all-to-all-start.1 = ((bf16[128,4,4096]{2,1,0:T(4,128)(2,1)}), bf16[128,4,4096]{2,1,0:T(4,128)(2,1)}, u32[]{:S(2)}, u32[]{:S(2)}) async-start(bf16[128,4,4096]{2,1,0:T(4,128)(2,1)} %reshape.100), calls=%async_computation.1 | async-start | bytes 8388608 | tf_op jit(solution)/shard_map/all_to_all | solution.py:10
  116.5 0.2 fusion.33
  116.8 0.0 copy-start.16
  116.8 5.2 %convolution_convert_fusion = bf16[768,2048]{1,0:T(8,128)(2,1)} fusion(bf16[512,768]{1,0:T(8,128)(2,1)S(1)} %copy-done.18, bf16[512,4096]{1,0:T(8,128)(2,1)} %reshape.99), kind=kOutput, calls=%fused_computation.13 | convolution fusion | flops 1612185600 | bytes 6029312 | tf_op jit(solution)/shard_map/dot_general | solution.py:14
  122.1 3.7 %convolution_convert_fusion.1 = bf16[2048,768]{1,0:T(8,128)(2,1)} fusion(bf16[512,768]{1,0:T(8,128)(2,1)S(1)} %copy-done.16, f32[2048]{0:T(1024)S(1)} %copy-done.9, f32[512]{0:T(512)S(1)} %add_rsqrt_fusion, bf16[512,4096]{1,0:T(8,128)(2,1)S(1)} %copy-done.4), kind=kOutput, calls=%fused_computation.14 | convolution fusion | flops 1616379904 | bytes 6039552 | tf_op jit(solution)/shard_map/dot_general | solution.py:14
  125.7 3.7 %convolution_convert_fusion.2 = bf16[2048,768]{1,0:T(8,128)(2,1)} fusion(bf16[512,768]{1,0:T(8,128)(2,1)S(1)} %copy-done.14, f32[2048]{0:T(1024)S(1)} %copy-done.9, f32[512]{0:T(512)S(1)} %add_rsqrt_fusion, bf16[512,4096]{1,0:T(8,128)(2,1)S(1)} %copy-done.4), kind=kOutput, calls=%fused_computation.15 | convolution fusion | flops 1616379904 | bytes 6039552 | tf_op jit(solution)/shard_map/dot_general | solution.py:14
  129.4 38.2 %all-to-all-done.1 = bf16[128,4,4096]{2,1,0:T(4,128)(2,1)} async-done(((bf16[128,4,4096]{2,1,0:T(4,128)(2,1)}), bf16[128,4,4096]{2,1,0:T(4,128)(2,1)}, u32[]{:S(2)}, u32[]{:S(2)}) %all-to-all-start.1) | async-done | bytes 4194336 | tf_op jit(solution)/shard_map/all_to_all | solution.py:10
  167.6 0.8 collective-permute-start
  168.5 0.9 collective-permute-start.1
  169.3 1.8 collective-permute-start.2
  171.1 4.7 %gather_fusion = bf16[128,4096]{1,0:T(8,128)(2,1)} fusion(bf16[128,4,4096]{2,1,0:T(4,128)(2,1)} %all-to-all-done.1, s32[128]{0:T(128)S(1)} %get-tuple-element.27), kind=kCustom, calls=%fused_computation | custom fusion | bytes 2098176 | tf_op jit(solution)/shard_map/gather | solution.py:113
  175.8 1.4 convert_element_type.92
  177.2 4.8 %gather_fusion.1 = bf16[128,4096]{1,0:T(8,128)(2,1)} fusion(bf16[128,4,4096]{2,1,0:T(4,128)(2,1)} %all-to-all-done.1, s32[128]{0:T(128)S(1)} %get-tuple-element.28), kind=kCustom, calls=%fused_computation.1 | custom fusion | bytes 2098176 | tf_op jit(solution)/shard_map/gather | solution.py:113
  182.0 1.5 convert_element_type.93
  183.6 0.7 fusion.27
  184.3 2.2 %collective-permute-start.3 = (f32[2048]{0:T(1024)S(1)}, f32[2048]{0:T(1024)S(1)}, u32[]{:S(2)}, u32[]{:S(2)}) collective-permute-start(f32[2048]{0:T(1024)S(1)} %add_add_fusion.2), channel_id=1, source_target_pairs={{0,4},{1,5},{2,6},{3,7},{4,0},{5,1},{6,2},{7,3},{8,12},{9,13},{10,... | collective-permute-start | bytes 24584 | tf_op jit(solution)/shard_map/ppermute | solution.py:26
  186.4 1.6 collective-permute-start.5
  188.0 1.5 collective-permute-done.3
  189.5 1.5 collective-permute-done.5
  191.0 0.2 collective-permute-start.6
  191.3 1.8 collective-permute-start.7
  193.1 2.8 %collective-permute-start.8 = (f32[2048]{0:T(1024)S(1)}, f32[2048]{0:T(1024)S(1)}, u32[]{:S(2)}, u32[]{:S(2)}) collective-permute-start(f32[2048]{0:T(1024)S(1)} %add_add_fusion.1), channel_id=1, source_target_pairs={{0,48},{1,49},{2,50},{3,51},{4,52},{5,53},{6,54},{7,55},{8,56},{9,... | collective-permute-start | bytes 24584 | tf_op jit(solution)/shard_map/ppermute | solution.py:26
  195.8 3.2 %fusion.31 = (bf16[128,2048]{1,0:T(8,128)(2,1)}, bf16[128,2048]{1,0:T(8,128)(2,1)}) fusion(bf16[128,2048]{1,0:T(8,128)(2,1)S(1)} %copy-done.6, bf16[128,2048]{1,0:T(8,128)(2,1)S(1)} %copy-done.7, f32[128]{0:T(128)S(1)} %broadcast_multiply_fusion, f32[128]{0:T(128)S(1)} %add_rsqrt_fusion.1, f32[2048]{0:T(1024)S(1)} %copy-done.9, ...), kind=kLoop, calls=%fused_computation.47 | loop fusion | flops 3932160 | bytes 6301696 | tf_op jit(solution)/shard_map/convert_element_type | solution.py:131
  199.0 0.8 collective-permute-start.9
  199.9 0.6 pad_maximum_fusion.2
  200.4 3.8 %collective-permute-done.9 = f32[2048]{0:T(1024)S(1)} collective-permute-done((f32[2048]{0:T(1024)S(1)}, f32[2048]{0:T(1024)S(1)}, u32[]{:S(2)}, u32[]{:S(2)}) %collective-permute-start.9) | collective-permute-done | bytes 8224 | tf_op jit(solution)/shard_map/ppermute | solution.py:26
  204.3 0.6 select_add_fusion
  (50 shorter events, 0.2 us)
Async XLA Ops:
  0.6 90.0 %copy-start = (bf16[1,2048,768]{2,1,0:T(8,128)(2,1)S(1)}, bf16[1,2048,768]{2,1,0:T(8,128)(2,1)}, u32[]{:S(2)}) copy-start(bf16[1,2048,768]{2,1,0:T(8,128)(2,1)} %param.13) | copy-start | bytes 9437188
  0.6 7.0 %copy-start.10 = (f32[128,2]{0,1:T(2,128)S(1)}, f32[128,2]{0,1:T(2,128)}, u32[]{:S(2)}) copy-start(f32[128,2]{0,1:T(2,128)} %param.10) | copy-start | bytes 3076
  5.8 1.9 copy-start.8
  84.0 4.5 %copy-start.3 = (bf16[512,4096]{1,0:T(8,128)(2,1)S(1)}, bf16[512,4096]{1,0:T(8,128)(2,1)}, u32[]{:S(2)}) copy-start(bf16[512,4096]{1,0:T(8,128)(2,1)} %reshape.99) | copy-start | bytes 12582916
  84.0 4.5 %copy-start.9 = (f32[2048]{0:T(1024)S(1)}, f32[2048]{0:T(1024)}, u32[]{:S(2)}) copy-start(f32[2048]{0:T(1024)} %param.11) | copy-start | bytes 24580
  84.0 4.7 %copy-start.12 = (bf16[1,2048,768]{2,1,0:T(8,128)(2,1)S(1)}, bf16[1,2048,768]{2,1,0:T(8,128)(2,1)}, u32[]{:S(2)}) copy-start(bf16[1,2048,768]{2,1,0:T(8,128)(2,1)} %param.12) | copy-start | bytes 9437188
  93.0 1.9 copy-start.15
  93.0 1.9 copy-start.17
  93.0 4.6 %copy-start.13 = (bf16[512,768]{1,0:T(8,128)(2,1)}, bf16[512,768]{1,0:T(8,128)(2,1)S(1)}, u32[]{:S(2)}) copy-start(bf16[512,768]{1,0:T(8,128)(2,1)S(1)} %get-tuple-element.23) | copy-start | bytes 2359300
  93.1 2.7 %copy-start.11 = (bf16[1,768,2048]{2,1,0:T(8,128)(2,1)S(1)}, bf16[1,768,2048]{2,1,0:T(8,128)(2,1)}, u32[]{:S(2)}) copy-start(bf16[1,768,2048]{2,1,0:T(8,128)(2,1)} %param.14) | copy-start | bytes 9437188
  109.2 7.3 %copy-start.5 = (bf16[128,2048]{1,0:T(8,128)(2,1)S(1)}, bf16[128,2048]{1,0:T(8,128)(2,1)}, u32[]{:S(2)}) copy-start(bf16[128,2048]{1,0:T(8,128)(2,1)} %param.8) | copy-start | bytes 1572868
  109.2 7.5 %copy-start.18 = (bf16[512,768]{1,0:T(8,128)(2,1)S(1)}, bf16[512,768]{1,0:T(8,128)(2,1)}, u32[]{:S(2)}) copy-start(bf16[512,768]{1,0:T(8,128)(2,1)} %copy-done.17) | copy-start | bytes 2359300
  109.2 58.4 %all-to-all-start.1 = ((bf16[128,4,4096]{2,1,0:T(4,128)(2,1)}), bf16[128,4,4096]{2,1,0:T(4,128)(2,1)}, u32[]{:S(2)}, u32[]{:S(2)}) async-start(bf16[128,4,4096]{2,1,0:T(4,128)(2,1)} %reshape.100), calls=%async_computation.1 | async-start | bytes 8388608 | tf_op jit(solution)/shard_map/all_to_all | solution.py:10
  116.8 5.3 %copy-start.4 = (bf16[512,4096]{1,0:T(8,128)(2,1)S(1)}, bf16[512,4096]{1,0:T(8,128)(2,1)}, u32[]{:S(2)}) copy-start(bf16[512,4096]{1,0:T(8,128)(2,1)} %reshape.99) | copy-start | bytes 12582916
  116.8 5.3 %copy-start.16 = (bf16[512,768]{1,0:T(8,128)(2,1)S(1)}, bf16[512,768]{1,0:T(8,128)(2,1)}, u32[]{:S(2)}) copy-start(bf16[512,768]{1,0:T(8,128)(2,1)} %copy-done.15) | copy-start | bytes 2359300
  122.1 3.7 %copy-start.14 = (bf16[512,768]{1,0:T(8,128)(2,1)S(1)}, bf16[512,768]{1,0:T(8,128)(2,1)}, u32[]{:S(2)}) copy-start(bf16[512,768]{1,0:T(8,128)(2,1)} %copy-done.13) | copy-start | bytes 2359300
  167.6 16.6 %collective-permute-start = (f32[2048]{0:T(1024)S(1)}, f32[2048]{0:T(1024)S(1)}, u32[]{:S(2)}, u32[]{:S(2)}) collective-permute-start(f32[2048]{0:T(1024)S(1)} %get-tuple-element.13), channel_id=1, source_target_pairs={{0,1},{1,0},{2,3},{3,2},{4,5},{5,4},{6,7},{7,6},{8,9},{9,8},{10,11... | collective-permute-start | bytes 24584 | tf_op jit(solution)/shard_map/ppermute | solution.py:26
  168.5 15.8 %collective-permute-start.1 = (f32[2048]{0:T(1024)S(1)}, f32[2048]{0:T(1024)S(1)}, u32[]{:S(2)}, u32[]{:S(2)}) collective-permute-start(f32[2048]{0:T(1024)S(1)} %get-tuple-element.13), channel_id=1, source_target_pairs={{0,2},{1,3},{2,0},{3,1},{4,6},{5,7},{6,4},{7,5},{8,10},{9,11},{10,... | collective-permute-start | bytes 24584 | tf_op jit(solution)/shard_map/ppermute | solution.py:26
  169.3 14.9 %collective-permute-start.2 = (f32[2048]{0:T(1024)S(1)}, f32[2048]{0:T(1024)S(1)}, u32[]{:S(2)}, u32[]{:S(2)}) collective-permute-start(f32[2048]{0:T(1024)S(1)} %get-tuple-element.13), channel_id=1, source_target_pairs={{0,3},{1,2},{2,1},{3,0},{4,7},{5,6},{6,5},{7,4},{8,11},{9,10},{10,... | collective-permute-start | bytes 24584 | tf_op jit(solution)/shard_map/ppermute | solution.py:26
  177.2 6.3 %copy-start.2 = (f32[128,4096]{1,0:T(8,128)}, f32[128,4096]{1,0:T(8,128)S(1)}, u32[]{:S(2)}) copy-start(f32[128,4096]{1,0:T(8,128)S(1)} %convert_element_type.92) | copy-start | bytes 6291460
  182.0 1.5 copy-start.7
  183.6 12.3 %copy-start.6 = (bf16[128,2048]{1,0:T(8,128)(2,1)S(1)}, bf16[128,2048]{1,0:T(8,128)(2,1)}, u32[]{:S(2)}) copy-start(bf16[128,2048]{1,0:T(8,128)(2,1)} %param.8) | copy-start | bytes 1572868
  184.3 5.2 %collective-permute-start.3 = (f32[2048]{0:T(1024)S(1)}, f32[2048]{0:T(1024)S(1)}, u32[]{:S(2)}, u32[]{:S(2)}) collective-permute-start(f32[2048]{0:T(1024)S(1)} %add_add_fusion.2), channel_id=1, source_target_pairs={{0,4},{1,5},{2,6},{3,7},{4,0},{5,1},{6,2},{7,3},{8,12},{9,13},{10,... | collective-permute-start | bytes 24584 | tf_op jit(solution)/shard_map/ppermute | solution.py:26
  186.4 3.1 %collective-permute-start.4 = (f32[2048]{0:T(1024)S(1)}, f32[2048]{0:T(1024)S(1)}, u32[]{:S(2)}, u32[]{:S(2)}) collective-permute-start(f32[2048]{0:T(1024)S(1)} %add_add_fusion.2), channel_id=1, source_target_pairs={{0,8},{1,9},{2,10},{3,11},{4,12},{5,13},{6,14},{7,15},{8,0},{9,1},... | collective-permute-start | bytes 24584 | tf_op jit(solution)/shard_map/ppermute | solution.py:26
  186.4 4.6 %collective-permute-start.5 = (f32[2048]{0:T(1024)S(1)}, f32[2048]{0:T(1024)S(1)}, u32[]{:S(2)}, u32[]{:S(2)}) collective-permute-start(f32[2048]{0:T(1024)S(1)} %add_add_fusion.2), channel_id=1, source_target_pairs={{0,12},{1,13},{2,14},{3,15},{4,8},{5,9},{6,10},{7,11},{8,4},{9,5},... | collective-permute-start | bytes 24584 | tf_op jit(solution)/shard_map/ppermute | solution.py:26
  191.0 8.0 %collective-permute-start.6 = (f32[2048]{0:T(1024)S(1)}, f32[2048]{0:T(1024)S(1)}, u32[]{:S(2)}, u32[]{:S(2)}) collective-permute-start(f32[2048]{0:T(1024)S(1)} %add_add_fusion.1), channel_id=1, source_target_pairs={{0,16},{1,17},{2,18},{3,19},{4,20},{5,21},{6,22},{7,23},{8,24},{9,... | collective-permute-start | bytes 24584 | tf_op jit(solution)/shard_map/ppermute | solution.py:26
  191.3 7.7 %collective-permute-start.7 = (f32[2048]{0:T(1024)S(1)}, f32[2048]{0:T(1024)S(1)}, u32[]{:S(2)}, u32[]{:S(2)}) collective-permute-start(f32[2048]{0:T(1024)S(1)} %add_add_fusion.1), channel_id=1, source_target_pairs={{0,32},{1,33},{2,34},{3,35},{4,36},{5,37},{6,38},{7,39},{8,40},{9,... | collective-permute-start | bytes 24584 | tf_op jit(solution)/shard_map/ppermute | solution.py:26
  193.1 6.0 %collective-permute-start.8 = (f32[2048]{0:T(1024)S(1)}, f32[2048]{0:T(1024)S(1)}, u32[]{:S(2)}, u32[]{:S(2)}) collective-permute-start(f32[2048]{0:T(1024)S(1)} %add_add_fusion.1), channel_id=1, source_target_pairs={{0,48},{1,49},{2,50},{3,51},{4,52},{5,53},{6,54},{7,55},{8,56},{9,... | collective-permute-start | bytes 24584 | tf_op jit(solution)/shard_map/ppermute | solution.py:26
  195.8 9.1 %copy-start.1 = (bf16[1,2048,768]{2,1,0:T(8,128)(2,1)S(1)}, bf16[1,2048,768]{2,1,0:T(8,128)(2,1)}, u32[]{:S(2)}) copy-start(bf16[1,2048,768]{2,1,0:T(8,128)(2,1)} %param.13) | copy-start | bytes 9437188
  199.0 5.2 %collective-permute-start.9 = (f32[2048]{0:T(1024)S(1)}, f32[2048]{0:T(1024)S(1)}, u32[]{:S(2)}, u32[]{:S(2)}) collective-permute-start(f32[2048]{0:T(1024)S(1)} %add_add_fusion), channel_id=1, source_target_pairs={{0,64},{1,65},{2,66},{3,67},{4,68},{5,69},{6,70},{7,71},{8,72},{9,... | collective-permute-start | bytes 24584 | tf_op jit(solution)/shard_map/ppermute | solution.py:26

commit v8 on v6

--- a/solution.py
+++ b/solution.py
@@ -21,7 +21,7 @@
     total = part
     step = 1
     while step < devices_all:
-        radix = 4 if step * 4 <= devices_all else 2
+        radix = 2
         held = [total] + [
             lax.ppermute(total, AXES, [(i, i ^ (x * step)) for i in range(devices_all)])
             for x in range(1, radix)

time: 203 us -> 201 us (level)
  starting transfers between devices: 21.1 us -> 14.3 us
  waiting for transfers between devices: 44.5 us -> 49.9 us
    ppermute x10 -> x7, starting transfers between devices: 13.9 us -> 7.16 us  [all_sum(): lax.ppermute(total, AXES, [(i, i ^ x * step) for i in range(devices_all)])]
    ppermute x10 -> x7, waiting for transfers between devices: 6.36 us -> 11.6 us  [all_sum(): lax.ppermute(total, AXES, [(i, i ^ x * step) for i in range(devices_all)])]
  transfers between devices with their start and end apart: 11 -> 8, of which waited for: 5 -> 6; matrix products, arithmetic and copies ran while one was open for 13% -> 13% of each run, Pallas kernels for 0% -> 0%
where the time goes in v8:
time: 201 us
  blocking collectives  63 us (31%)
  waiting for transfers between devices  49.9 us (25%)
  matrix products  33.5 us (17%)
  local copies, waits for them, and re-layouts  27 us (13%)
  starting transfers between devices  14.3 us (7%)
  other arithmetic  11.8 us (6%)
    all_to_all x1, blocking collectives, exchange(): return lax.all_to_all(rows, AXES, split_axis=0, concat_axis=0, tiled=True)  63 us
    all_to_all x1, waiting for transfers between devices, exchange(): return lax.all_to_all(rows, AXES, split_axis=0, concat_axis=0, tiled=True)  38.3 us
    dot_general x8, matrix products, contract(): lax.dot_general(left, right, (((left_dim,), (right_dim,)), ((), ())), pre...  24.8 us
    ppermute x7, waiting for transfers between devices, all_sum(): lax.ppermute(total, AXES, [(i, i ^ x * step) for i in range(devices_all)])  11.6 us
    reshape x1, local copies, waits for them, and re-layouts, on_device(): jnp.concatenate([expert_out, grad_back], axis=1)  7.17 us
    ppermute x7, starting transfers between devices, all_sum(): lax.ppermute(total, AXES, [(i, i ^ x * step) for i in range(devices_all)])  7.16 us
    all_to_all x1, starting transfers between devices, exchange(): return lax.all_to_all(rows, AXES, split_axis=0, concat_axis=0, tiled=True)  7.12 us
    reshape x1, local copies, waits for them, and re-layouts, on_device(): arrived_all = exchange(sent).reshape(slots, 2 * width)  6.88 us
  transfers between devices with their start and end apart: 8, of which 6 were waited for; matrix products, arithmetic and copies ran while one was open for 13% of the time, Pallas kernels for 0%

profile of v8, /device:TPU:0, one launch (start us, length us, event | category | flops | bytes accessed | tf_op | source)
XLA Modules:
  0.0 200.5 jit_solution(4619700804172658525)
XLA Ops:
  0.6 0.0 copy-start
  0.7 0.9 copy.37
  1.6 0.1 eq.65
  1.7 0.1 eq.61
  1.9 0.1 copy.39
  2.0 0.2 fusion.45
  2.3 0.2 fusion.47
  2.5 0.1 reduce_sum.78
  2.6 0.1 copy.41
  2.7 0.7 multiply_add_fusion.1
  3.4 2.1 %convert_element_type.72 = f32[128,2048]{1,0:T(8,128)} convert(bf16[128,2048]{1,0:T(8,128)(2,1)} %param.15) | non-fusion elementwise | flops 262144 | bytes 1572864 | tf_op jit(solution)/shard_map/convert_element_type | solution.py:83
  5.5 0.1 convert_reduce_fusion
  5.6 0.1 copy.42
  5.8 0.0 copy-start.8
  5.8 1.8 convolution_convert_fusion.3
  7.6 0.8 bitcast_convert_fusion
  8.4 0.3 pad_maximum_fusion
  8.7 3.2 %copy.44 = bf16[128,4,4096]{2,1,0:T(4,128)(2,1)S(1)} copy(bf16[128,4,4096]{2,0,1:T(8,128)(2,1)S(1)} %pad_maximum_fusion) | data formatting | bytes 8388608 | tf_op jit(solution)/shard_map/concatenate | solution.py:91
  12.0 63.0 %all_to_all.10 = bf16[128,4,4096]{2,1,0:T(4,128)(2,1)} all-to-all(bf16[128,4,4096]{2,1,0:T(4,128)(2,1)S(1)} %copy.44), channel_id=1, replica_groups=mesh['expert'=16,'dp'=8] {'expert','dp'}, dimensions={0} | all-to-all | bytes 8388608 | tf_op jit(solution)/shard_map/all_to_all | solution.py:10
  74.9 6.9 %reshape.108 = bf16[512,4096]{1,0:T(8,128)(2,1)} reshape(bf16[128,4,4096]{2,1,0:T(4,128)(2,1)} %all_to_all.10) | data formatting | bytes 8388608 | tf_op jit(solution)/shard_map/reshape | solution.py:92
  81.8 2.1 %fusion.4 = f32[512]{0:T(512)S(1)} fusion(bf16[512,4096]{1,0:T(8,128)(2,1)} %reshape.108), kind=kLoop, calls=%fused_computation.6 | loop fusion | flops 3145216 | bytes 2099200 | tf_op jit(solution)/shard_map/reduce_sum | solution.py:95
  83.9 0.0 copy-start.9
  83.9 0.0 copy-start.12
  83.9 4.5 %fusion.5 = f32[512,768]{1,0:T(8,128)S(1)} fusion(bf16[1,768,2048]{2,1,0:T(8,128)(2,1)} %param.14, bf16[512,4096]{1,0:T(8,128)(2,1)} %reshape.108), kind=kOutput, calls=%fused_computation.14 | convolution fusion | flops 1610612736 | bytes 6815744 | tf_op jit(solution)/shard_map/dot_general | solution.py:14
  88.5 0.2 copy-done.12
  88.7 1.9 fusion.15
  90.6 2.4 %multiply_convert_fusion.3 = (bf16[512,768]{1,0:T(8,128)(2,1)S(1)}, bf16[512,768]{1,0:T(8,128)(2,1)S(1)}, bf16[512,768]{1,0:T(8,128)(2,1)S(1)}) fusion(f32[512,768]{1,0:T(8,128)S(1)} %fusion.15, f32[512,768]{1,0:T(8,128)S(1)} %fusion.5, bf16[1,2048,768]{2,1,0:T(8,128)(2,1)S(1)} %copy-done, f32[2048]{0:T(1024)S(1)} %copy-done.9, f32[512]{0:T(512)S(1)} %add_rsqrt_fusion, ...), kind=kOutput, calls=%fused_computation.33 | convolution fusion | flops 1620705280 | bytes 10758144 | tf_op jit(solution)/shard_map/dot_general | solution.py:41
  93.0 0.0 copy-start.15
  93.0 0.0 copy-start.17
  93.0 0.0 copy-start.13
  93.0 0.0 copy-start.11
  93.0 1.8 fusion.9
  94.9 0.9 copy-done.11
  95.7 1.8 fusion.17
  97.6 2.0 fusion.3
  99.5 2.5 %pad_maximum_fusion.1 = bf16[512,4096]{1,0:T(8,128)(2,1)} fusion(bf16[512,2048]{1,0:T(8,128)(2,1)S(1)} %get-tuple-element.28, bf16[512,2048]{1,0:T(8,128)(2,1)S(1)} %fusion.17), kind=kLoop, calls=%fused_computation.8 | loop fusion | flops 8388608 | bytes 8388608 | tf_op jit(solution)/shard_map/concatenate | solution.py:104
  102.0 7.2 %reshape.109 = bf16[128,4,4096]{2,1,0:T(4,128)(2,1)} reshape(bf16[512,4096]{1,0:T(8,128)(2,1)} %pad_maximum_fusion.1) | data formatting | bytes 8388608 | tf_op jit(solution)/shard_map/reshape | solution.py:104
  109.2 7.1 %all-to-all-start.1 = ((bf16[128,4,4096]{2,1,0:T(4,128)(2,1)}), bf16[128,4,4096]{2,1,0:T(4,128)(2,1)}, u32[]{:S(2)}, u32[]{:S(2)}) async-start(bf16[128,4,4096]{2,1,0:T(4,128)(2,1)} %reshape.109), calls=%async_computation.1 | async-start | bytes 8388608 | tf_op jit(solution)/shard_map/all_to_all | solution.py:10
  116.3 0.2 fusion.33
  116.5 0.1 iota_compare_fusion
  116.7 5.2 %convolution_convert_fusion = bf16[768,2048]{1,0:T(8,128)(2,1)} fusion(bf16[512,768]{1,0:T(8,128)(2,1)S(1)} %copy-done.18, bf16[512,4096]{1,0:T(8,128)(2,1)} %reshape.108), kind=kOutput, calls=%fused_computation.11 | convolution fusion | flops 1612185600 | bytes 6029312 | tf_op jit(solution)/shard_map/dot_general | solution.py:14
  122.0 3.7 %convolution_convert_fusion.1 = bf16[2048,768]{1,0:T(8,128)(2,1)} fusion(bf16[512,768]{1,0:T(8,128)(2,1)S(1)} %copy-done.16, f32[2048]{0:T(1024)S(1)} %copy-done.9, f32[512]{0:T(512)S(1)} %add_rsqrt_fusion, bf16[512,4096]{1,0:T(8,128)(2,1)S(1)} %copy-done.4), kind=kOutput, calls=%fused_computation.12 | convolution fusion | flops 1616379904 | bytes 6039552 | tf_op jit(solution)/shard_map/dot_general | solution.py:14
  125.6 3.7 %convolution_convert_fusion.2 = bf16[2048,768]{1,0:T(8,128)(2,1)} fusion(bf16[512,768]{1,0:T(8,128)(2,1)S(1)} %copy-done.14, f32[2048]{0:T(1024)S(1)} %copy-done.9, f32[512]{0:T(512)S(1)} %add_rsqrt_fusion, bf16[512,4096]{1,0:T(8,128)(2,1)S(1)} %copy-done.4), kind=kOutput, calls=%fused_computation.13 | convolution fusion | flops 1616379904 | bytes 6039552 | tf_op jit(solution)/shard_map/dot_general | solution.py:14
  129.3 38.3 %all-to-all-done.1 = bf16[128,4,4096]{2,1,0:T(4,128)(2,1)} async-done(((bf16[128,4,4096]{2,1,0:T(4,128)(2,1)}), bf16[128,4,4096]{2,1,0:T(4,128)(2,1)}, u32[]{:S(2)}, u32[]{:S(2)}) %all-to-all-start.1) | async-done | bytes 4194336 | tf_op jit(solution)/shard_map/all_to_all | solution.py:10
  167.6 0.8 collective-permute-start
  168.4 6.9 %reshape.110 = bf16[512,4096]{1,0:T(8,128)(2,1)} reshape(bf16[128,4,4096]{2,1,0:T(4,128)(2,1)} %all-to-all-done.1) | data formatting | bytes 8388608 | tf_op jit(solution)/shard_map/reshape | solution.py:111
  175.3 1.0 collective-permute-start.1
  176.3 3.2 %fusion.44 = f32[128,4096]{1,0:T(8,128)S(1)} fusion(bf16[512,4096]{1,0:T(8,128)(2,1)} %reshape.110, pred[128,2,512]{2,0,1:T(32,128)(4,1)S(1)} %iota_compare_fusion), kind=kOutput, calls=%fused_computation.64 | convolution fusion | flops 536870912 | bytes 6356992 | tf_op jit(solution)/shard_map/dot_general | solution.py:14
  179.5 0.0 copy-start.7
  179.5 1.8 collective-permute-start.2
  181.3 0.7 fusion.43
  182.0 0.0 copy-start.6
  182.1 2.7 %collective-permute-done.2 = f32[2048]{0:T(1024)S(1)} collective-permute-done((f32[2048]{0:T(1024)S(1)}, f32[2048]{0:T(1024)S(1)}, u32[]{:S(2)}, u32[]{:S(2)}) %collective-permute-start.2) | collective-permute-done | bytes 8224 | tf_op jit(solution)/shard_map/ppermute | solution.py:26
  184.8 0.6 fusion.27
  185.4 0.6 collective-permute-done.3
  185.9 0.4 collective-permute-start.4
  186.3 3.3 %collective-permute-done.4 = f32[2048]{0:T(1024)S(1)} collective-permute-done((f32[2048]{0:T(1024)S(1)}, f32[2048]{0:T(1024)S(1)}, u32[]{:S(2)}, u32[]{:S(2)}) %collective-permute-start.4) | collective-permute-done | bytes 8224 | tf_op jit(solution)/shard_map/ppermute | solution.py:26
  189.6 1.7 collective-permute-start.5
  191.2 1.4 fusion.31
  192.7 2.0 %collective-permute-done.5 = f32[2048]{0:T(1024)S(1)} collective-permute-done((f32[2048]{0:T(1024)S(1)}, f32[2048]{0:T(1024)S(1)}, u32[]{:S(2)}, u32[]{:S(2)}) %collective-permute-start.5) | collective-permute-done | bytes 8224 | tf_op jit(solution)/shard_map/ppermute | solution.py:26
  194.7 1.5 collective-permute-start.6
  196.3 0.6 pad_maximum_fusion.2
  196.8 3.1 %collective-permute-done.6 = f32[2048]{0:T(1024)S(1)} collective-permute-done((f32[2048]{0:T(1024)S(1)}, f32[2048]{0:T(1024)S(1)}, u32[]{:S(2)}, u32[]{:S(2)}) %collective-permute-start.6) | collective-permute-done | bytes 8224 | tf_op jit(solution)/shard_map/ppermute | solution.py:26
  199.9 0.6 select_add_fusion
  (46 shorter events, 0.2 us)
Async XLA Ops:
  0.6 89.9 %copy-start = (bf16[1,2048,768]{2,1,0:T(8,128)(2,1)S(1)}, bf16[1,2048,768]{2,1,0:T(8,128)(2,1)}, u32[]{:S(2)}) copy-start(bf16[1,2048,768]{2,1,0:T(8,128)(2,1)} %param.13) | copy-start | bytes 9437188
  0.6 7.0 %copy-start.10 = (f32[128,2]{0,1:T(2,128)S(1)}, f32[128,2]{0,1:T(2,128)}, u32[]{:S(2)}) copy-start(f32[128,2]{0,1:T(2,128)} %param.10) | copy-start | bytes 3076
  5.8 1.9 copy-start.8
  83.9 4.5 %copy-start.3 = (bf16[512,4096]{1,0:T(8,128)(2,1)S(1)}, bf16[512,4096]{1,0:T(8,128)(2,1)}, u32[]{:S(2)}) copy-start(bf16[512,4096]{1,0:T(8,128)(2,1)} %reshape.108) | copy-start | bytes 12582916
  83.9 4.5 %copy-start.9 = (f32[2048]{0:T(1024)S(1)}, f32[2048]{0:T(1024)}, u32[]{:S(2)}) copy-start(f32[2048]{0:T(1024)} %param.11) | copy-start | bytes 24580
  83.9 4.7 %copy-start.12 = (bf16[1,2048,768]{2,1,0:T(8,128)(2,1)S(1)}, bf16[1,2048,768]{2,1,0:T(8,128)(2,1)}, u32[]{:S(2)}) copy-start(bf16[1,2048,768]{2,1,0:T(8,128)(2,1)} %param.12) | copy-start | bytes 9437188
  93.0 1.9 copy-start.15
  93.0 1.9 copy-start.17
  93.0 4.6 %copy-start.13 = (bf16[512,768]{1,0:T(8,128)(2,1)}, bf16[512,768]{1,0:T(8,128)(2,1)S(1)}, u32[]{:S(2)}) copy-start(bf16[512,768]{1,0:T(8,128)(2,1)S(1)} %get-tuple-element.23) | copy-start | bytes 2359300
  93.0 2.7 %copy-start.11 = (bf16[1,768,2048]{2,1,0:T(8,128)(2,1)S(1)}, bf16[1,768,2048]{2,1,0:T(8,128)(2,1)}, u32[]{:S(2)}) copy-start(bf16[1,768,2048]{2,1,0:T(8,128)(2,1)} %param.14) | copy-start | bytes 9437188
  109.2 7.1 %copy-start.5 = (bf16[128,2048]{1,0:T(8,128)(2,1)S(1)}, bf16[128,2048]{1,0:T(8,128)(2,1)}, u32[]{:S(2)}) copy-start(bf16[128,2048]{1,0:T(8,128)(2,1)} %param.8) | copy-start | bytes 1572868
  109.2 7.5 %copy-start.18 = (bf16[512,768]{1,0:T(8,128)(2,1)S(1)}, bf16[512,768]{1,0:T(8,128)(2,1)}, u32[]{:S(2)}) copy-start(bf16[512,768]{1,0:T(8,128)(2,1)} %copy-done.17) | copy-start | bytes 2359300
  109.2 58.4 %all-to-all-start.1 = ((bf16[128,4,4096]{2,1,0:T(4,128)(2,1)}), bf16[128,4,4096]{2,1,0:T(4,128)(2,1)}, u32[]{:S(2)}, u32[]{:S(2)}) async-start(bf16[128,4,4096]{2,1,0:T(4,128)(2,1)} %reshape.109), calls=%async_computation.1 | async-start | bytes 8388608 | tf_op jit(solution)/shard_map/all_to_all | solution.py:10
  116.7 5.3 %copy-start.4 = (bf16[512,4096]{1,0:T(8,128)(2,1)S(1)}, bf16[512,4096]{1,0:T(8,128)(2,1)}, u32[]{:S(2)}) copy-start(bf16[512,4096]{1,0:T(8,128)(2,1)} %reshape.108) | copy-start | bytes 12582916
  116.7 5.3 %copy-start.16 = (bf16[512,768]{1,0:T(8,128)(2,1)S(1)}, bf16[512,768]{1,0:T(8,128)(2,1)}, u32[]{:S(2)}) copy-start(bf16[512,768]{1,0:T(8,128)(2,1)} %copy-done.15) | copy-start | bytes 2359300
  122.0 3.7 %copy-start.14 = (bf16[512,768]{1,0:T(8,128)(2,1)S(1)}, bf16[512,768]{1,0:T(8,128)(2,1)}, u32[]{:S(2)}) copy-start(bf16[512,768]{1,0:T(8,128)(2,1)} %copy-done.13) | copy-start | bytes 2359300
  167.6 7.7 %collective-permute-start = (f32[2048]{0:T(1024)S(1)}, f32[2048]{0:T(1024)S(1)}, u32[]{:S(2)}, u32[]{:S(2)}) collective-permute-start(f32[2048]{0:T(1024)S(1)} %get-tuple-element.13), channel_id=1, source_target_pairs={{0,1},{1,0},{2,3},{3,2},{4,5},{5,4},{6,7},{7,6},{8,9},{9,8},{10,11... | collective-permute-start | bytes 24584 | tf_op jit(solution)/shard_map/ppermute | solution.py:26
  175.3 6.0 %copy-start.2 = (bf16[512,4096]{1,0:T(8,128)(2,1)S(1)}, bf16[512,4096]{1,0:T(8,128)(2,1)}, u32[]{:S(2)}) copy-start(bf16[512,4096]{1,0:T(8,128)(2,1)} %reshape.110) | copy-start | bytes 12582916
  175.3 4.2 %collective-permute-start.1 = (f32[2048]{0:T(1024)S(1)}, f32[2048]{0:T(1024)S(1)}, u32[]{:S(2)}, u32[]{:S(2)}) collective-permute-start(f32[2048]{0:T(1024)S(1)} %select_add_fusion.6), channel_id=1, source_target_pairs={{0,2},{1,3},{2,0},{3,1},{4,6},{5,7},{6,4},{7,5},{8,10},{9,11},{10,... | collective-permute-start | bytes 24584 | tf_op jit(solution)/shard_map/ppermute | solution.py:26
  179.5 5.3 %copy-start.7 = (bf16[128,2048]{1,0:T(8,128)(2,1)S(1)}, bf16[128,2048]{1,0:T(8,128)(2,1)}, u32[]{:S(2)}) copy-start(bf16[128,2048]{1,0:T(8,128)(2,1)} %param.15) | copy-start | bytes 1572868
  179.5 5.2 %collective-permute-start.2 = (f32[2048]{0:T(1024)S(1)}, f32[2048]{0:T(1024)S(1)}, u32[]{:S(2)}, u32[]{:S(2)}) collective-permute-start(f32[2048]{0:T(1024)S(1)} %select_add_fusion.5), channel_id=1, source_target_pairs={{0,4},{1,5},{2,6},{3,7},{4,0},{5,1},{6,2},{7,3},{8,12},{9,13},{10,... | collective-permute-start | bytes 24584 | tf_op jit(solution)/shard_map/ppermute | solution.py:26
  182.0 9.2 %copy-start.6 = (bf16[128,2048]{1,0:T(8,128)(2,1)S(1)}, bf16[128,2048]{1,0:T(8,128)(2,1)}, u32[]{:S(2)}) copy-start(bf16[128,2048]{1,0:T(8,128)(2,1)} %param.8) | copy-start | bytes 1572868
  184.7 1.2 collective-permute-start.3
  185.9 3.7 %collective-permute-start.4 = (f32[2048]{0:T(1024)S(1)}, f32[2048]{0:T(1024)S(1)}, u32[]{:S(2)}, u32[]{:S(2)}) collective-permute-start(f32[2048]{0:T(1024)S(1)} %select_add_fusion.3), channel_id=1, source_target_pairs={{0,16},{1,17},{2,18},{3,19},{4,20},{5,21},{6,22},{7,23},{8,24},{9,... | collective-permute-start | bytes 24584 | tf_op jit(solution)/shard_map/ppermute | solution.py:26
  189.6 5.2 %collective-permute-start.5 = (f32[2048]{0:T(1024)S(1)}, f32[2048]{0:T(1024)S(1)}, u32[]{:S(2)}, u32[]{:S(2)}) collective-permute-start(f32[2048]{0:T(1024)S(1)} %select_add_fusion.2), channel_id=1, source_target_pairs={{0,32},{1,33},{2,34},{3,35},{4,36},{5,37},{6,38},{7,39},{8,40},{9,... | collective-permute-start | bytes 24584 | tf_op jit(solution)/shard_map/ppermute | solution.py:26
  191.2 9.3 %copy-start.1 = (bf16[1,2048,768]{2,1,0:T(8,128)(2,1)S(1)}, bf16[1,2048,768]{2,1,0:T(8,128)(2,1)}, u32[]{:S(2)}) copy-start(bf16[1,2048,768]{2,1,0:T(8,128)(2,1)} %param.13) | copy-start | bytes 9437188
  194.7 5.2 %collective-permute-start.6 = (f32[2048]{0:T(1024)S(1)}, f32[2048]{0:T(1024)S(1)}, u32[]{:S(2)}, u32[]{:S(2)}) collective-permute-start(f32[2048]{0:T(1024)S(1)} %select_add_fusion.1), channel_id=1, source_target_pairs={{0,64},{1,65},{2,66},{3,67},{4,68},{5,69},{6,70},{7,71},{8,72},{9,... | collective-permute-start | bytes 24584 | tf_op jit(solution)/shard_map/ppermute | solution.py:26

commit v9 on v8

--- a/solution.py
+++ b/solution.py
@@ -16,23 +16,11 @@
     )
 
 
-def all_sum(part, devices_all):
-    me = lax.axis_index(AXES)
+def all_sum(part, devices_all, steps):
     total = part
-    step = 1
-    while step < devices_all:
-        radix = 2
-        held = [total] + [
-            lax.ppermute(total, AXES, [(i, i ^ (x * step)) for i in range(devices_all)])
-            for x in range(1, radix)
-        ]
-        position = (me // step) % radix
-        canon = [lax.select_n(position ^ q, *held) for q in range(radix)]
-        if radix == 4:
-            total = (canon[0] + canon[1]) + (canon[2] + canon[3])
-        else:
-            total = canon[0] + canon[1]
-        step *= radix
+    for step in steps:
+        pairs = [(i, i ^ step) for i in range(devices_all)]
+        total = total + lax.ppermute(total, AXES, pairs)
     return total
 
 
@@ -104,10 +92,13 @@
     back = jnp.concatenate([expert_out, grad_back], axis=1).reshape(
         devices_all, capacity, 2 * width
     )
+    bits = [1 << b for b in range(devices_all.bit_length() - 1)]
+    gain_part = all_sum(gain_part, devices_all, bits[:3])
+    back, gain_part = lax.optimization_barrier((back, gain_part))
     returned, grad_gate, grad_up, grad_down, gain_part = lax.optimization_barrier(
         (exchange(back), grad_gate, grad_up, grad_down, gain_part)
     )
-    grad_gain = all_sum(gain_part, devices_all)
+    grad_gain = all_sum(gain_part, devices_all, bits[3:])
     returned = returned.reshape(slots, 2 * width)
     picked = [
         contract(select_tk[:, k, :], returned, 1, 0) for k in range(top_count)

time: 201 us -> 201 us (level)
  transfers between devices with their start and end apart: 8 -> 8, of which waited for: 6 -> 7; matrix products, arithmetic and copies ran while one was open for 13% -> 13% of each run, Pallas kernels for 0% -> 0%
where the time goes in v9:
time: 201 us; the launch traced here: 200 us
  blocking collectives  63 us (31%)
  waiting for transfers between devices  50.9 us (25%)
  matrix products  33.4 us (17%)
  local copies, waits for them, and re-layouts  26.7 us (13%)
  starting transfers between devices  13.5 us (7%)
  other arithmetic  11.8 us (6%)
    all_to_all x1, blocking collectives, exchange(): return lax.all_to_all(rows, AXES, split_axis=0, concat_axis=0, tiled=True)  63 us
    all_to_all x1, waiting for transfers between devices, exchange(): return lax.all_to_all(rows, AXES, split_axis=0, concat_axis=0, tiled=True)  38.2 us
    dot_general x8, matrix products, contract(): lax.dot_general(left, right, (((left_dim,), (right_dim,)), ((), ())), pre...  24.8 us
    ppermute x7, waiting for transfers between devices, all_sum(): total = total + lax.ppermute(total, AXES, pairs)  12.7 us
    ppermute x7, starting transfers between devices, all_sum(): total = total + lax.ppermute(total, AXES, pairs)  7.28 us
    reshape x1, local copies, waits for them, and re-layouts, on_device(): jnp.concatenate([expert_out, grad_back], axis=1)  7.17 us
    reshape x1, local copies, waits for them, and re-layouts, on_device(): arrived_all = exchange(sent).reshape(slots, 2 * width)  6.88 us
    reshape x1, local copies, waits for them, and re-layouts, on_device(): returned = returned.reshape(slots, 2 * width)  6.88 us
  transfers between devices with their start and end apart: 8, of which 7 were waited for; matrix products, arithmetic and copies ran while one was open for 13% of the time, Pallas kernels for 0%

profile of v9, /device:TPU:0, one launch (start us, length us, event | category | flops | bytes accessed | tf_op | source)
XLA Modules:
  0.0 200.3 jit_solution(6249217702425828514)
XLA Ops:
  0.6 0.0 copy-start
  0.7 0.9 copy.37
  1.6 0.1 eq.57
  1.7 0.1 eq.53
  1.9 2.1 %convert_element_type.72 = f32[128,2048]{1,0:T(8,128)} convert(bf16[128,2048]{1,0:T(8,128)(2,1)} %param.15) | non-fusion elementwise | flops 262144 | bytes 1572864 | tf_op jit(solution)/shard_map/convert_element_type | solution.py:71
  4.0 0.1 copy.39
  4.1 0.2 fusion.45
  4.4 0.2 fusion.47
  4.6 0.1 reduce_sum.78
  4.8 0.1 copy.41
  4.8 0.7 multiply_add_fusion.1
  5.5 0.1 convert_reduce_fusion
  5.7 0.1 copy.42
  5.8 0.0 copy-start.8
  5.8 1.8 convolution_convert_fusion.3
  7.6 0.8 bitcast_convert_fusion
  8.4 0.3 pad_maximum_fusion
  8.7 3.2 %copy.44 = bf16[128,4,4096]{2,1,0:T(4,128)(2,1)S(1)} copy(bf16[128,4,4096]{2,0,1:T(8,128)(2,1)S(1)} %pad_maximum_fusion) | data formatting | bytes 8388608 | tf_op jit(solution)/shard_map/concatenate | solution.py:79
  12.0 63.0 %all_to_all.10 = bf16[128,4,4096]{2,1,0:T(4,128)(2,1)} all-to-all(bf16[128,4,4096]{2,1,0:T(4,128)(2,1)S(1)} %copy.44), channel_id=1, replica_groups=mesh['expert'=16,'dp'=8] {'expert','dp'}, dimensions={0} | all-to-all | bytes 8388608 | tf_op jit(solution)/shard_map/all_to_all | solution.py:10
  75.0 6.9 %reshape.108 = bf16[512,4096]{1,0:T(8,128)(2,1)} reshape(bf16[128,4,4096]{2,1,0:T(4,128)(2,1)} %all_to_all.10) | data formatting | bytes 8388608 | tf_op jit(solution)/shard_map/reshape | solution.py:80
  81.8 2.1 %fusion.4 = f32[512]{0:T(512)S(1)} fusion(bf16[512,4096]{1,0:T(8,128)(2,1)} %reshape.108), kind=kLoop, calls=%fused_computation.6 | loop fusion | flops 3145216 | bytes 2099200 | tf_op jit(solution)/shard_map/reduce_sum | solution.py:83
  83.9 0.0 copy-start.9
  84.0 4.5 %fusion.5 = f32[512,768]{1,0:T(8,128)S(1)} fusion(bf16[1,768,2048]{2,1,0:T(8,128)(2,1)} %param.14, bf16[512,4096]{1,0:T(8,128)(2,1)} %reshape.108), kind=kOutput, calls=%fused_computation.14 | convolution fusion | flops 1610612736 | bytes 6815744 | tf_op jit(solution)/shard_map/dot_general | solution.py:14
  88.5 0.2 copy-done.11
  88.7 1.9 fusion.15
  90.6 2.4 %multiply_convert_fusion.3 = (bf16[512,768]{1,0:T(8,128)(2,1)S(1)}, bf16[512,768]{1,0:T(8,128)(2,1)S(1)}, bf16[512,768]{1,0:T(8,128)(2,1)S(1)}) fusion(f32[512,768]{1,0:T(8,128)S(1)} %fusion.15, f32[512,768]{1,0:T(8,128)S(1)} %fusion.5, bf16[1,2048,768]{2,1,0:T(8,128)(2,1)S(1)} %copy-done, f32[2048]{0:T(1024)S(1)} %copy-done.9, f32[512]{0:T(512)S(1)} %add_rsqrt_fusion, ...), kind=kOutput, calls=%fused_computation.33 | convolution fusion | flops 1620705280 | bytes 10758144 | tf_op jit(solution)/shard_map/dot_general | solution.py:29
  92.9 0.0 copy-start.17
  93.0 1.8 fusion.9
  94.8 0.0 copy-start.12
  94.8 2.0 %fusion.3 = (f32[2048]{0:T(1024)S(1)}, bf16[512,2048]{1,0:T(8,128)(2,1)S(1)}) fusion(f32[512]{0:T(512)S(1)} %add_rsqrt_fusion, bf16[512,4096]{1,0:T(8,128)(2,1)S(1)} %copy-done.3, f32[512,2048]{1,0:T(8,128)S(1)} %fusion.9, bf16[512,768]{1,0:T(8,128)(2,1)S(1)} %get-tuple-element.27, bf16[1,2048,768]{2,1,0:T(8,128)(2,1)S(1)} %copy-done.11), kind=kOutput, calls=%fused_computation.5 | convolution fusion | flops 1617950720 | bytes 12331008 | tf_op jit(solution)/shard_map/dot_general | solution.py:14
  96.8 0.9 collective-permute-start
  97.8 2.8 %collective-permute-done = f32[2048]{0:T(1024)S(1)} collective-permute-done((f32[2048]{0:T(1024)S(1)}, f32[2048]{0:T(1024)S(1)}, u32[]{:S(2)}, u32[]{:S(2)}) %collective-permute-start) | collective-permute-done | bytes 8224 | tf_op jit(solution)/shard_map/ppermute | solution.py:23
  100.6 0.7 collective-permute-start.1
  101.3 1.8 fusion.17
  103.1 1.1 collective-permute-done.1
  104.2 2.1 %collective-permute-start.2 = (f32[2048]{0:T(1024)S(1)}, f32[2048]{0:T(1024)S(1)}, u32[]{:S(2)}, u32[]{:S(2)}) collective-permute-start(f32[2048]{0:T(1024)S(1)} %add.82), channel_id=1, source_target_pairs={{0,4},{1,5},{2,6},{3,7},{4,0},{5,1},{6,2},{7,3},{8,12},{9,13},{10,... | collective-permute-start | bytes 24584 | tf_op jit(solution)/shard_map/ppermute | solution.py:23
  106.3 2.5 %pad_maximum_fusion.1 = bf16[512,4096]{1,0:T(8,128)(2,1)} fusion(bf16[512,2048]{1,0:T(8,128)(2,1)S(1)} %get-tuple-element.32, bf16[512,2048]{1,0:T(8,128)(2,1)S(1)} %fusion.17), kind=kLoop, calls=%fused_computation.8 | loop fusion | flops 8388608 | bytes 8388608 | tf_op jit(solution)/shard_map/concatenate | solution.py:92
  108.8 7.2 %reshape.109 = bf16[128,4,4096]{2,1,0:T(4,128)(2,1)} reshape(bf16[512,4096]{1,0:T(8,128)(2,1)} %pad_maximum_fusion.1) | data formatting | bytes 8388608 | tf_op jit(solution)/shard_map/reshape | solution.py:92
  115.9 0.0 copy-start.18
  116.0 6.2 %all-to-all-start.1 = ((bf16[128,4,4096]{2,1,0:T(4,128)(2,1)}), bf16[128,4,4096]{2,1,0:T(4,128)(2,1)}, u32[]{:S(2)}, u32[]{:S(2)}) async-start(bf16[128,4,4096]{2,1,0:T(4,128)(2,1)} %reshape.109), calls=%async_computation.1 | async-start | bytes 8388608 | tf_op jit(solution)/shard_map/all_to_all | solution.py:10
  122.2 0.2 fusion.33
  122.4 0.1 iota_compare_fusion
  122.5 5.3 %convolution_convert_fusion = bf16[768,2048]{1,0:T(8,128)(2,1)} fusion(bf16[512,768]{1,0:T(8,128)(2,1)S(1)} %copy-done.18, bf16[512,4096]{1,0:T(8,128)(2,1)} %reshape.108), kind=kOutput, calls=%fused_computation.11 | convolution fusion | flops 1612185600 | bytes 6029312 | tf_op jit(solution)/shard_map/dot_general | solution.py:14
  127.8 3.7 %convolution_convert_fusion.2 = bf16[2048,768]{1,0:T(8,128)(2,1)} fusion(bf16[512,768]{1,0:T(8,128)(2,1)S(1)} %copy-done.14, f32[2048]{0:T(1024)S(1)} %copy-done.9, f32[512]{0:T(512)S(1)} %add_rsqrt_fusion, bf16[512,4096]{1,0:T(8,128)(2,1)S(1)} %copy-done.4), kind=kOutput, calls=%fused_computation.13 | convolution fusion | flops 1616379904 | bytes 6039552 | tf_op jit(solution)/shard_map/dot_general | solution.py:14
  131.5 3.7 %convolution_convert_fusion.1 = bf16[2048,768]{1,0:T(8,128)(2,1)} fusion(bf16[512,768]{1,0:T(8,128)(2,1)S(1)} %copy-done.16, f32[2048]{0:T(1024)S(1)} %copy-done.9, f32[512]{0:T(512)S(1)} %add_rsqrt_fusion, bf16[512,4096]{1,0:T(8,128)(2,1)S(1)} %copy-done.4), kind=kOutput, calls=%fused_computation.12 | convolution fusion | flops 1616379904 | bytes 6039552 | tf_op jit(solution)/shard_map/dot_general | solution.py:14
  135.2 38.2 %all-to-all-done.1 = bf16[128,4,4096]{2,1,0:T(4,128)(2,1)} async-done(((bf16[128,4,4096]{2,1,0:T(4,128)(2,1)}), bf16[128,4,4096]{2,1,0:T(4,128)(2,1)}, u32[]{:S(2)}, u32[]{:S(2)}) %all-to-all-start.1) | async-done | bytes 4194336 | tf_op jit(solution)/shard_map/all_to_all | solution.py:10
  173.4 6.9 %reshape.110 = bf16[512,4096]{1,0:T(8,128)(2,1)} reshape(bf16[128,4,4096]{2,1,0:T(4,128)(2,1)} %all-to-all-done.1) | data formatting | bytes 8388608 | tf_op jit(solution)/shard_map/reshape | solution.py:102
  180.3 3.1 %fusion.43 = f32[128,4096]{1,0:T(8,128)S(1)} fusion(bf16[512,4096]{1,0:T(8,128)(2,1)} %reshape.110, pred[128,2,512]{2,0,1:T(32,128)(4,1)S(1)} %iota_compare_fusion), kind=kOutput, calls=%fused_computation.62 | convolution fusion | flops 536870912 | bytes 6356992 | tf_op jit(solution)/shard_map/dot_general | solution.py:14
  183.4 0.4 copy-done.2
  183.7 0.7 fusion.44
  184.5 0.0 copy-start.6
  184.5 0.1 collective-permute-start.3
  184.6 0.2 copy-done.7
  184.8 0.6 fusion.27
  185.4 0.4 collective-permute-done.3
  185.8 1.2 collective-permute-start.4
  187.0 2.4 %collective-permute-done.4 = f32[2048]{0:T(1024)S(1)} collective-permute-done((f32[2048]{0:T(1024)S(1)}, f32[2048]{0:T(1024)S(1)}, u32[]{:S(2)}, u32[]{:S(2)}) %collective-permute-start.4) | collective-permute-done | bytes 8224 | tf_op jit(solution)/shard_map/ppermute | solution.py:23
  189.4 2.2 %collective-permute-start.5 = (f32[2048]{0:T(1024)S(1)}, f32[2048]{0:T(1024)S(1)}, u32[]{:S(2)}, u32[]{:S(2)}) collective-permute-start(f32[2048]{0:T(1024)S(1)} %add.87), channel_id=1, source_target_pairs={{0,32},{1,33},{2,34},{3,35},{4,36},{5,37},{6,38},{7,39},{8,40},{9,... | collective-permute-start | bytes 24584 | tf_op jit(solution)/shard_map/ppermute | solution.py:23
  191.7 1.4 fusion.31
  193.1 1.5 collective-permute-done.5
  194.6 0.0 collective-permute-start.6
  194.6 0.6 pad_maximum_fusion.2
  195.2 4.6 %collective-permute-done.6 = f32[2048]{0:T(1024)S(1)} collective-permute-done((f32[2048]{0:T(1024)S(1)}, f32[2048]{0:T(1024)S(1)}, u32[]{:S(2)}, u32[]{:S(2)}) %collective-permute-start.6) | collective-permute-done | bytes 8224 | tf_op jit(solution)/shard_map/ppermute | solution.py:23
  199.7 0.6 add.89
  (46 shorter events, 0.2 us)
Async XLA Ops:
  0.6 89.9 %copy-start = (bf16[1,2048,768]{2,1,0:T(8,128)(2,1)S(1)}, bf16[1,2048,768]{2,1,0:T(8,128)(2,1)}, u32[]{:S(2)}) copy-start(bf16[1,2048,768]{2,1,0:T(8,128)(2,1)} %param.13) | copy-start | bytes 9437188
  0.6 7.0 %copy-start.10 = (f32[128,2]{0,1:T(2,128)S(1)}, f32[128,2]{0,1:T(2,128)}, u32[]{:S(2)}) copy-start(f32[128,2]{0,1:T(2,128)} %param.10) | copy-start | bytes 3076
  5.8 1.9 copy-start.8
  83.9 4.5 %copy-start.3 = (bf16[512,4096]{1,0:T(8,128)(2,1)S(1)}, bf16[512,4096]{1,0:T(8,128)(2,1)}, u32[]{:S(2)}) copy-start(bf16[512,4096]{1,0:T(8,128)(2,1)} %reshape.108) | copy-start | bytes 12582916
  83.9 4.5 %copy-start.9 = (f32[2048]{0:T(1024)S(1)}, f32[2048]{0:T(1024)}, u32[]{:S(2)}) copy-start(f32[2048]{0:T(1024)} %param.11) | copy-start | bytes 24580
  83.9 4.7 %copy-start.11 = (bf16[1,2048,768]{2,1,0:T(8,128)(2,1)S(1)}, bf16[1,2048,768]{2,1,0:T(8,128)(2,1)}, u32[]{:S(2)}) copy-start(bf16[1,2048,768]{2,1,0:T(8,128)(2,1)} %param.12) | copy-start | bytes 9437188
  92.9 1.9 copy-start.15
  92.9 1.9 copy-start.13
  92.9 8.4 %copy-start.17 = (bf16[512,768]{1,0:T(8,128)(2,1)}, bf16[512,768]{1,0:T(8,128)(2,1)S(1)}, u32[]{:S(2)}) copy-start(bf16[512,768]{1,0:T(8,128)(2,1)S(1)} %get-tuple-element.26) | copy-start | bytes 2359300
  94.8 6.5 %copy-start.12 = (bf16[1,768,2048]{2,1,0:T(8,128)(2,1)S(1)}, bf16[1,768,2048]{2,1,0:T(8,128)(2,1)}, u32[]{:S(2)}) copy-start(bf16[1,768,2048]{2,1,0:T(8,128)(2,1)} %param.14) | copy-start | bytes 9437188
  96.8 3.7 %collective-permute-start = (f32[2048]{0:T(1024)S(1)}, f32[2048]{0:T(1024)S(1)}, u32[]{:S(2)}, u32[]{:S(2)}) collective-permute-start(f32[2048]{0:T(1024)S(1)} %get-tuple-element.31), channel_id=1, source_target_pairs={{0,1},{1,0},{2,3},{3,2},{4,5},{5,4},{6,7},{7,6},{8,9},{9,8},{10,11... | collective-permute-start | bytes 24584 | tf_op jit(solution)/shard_map/ppermute | solution.py:23
  100.6 3.7 %collective-permute-start.1 = (f32[2048]{0:T(1024)S(1)}, f32[2048]{0:T(1024)S(1)}, u32[]{:S(2)}, u32[]{:S(2)}) collective-permute-start(f32[2048]{0:T(1024)S(1)} %add.81), channel_id=1, source_target_pairs={{0,2},{1,3},{2,0},{3,1},{4,6},{5,7},{6,4},{7,5},{8,10},{9,11},{10,... | collective-permute-start | bytes 24584 | tf_op jit(solution)/shard_map/ppermute | solution.py:23
  104.2 11.7 %collective-permute-start.2 = (f32[2048]{0:T(1024)S(1)}, f32[2048]{0:T(1024)S(1)}, u32[]{:S(2)}, u32[]{:S(2)}) collective-permute-start(f32[2048]{0:T(1024)S(1)} %add.82), channel_id=1, source_target_pairs={{0,4},{1,5},{2,6},{3,7},{4,0},{5,1},{6,2},{7,3},{8,12},{9,13},{10,... | collective-permute-start | bytes 24584 | tf_op jit(solution)/shard_map/ppermute | solution.py:23
  115.9 6.2 %copy-start.5 = (bf16[128,2048]{1,0:T(8,128)(2,1)S(1)}, bf16[128,2048]{1,0:T(8,128)(2,1)}, u32[]{:S(2)}) copy-start(bf16[128,2048]{1,0:T(8,128)(2,1)} %param.8) | copy-start | bytes 1572868
  115.9 6.6 %copy-start.18 = (bf16[512,768]{1,0:T(8,128)(2,1)S(1)}, bf16[512,768]{1,0:T(8,128)(2,1)}, u32[]{:S(2)}) copy-start(bf16[512,768]{1,0:T(8,128)(2,1)} %copy-done.17) | copy-start | bytes 2359300
  116.0 57.5 %all-to-all-start.1 = ((bf16[128,4,4096]{2,1,0:T(4,128)(2,1)}), bf16[128,4,4096]{2,1,0:T(4,128)(2,1)}, u32[]{:S(2)}, u32[]{:S(2)}) async-start(bf16[128,4,4096]{2,1,0:T(4,128)(2,1)} %reshape.109), calls=%async_computation.1 | async-start | bytes 8388608 | tf_op jit(solution)/shard_map/all_to_all | solution.py:10
  122.5 5.3 %copy-start.4 = (bf16[512,4096]{1,0:T(8,128)(2,1)S(1)}, bf16[512,4096]{1,0:T(8,128)(2,1)}, u32[]{:S(2)}) copy-start(bf16[512,4096]{1,0:T(8,128)(2,1)} %reshape.108) | copy-start | bytes 12582916
  122.5 5.3 %copy-start.14 = (bf16[512,768]{1,0:T(8,128)(2,1)S(1)}, bf16[512,768]{1,0:T(8,128)(2,1)}, u32[]{:S(2)}) copy-start(bf16[512,768]{1,0:T(8,128)(2,1)} %copy-done.13) | copy-start | bytes 2359300
  127.8 3.7 %copy-start.16 = (bf16[512,768]{1,0:T(8,128)(2,1)S(1)}, bf16[512,768]{1,0:T(8,128)(2,1)}, u32[]{:S(2)}) copy-start(bf16[512,768]{1,0:T(8,128)(2,1)} %copy-done.15) | copy-start | bytes 2359300
  180.3 3.4 %copy-start.2 = (bf16[512,4096]{1,0:T(8,128)(2,1)S(1)}, bf16[512,4096]{1,0:T(8,128)(2,1)}, u32[]{:S(2)}) copy-start(bf16[512,4096]{1,0:T(8,128)(2,1)} %reshape.110) | copy-start | bytes 12582916
  183.7 1.0 copy-start.7
  184.5 7.2 %copy-start.6 = (bf16[128,2048]{1,0:T(8,128)(2,1)S(1)}, bf16[128,2048]{1,0:T(8,128)(2,1)}, u32[]{:S(2)}) copy-start(bf16[128,2048]{1,0:T(8,128)(2,1)} %param.8) | copy-start | bytes 1572868
  184.5 1.3 collective-permute-start.3
  185.8 3.7 %collective-permute-start.4 = (f32[2048]{0:T(1024)S(1)}, f32[2048]{0:T(1024)S(1)}, u32[]{:S(2)}, u32[]{:S(2)}) collective-permute-start(f32[2048]{0:T(1024)S(1)} %add.86), channel_id=1, source_target_pairs={{0,16},{1,17},{2,18},{3,19},{4,20},{5,21},{6,22},{7,23},{8,24},{9,... | collective-permute-start | bytes 24584 | tf_op jit(solution)/shard_map/ppermute | solution.py:23
  189.4 5.2 %collective-permute-start.5 = (f32[2048]{0:T(1024)S(1)}, f32[2048]{0:T(1024)S(1)}, u32[]{:S(2)}, u32[]{:S(2)}) collective-permute-start(f32[2048]{0:T(1024)S(1)} %add.87), channel_id=1, source_target_pairs={{0,32},{1,33},{2,34},{3,35},{4,36},{5,37},{6,38},{7,39},{8,40},{9,... | collective-permute-start | bytes 24584 | tf_op jit(solution)/shard_map/ppermute | solution.py:23
  191.7 8.7 %copy-start.1 = (bf16[1,2048,768]{2,1,0:T(8,128)(2,1)S(1)}, bf16[1,2048,768]{2,1,0:T(8,128)(2,1)}, u32[]{:S(2)}) copy-start(bf16[1,2048,768]{2,1,0:T(8,128)(2,1)} %param.13) | copy-start | bytes 9437188
  194.6 5.2 %collective-permute-start.6 = (f32[2048]{0:T(1024)S(1)}, f32[2048]{0:T(1024)S(1)}, u32[]{:S(2)}, u32[]{:S(2)}) collective-permute-start(f32[2048]{0:T(1024)S(1)} %add.88), channel_id=1, source_target_pairs={{0,64},{1,65},{2,66},{3,67},{4,68},{5,69},{6,70},{7,71},{8,72},{9,... | collective-permute-start | bytes 24584 | tf_op jit(solution)/shard_map/ppermute | solution.py:23

commit v10 on v9

--- a/solution.py
+++ b/solution.py
@@ -92,7 +92,7 @@
     back = jnp.concatenate([expert_out, grad_back], axis=1).reshape(
         devices_all, capacity, 2 * width
     )
-    bits = [1 << b for b in range(devices_all.bit_length() - 1)]
+    bits = [1 << b for b in (6, 5, 2, 0, 1, 3, 4)]
     gain_part = all_sum(gain_part, devices_all, bits[:3])
     back, gain_part = lax.optimization_barrier((back, gain_part))
     returned, grad_gate, grad_up, grad_down, gain_part = lax.optimization_barrier(

time: 201 us -> 202 us (level)
  transfers between devices with their start and end apart: 8 -> 8, of which waited for: 7 -> 6; matrix products, arithmetic and copies ran while one was open for 13% -> 13% of each run, Pallas kernels for 0% -> 0%
where the time goes in v10:
time: 202 us; the launch traced here: 201 us
  blocking collectives  63 us (31%)
  waiting for transfers between devices  51.5 us (25%)
  matrix products  33.4 us (17%)
  local copies, waits for them, and re-layouts  26.5 us (13%)
  starting transfers between devices  13.5 us (7%)
  other arithmetic  11.8 us (6%)
    all_to_all x1, blocking collectives, exchange(): return lax.all_to_all(rows, AXES, split_axis=0, concat_axis=0, tiled=True)  63 us
    all_to_all x1, waiting for transfers between devices, exchange(): return lax.all_to_all(rows, AXES, split_axis=0, concat_axis=0, tiled=True)  38.2 us
    dot_general x8, matrix products, contract(): lax.dot_general(left, right, (((left_dim,), (right_dim,)), ((), ())), pre...  24.7 us
    ppermute x7, waiting for transfers between devices, all_sum(): total = total + lax.ppermute(total, AXES, pairs)  13.2 us
    ppermute x7, starting transfers between devices, all_sum(): total = total + lax.ppermute(total, AXES, pairs)  7.27 us
    reshape x1, local copies, waits for them, and re-layouts, on_device(): jnp.concatenate([expert_out, grad_back], axis=1)  7.17 us
    reshape x1, local copies, waits for them, and re-layouts, on_device(): returned = returned.reshape(slots, 2 * width)  6.88 us
    reshape x1, local copies, waits for them, and re-layouts, on_device(): arrived_all = exchange(sent).reshape(slots, 2 * width)  6.88 us
  transfers between devices with their start and end apart: 8, of which 6 were waited for; matrix products, arithmetic and copies ran while one was open for 13% of the time, Pallas kernels for 0%

profile of v10, /device:TPU:0, one launch (start us, length us, event | category | flops | bytes accessed | tf_op | source)
XLA Modules:
  0.0 200.6 jit_solution(18354477908013195505)
XLA Ops:
  0.6 0.0 copy-start
  0.7 0.9 copy.37
  1.6 0.1 eq.57
  1.7 0.1 eq.53
  1.9 2.1 %convert_element_type.72 = f32[128,2048]{1,0:T(8,128)} convert(bf16[128,2048]{1,0:T(8,128)(2,1)} %param.15) | non-fusion elementwise | flops 262144 | bytes 1572864 | tf_op jit(solution)/shard_map/convert_element_type | solution.py:71
  4.0 0.1 copy.39
  4.1 0.2 fusion.45
  4.4 0.2 fusion.47
  4.6 0.1 reduce_sum.78
  4.8 0.1 copy.41
  4.8 0.7 multiply_add_fusion.1
  5.5 0.1 convert_reduce_fusion
  5.7 0.1 copy.42
  5.8 0.0 copy-start.8
  5.8 1.8 convolution_convert_fusion.3
  7.6 0.8 bitcast_convert_fusion
  8.4 0.3 pad_maximum_fusion
  8.7 3.2 %copy.44 = bf16[128,4,4096]{2,1,0:T(4,128)(2,1)S(1)} copy(bf16[128,4,4096]{2,0,1:T(8,128)(2,1)S(1)} %pad_maximum_fusion) | data formatting | bytes 8388608 | tf_op jit(solution)/shard_map/concatenate | solution.py:79
  12.0 63.0 %all_to_all.10 = bf16[128,4,4096]{2,1,0:T(4,128)(2,1)} all-to-all(bf16[128,4,4096]{2,1,0:T(4,128)(2,1)S(1)} %copy.44), channel_id=1, replica_groups=mesh['expert'=16,'dp'=8] {'expert','dp'}, dimensions={0} | all-to-all | bytes 8388608 | tf_op jit(solution)/shard_map/all_to_all | solution.py:10
  75.0 6.9 %reshape.108 = bf16[512,4096]{1,0:T(8,128)(2,1)} reshape(bf16[128,4,4096]{2,1,0:T(4,128)(2,1)} %all_to_all.10) | data formatting | bytes 8388608 | tf_op jit(solution)/shard_map/reshape | solution.py:80
  81.8 2.1 %fusion.4 = f32[512]{0:T(512)S(1)} fusion(bf16[512,4096]{1,0:T(8,128)(2,1)} %reshape.108), kind=kLoop, calls=%fused_computation.6 | loop fusion | flops 3145216 | bytes 2099200 | tf_op jit(solution)/shard_map/reduce_sum | solution.py:83
  83.9 0.0 copy-start.9
  83.9 0.0 copy-start.11
  84.0 4.5 %fusion.5 = f32[512,768]{1,0:T(8,128)S(1)} fusion(bf16[1,768,2048]{2,1,0:T(8,128)(2,1)} %param.14, bf16[512,4096]{1,0:T(8,128)(2,1)} %reshape.108), kind=kOutput, calls=%fused_computation.14 | convolution fusion | flops 1610612736 | bytes 6815744 | tf_op jit(solution)/shard_map/dot_general | solution.py:14
  88.5 0.2 copy-done.11
  88.7 1.9 fusion.15
  90.6 2.4 %multiply_convert_fusion.3 = (bf16[512,768]{1,0:T(8,128)(2,1)S(1)}, bf16[512,768]{1,0:T(8,128)(2,1)S(1)}, bf16[512,768]{1,0:T(8,128)(2,1)S(1)}) fusion(f32[512,768]{1,0:T(8,128)S(1)} %fusion.15, f32[512,768]{1,0:T(8,128)S(1)} %fusion.5, bf16[1,2048,768]{2,1,0:T(8,128)(2,1)S(1)} %copy-done, f32[2048]{0:T(1024)S(1)} %copy-done.9, f32[512]{0:T(512)S(1)} %add_rsqrt_fusion, ...), kind=kOutput, calls=%fused_computation.33 | convolution fusion | flops 1620705280 | bytes 10758144 | tf_op jit(solution)/shard_map/dot_general | solution.py:29
  92.9 0.0 copy-start.13
  92.9 0.0 copy-start.17
  93.0 1.8 fusion.9
  94.8 0.0 copy-start.12
  94.8 2.0 %fusion.3 = (f32[2048]{0:T(1024)S(1)}, bf16[512,2048]{1,0:T(8,128)(2,1)S(1)}) fusion(f32[512]{0:T(512)S(1)} %add_rsqrt_fusion, bf16[512,4096]{1,0:T(8,128)(2,1)S(1)} %copy-done.3, f32[512,2048]{1,0:T(8,128)S(1)} %fusion.9, bf16[512,768]{1,0:T(8,128)(2,1)S(1)} %get-tuple-element.27, bf16[1,2048,768]{2,1,0:T(8,128)(2,1)S(1)} %copy-done.11), kind=kOutput, calls=%fused_computation.5 | convolution fusion | flops 1617950720 | bytes 12331008 | tf_op jit(solution)/shard_map/dot_general | solution.py:14
  96.8 0.1 collective-permute-start
  96.9 5.1 %collective-permute-done = f32[2048]{0:T(1024)S(1)} collective-permute-done((f32[2048]{0:T(1024)S(1)}, f32[2048]{0:T(1024)S(1)}, u32[]{:S(2)}, u32[]{:S(2)}) %collective-permute-start) | collective-permute-done | bytes 8224 | tf_op jit(solution)/shard_map/ppermute | solution.py:23
  102.1 2.2 %collective-permute-start.1 = (f32[2048]{0:T(1024)S(1)}, f32[2048]{0:T(1024)S(1)}, u32[]{:S(2)}, u32[]{:S(2)}) collective-permute-start(f32[2048]{0:T(1024)S(1)} %add.81), channel_id=1, source_target_pairs={{0,32},{1,33},{2,34},{3,35},{4,36},{5,37},{6,38},{7,39},{8,40},{9,... | collective-permute-start | bytes 24584 | tf_op jit(solution)/shard_map/ppermute | solution.py:23
  104.3 1.8 fusion.17
  106.1 1.1 collective-permute-done.1
  107.2 2.1 %collective-permute-start.2 = (f32[2048]{0:T(1024)S(1)}, f32[2048]{0:T(1024)S(1)}, u32[]{:S(2)}, u32[]{:S(2)}) collective-permute-start(f32[2048]{0:T(1024)S(1)} %add.82), channel_id=1, source_target_pairs={{0,4},{1,5},{2,6},{3,7},{4,0},{5,1},{6,2},{7,3},{8,12},{9,13},{10,... | collective-permute-start | bytes 24584 | tf_op jit(solution)/shard_map/ppermute | solution.py:23
  109.3 2.5 %pad_maximum_fusion.1 = bf16[512,4096]{1,0:T(8,128)(2,1)} fusion(bf16[512,2048]{1,0:T(8,128)(2,1)S(1)} %get-tuple-element.32, bf16[512,2048]{1,0:T(8,128)(2,1)S(1)} %fusion.17), kind=kLoop, calls=%fused_computation.8 | loop fusion | flops 8388608 | bytes 8388608 | tf_op jit(solution)/shard_map/concatenate | solution.py:92
  111.8 7.2 %reshape.109 = bf16[128,4,4096]{2,1,0:T(4,128)(2,1)} reshape(bf16[512,4096]{1,0:T(8,128)(2,1)} %pad_maximum_fusion.1) | data formatting | bytes 8388608 | tf_op jit(solution)/shard_map/reshape | solution.py:92
  118.9 0.0 copy-start.18
  119.0 6.2 %all-to-all-start.1 = ((bf16[128,4,4096]{2,1,0:T(4,128)(2,1)}), bf16[128,4,4096]{2,1,0:T(4,128)(2,1)}, u32[]{:S(2)}, u32[]{:S(2)}) async-start(bf16[128,4,4096]{2,1,0:T(4,128)(2,1)} %reshape.109), calls=%async_computation.1 | async-start | bytes 8388608 | tf_op jit(solution)/shard_map/all_to_all | solution.py:10
  125.2 0.2 fusion.33
  125.4 0.1 iota_compare_fusion
  125.5 0.0 copy-start.14
  125.6 5.3 %convolution_convert_fusion = bf16[768,2048]{1,0:T(8,128)(2,1)} fusion(bf16[512,768]{1,0:T(8,128)(2,1)S(1)} %copy-done.18, bf16[512,4096]{1,0:T(8,128)(2,1)} %reshape.108), kind=kOutput, calls=%fused_computation.11 | convolution fusion | flops 1612185600 | bytes 6029312 | tf_op jit(solution)/shard_map/dot_general | solution.py:14
  130.8 3.7 %convolution_convert_fusion.2 = bf16[2048,768]{1,0:T(8,128)(2,1)} fusion(bf16[512,768]{1,0:T(8,128)(2,1)S(1)} %copy-done.14, f32[2048]{0:T(1024)S(1)} %copy-done.9, f32[512]{0:T(512)S(1)} %add_rsqrt_fusion, bf16[512,4096]{1,0:T(8,128)(2,1)S(1)} %copy-done.4), kind=kOutput, calls=%fused_computation.13 | convolution fusion | flops 1616379904 | bytes 6039552 | tf_op jit(solution)/shard_map/dot_general | solution.py:14
  134.5 3.7 %convolution_convert_fusion.1 = bf16[2048,768]{1,0:T(8,128)(2,1)} fusion(bf16[512,768]{1,0:T(8,128)(2,1)S(1)} %copy-done.16, f32[2048]{0:T(1024)S(1)} %copy-done.9, f32[512]{0:T(512)S(1)} %add_rsqrt_fusion, bf16[512,4096]{1,0:T(8,128)(2,1)S(1)} %copy-done.4), kind=kOutput, calls=%fused_computation.12 | convolution fusion | flops 1616379904 | bytes 6039552 | tf_op jit(solution)/shard_map/dot_general | solution.py:14
  138.2 38.2 %all-to-all-done.1 = bf16[128,4,4096]{2,1,0:T(4,128)(2,1)} async-done(((bf16[128,4,4096]{2,1,0:T(4,128)(2,1)}), bf16[128,4,4096]{2,1,0:T(4,128)(2,1)}, u32[]{:S(2)}, u32[]{:S(2)}) %all-to-all-start.1) | async-done | bytes 4194336 | tf_op jit(solution)/shard_map/all_to_all | solution.py:10
  176.4 6.9 %reshape.110 = bf16[512,4096]{1,0:T(8,128)(2,1)} reshape(bf16[128,4,4096]{2,1,0:T(4,128)(2,1)} %all-to-all-done.1) | data formatting | bytes 8388608 | tf_op jit(solution)/shard_map/reshape | solution.py:102
  183.3 3.1 %fusion.43 = f32[128,4096]{1,0:T(8,128)S(1)} fusion(bf16[512,4096]{1,0:T(8,128)(2,1)} %reshape.110, pred[128,2,512]{2,0,1:T(32,128)(4,1)S(1)} %iota_compare_fusion), kind=kOutput, calls=%fused_computation.62 | convolution fusion | flops 536870912 | bytes 6356992 | tf_op jit(solution)/shard_map/dot_general | solution.py:14
  186.4 0.4 copy-done.2
  186.7 0.7 fusion.44
  187.5 0.0 copy-start.6
  187.5 0.9 collective-permute-start.3
  188.4 0.6 fusion.27
  189.0 2.2 %collective-permute-done.3 = f32[2048]{0:T(1024)S(1)} collective-permute-done((f32[2048]{0:T(1024)S(1)}, f32[2048]{0:T(1024)S(1)}, u32[]{:S(2)}, u32[]{:S(2)}) %collective-permute-start.3) | collective-permute-done | bytes 8224 | tf_op jit(solution)/shard_map/ppermute | solution.py:23
  191.2 0.7 collective-permute-start.4
  192.0 2.9 %collective-permute-done.4 = f32[2048]{0:T(1024)S(1)} collective-permute-done((f32[2048]{0:T(1024)S(1)}, f32[2048]{0:T(1024)S(1)}, u32[]{:S(2)}, u32[]{:S(2)}) %collective-permute-start.4) | collective-permute-done | bytes 8224 | tf_op jit(solution)/shard_map/ppermute | solution.py:23
  194.9 1.5 fusion.31
  196.4 1.2 collective-permute-start.6
  197.6 0.6 pad_maximum_fusion.2
  198.2 1.8 collective-permute-done.6
  200.0 0.6 add.89
  (46 shorter events, 0.2 us)
Async XLA Ops:
  0.6 89.9 %copy-start = (bf16[1,2048,768]{2,1,0:T(8,128)(2,1)S(1)}, bf16[1,2048,768]{2,1,0:T(8,128)(2,1)}, u32[]{:S(2)}) copy-start(bf16[1,2048,768]{2,1,0:T(8,128)(2,1)} %param.13) | copy-start | bytes 9437188
  0.6 7.0 %copy-start.10 = (f32[128,2]{0,1:T(2,128)S(1)}, f32[128,2]{0,1:T(2,128)}, u32[]{:S(2)}) copy-start(f32[128,2]{0,1:T(2,128)} %param.10) | copy-start | bytes 3076
  5.8 1.9 copy-start.8
  83.9 4.5 %copy-start.3 = (bf16[512,4096]{1,0:T(8,128)(2,1)S(1)}, bf16[512,4096]{1,0:T(8,128)(2,1)}, u32[]{:S(2)}) copy-start(bf16[512,4096]{1,0:T(8,128)(2,1)} %reshape.108) | copy-start | bytes 12582916
  83.9 4.5 %copy-start.9 = (f32[2048]{0:T(1024)S(1)}, f32[2048]{0:T(1024)}, u32[]{:S(2)}) copy-start(f32[2048]{0:T(1024)} %param.11) | copy-start | bytes 24580
  83.9 4.7 %copy-start.11 = (bf16[1,2048,768]{2,1,0:T(8,128)(2,1)S(1)}, bf16[1,2048,768]{2,1,0:T(8,128)(2,1)}, u32[]{:S(2)}) copy-start(bf16[1,2048,768]{2,1,0:T(8,128)(2,1)} %param.12) | copy-start | bytes 9437188
  92.9 1.9 copy-start.15
  92.9 1.9 copy-start.13
  92.9 11.4 %copy-start.17 = (bf16[512,768]{1,0:T(8,128)(2,1)}, bf16[512,768]{1,0:T(8,128)(2,1)S(1)}, u32[]{:S(2)}) copy-start(bf16[512,768]{1,0:T(8,128)(2,1)S(1)} %get-tuple-element.26) | copy-start | bytes 2359300
  94.8 9.5 %copy-start.12 = (bf16[1,768,2048]{2,1,0:T(8,128)(2,1)S(1)}, bf16[1,768,2048]{2,1,0:T(8,128)(2,1)}, u32[]{:S(2)}) copy-start(bf16[1,768,2048]{2,1,0:T(8,128)(2,1)} %param.14) | copy-start | bytes 9437188
  96.8 5.2 %collective-permute-start = (f32[2048]{0:T(1024)S(1)}, f32[2048]{0:T(1024)S(1)}, u32[]{:S(2)}, u32[]{:S(2)}) collective-permute-start(f32[2048]{0:T(1024)S(1)} %get-tuple-element.31), channel_id=1, source_target_pairs={{0,64},{1,65},{2,66},{3,67},{4,68},{5,69},{6,70},{7,71},{8,72},{9,... | collective-permute-start | bytes 24584 | tf_op jit(solution)/shard_map/ppermute | solution.py:23
  102.1 5.2 %collective-permute-start.1 = (f32[2048]{0:T(1024)S(1)}, f32[2048]{0:T(1024)S(1)}, u32[]{:S(2)}, u32[]{:S(2)}) collective-permute-start(f32[2048]{0:T(1024)S(1)} %add.81), channel_id=1, source_target_pairs={{0,32},{1,33},{2,34},{3,35},{4,36},{5,37},{6,38},{7,39},{8,40},{9,... | collective-permute-start | bytes 24584 | tf_op jit(solution)/shard_map/ppermute | solution.py:23
  107.2 11.7 %collective-permute-start.2 = (f32[2048]{0:T(1024)S(1)}, f32[2048]{0:T(1024)S(1)}, u32[]{:S(2)}, u32[]{:S(2)}) collective-permute-start(f32[2048]{0:T(1024)S(1)} %add.82), channel_id=1, source_target_pairs={{0,4},{1,5},{2,6},{3,7},{4,0},{5,1},{6,2},{7,3},{8,12},{9,13},{10,... | collective-permute-start | bytes 24584 | tf_op jit(solution)/shard_map/ppermute | solution.py:23
  118.9 6.2 %copy-start.5 = (bf16[128,2048]{1,0:T(8,128)(2,1)S(1)}, bf16[128,2048]{1,0:T(8,128)(2,1)}, u32[]{:S(2)}) copy-start(bf16[128,2048]{1,0:T(8,128)(2,1)} %param.8) | copy-start | bytes 1572868
  118.9 6.6 %copy-start.18 = (bf16[512,768]{1,0:T(8,128)(2,1)S(1)}, bf16[512,768]{1,0:T(8,128)(2,1)}, u32[]{:S(2)}) copy-start(bf16[512,768]{1,0:T(8,128)(2,1)} %copy-done.17) | copy-start | bytes 2359300
  119.0 57.5 %all-to-all-start.1 = ((bf16[128,4,4096]{2,1,0:T(4,128)(2,1)}), bf16[128,4,4096]{2,1,0:T(4,128)(2,1)}, u32[]{:S(2)}, u32[]{:S(2)}) async-start(bf16[128,4,4096]{2,1,0:T(4,128)(2,1)} %reshape.109), calls=%async_computation.1 | async-start | bytes 8388608 | tf_op jit(solution)/shard_map/all_to_all | solution.py:10
  125.5 5.3 %copy-start.4 = (bf16[512,4096]{1,0:T(8,128)(2,1)S(1)}, bf16[512,4096]{1,0:T(8,128)(2,1)}, u32[]{:S(2)}) copy-start(bf16[512,4096]{1,0:T(8,128)(2,1)} %reshape.108) | copy-start | bytes 12582916
  125.5 5.3 %copy-start.14 = (bf16[512,768]{1,0:T(8,128)(2,1)S(1)}, bf16[512,768]{1,0:T(8,128)(2,1)}, u32[]{:S(2)}) copy-start(bf16[512,768]{1,0:T(8,128)(2,1)} %copy-done.13) | copy-start | bytes 2359300
  130.8 3.7 %copy-start.16 = (bf16[512,768]{1,0:T(8,128)(2,1)S(1)}, bf16[512,768]{1,0:T(8,128)(2,1)}, u32[]{:S(2)}) copy-start(bf16[512,768]{1,0:T(8,128)(2,1)} %copy-done.15) | copy-start | bytes 2359300
  183.3 3.4 %copy-start.2 = (bf16[512,4096]{1,0:T(8,128)(2,1)S(1)}, bf16[512,4096]{1,0:T(8,128)(2,1)}, u32[]{:S(2)}) copy-start(bf16[512,4096]{1,0:T(8,128)(2,1)} %reshape.110) | copy-start | bytes 12582916
  186.7 1.7 copy-start.7
  187.5 7.4 %copy-start.6 = (bf16[128,2048]{1,0:T(8,128)(2,1)S(1)}, bf16[128,2048]{1,0:T(8,128)(2,1)}, u32[]{:S(2)}) copy-start(bf16[128,2048]{1,0:T(8,128)(2,1)} %param.8) | copy-start | bytes 1572868
  187.5 3.7 %collective-permute-start.3 = (f32[2048]{0:T(1024)S(1)}, f32[2048]{0:T(1024)S(1)}, u32[]{:S(2)}, u32[]{:S(2)}) collective-permute-start(f32[2048]{0:T(1024)S(1)} %add.83), channel_id=1, source_target_pairs={{0,1},{1,0},{2,3},{3,2},{4,5},{5,4},{6,7},{7,6},{8,9},{9,8},{10,11... | collective-permute-start | bytes 24584 | tf_op jit(solution)/shard_map/ppermute | solution.py:23
  191.2 3.7 %collective-permute-start.4 = (f32[2048]{0:T(1024)S(1)}, f32[2048]{0:T(1024)S(1)}, u32[]{:S(2)}, u32[]{:S(2)}) collective-permute-start(f32[2048]{0:T(1024)S(1)} %add.86), channel_id=1, source_target_pairs={{0,2},{1,3},{2,0},{3,1},{4,6},{5,7},{6,4},{7,5},{8,10},{9,11},{10,... | collective-permute-start | bytes 24584 | tf_op jit(solution)/shard_map/ppermute | solution.py:23
  194.9 1.5 collective-permute-start.5
  194.9 5.7 %copy-start.1 = (bf16[1,2048,768]{2,1,0:T(8,128)(2,1)S(1)}, bf16[1,2048,768]{2,1,0:T(8,128)(2,1)}, u32[]{:S(2)}) copy-start(bf16[1,2048,768]{2,1,0:T(8,128)(2,1)} %param.13) | copy-start | bytes 9437188
  196.4 3.7 %collective-permute-start.6 = (f32[2048]{0:T(1024)S(1)}, f32[2048]{0:T(1024)S(1)}, u32[]{:S(2)}, u32[]{:S(2)}) collective-permute-start(f32[2048]{0:T(1024)S(1)} %add.88), channel_id=1, source_target_pairs={{0,16},{1,17},{2,18},{3,19},{4,20},{5,21},{6,22},{7,23},{8,24},{9,... | collective-permute-start | bytes 24584 | tf_op jit(solution)/shard_map/ppermute | solution.py:23

commit v11 on v9

--- a/solution.py
+++ b/solution.py
@@ -54,9 +54,6 @@
     assigned = tok_rows * top_count
     capacity = 2 * assigned // devices_all
     slots = devices_all * capacity
-    inputs = tokens.astype(jnp.float32)
-    inverse_rms = lax.rsqrt(jnp.mean(inputs * inputs, axis=1, keepdims=True) + 1e-06)
-    normed = inputs * inverse_rms
     flat_ids = routes.reshape(assigned)
     onehot = (flat_ids[:, None] == jnp.arange(devices_all, dtype=jnp.int32)[None, :]).astype(
         jnp.int32
@@ -68,8 +65,9 @@
     )
     select_tk = select.reshape(tok_rows, top_count, slots)
     select_tok = jnp.sum(select_tk, axis=1)
-    grad_in = out_grad.astype(jnp.float32)
-    grad_rows = (gate_probs[:, :, None] * grad_in[:, None, :]).astype(jnp.bfloat16)
+    grad_rows = (gate_probs[:, :, None] * out_grad.astype(jnp.float32)[:, None, :]).astype(
+        jnp.bfloat16
+    )
     sel_tok3 = select_tok.reshape(tok_rows, devices_all, capacity)
     sel_tk3 = select_tk.reshape(tok_rows, top_count, devices_all, capacity)
     send_scaled = lax.dot_general(sel_tok3, tokens, (((0,), (0,)), ((), ())), preferred_element_type=jnp.float32).astype(jnp.bfloat16)
@@ -95,9 +93,15 @@
     bits = [1 << b for b in range(devices_all.bit_length() - 1)]
     gain_part = all_sum(gain_part, devices_all, bits[:3])
     back, gain_part = lax.optimization_barrier((back, gain_part))
-    returned, grad_gate, grad_up, grad_down, gain_part = lax.optimization_barrier(
-        (exchange(back), grad_gate, grad_up, grad_down, gain_part)
+    returned, grad_gate, grad_up, grad_down, gain_part, late_grad, late_tokens = (
+        lax.optimization_barrier(
+            (exchange(back), grad_gate, grad_up, grad_down, gain_part, out_grad, tokens)
+        )
     )
+    inputs = late_tokens.astype(jnp.float32)
+    inverse_rms = lax.rsqrt(jnp.mean(inputs * inputs, axis=1, keepdims=True) + 1e-06)
+    normed = inputs * inverse_rms
+    grad_in = late_grad.astype(jnp.float32)
     grad_gain = all_sum(gain_part, devices_all, bits[3:])
     returned = returned.reshape(slots, 2 * width)
     picked = [

time: 201 us -> 202 us (level)
  no operation moved by 1% of the time
where the time goes in v11:
time: 202 us; the launch traced here: 201 us
  blocking collectives  63 us (31%)
  waiting for transfers between devices  51.4 us (25%)
  matrix products  33.4 us (17%)
  local copies, waits for them, and re-layouts  26.8 us (13%)
  starting transfers between devices  13.5 us (7%)
  other arithmetic  11.8 us (6%)
    all_to_all x1, blocking collectives, exchange(): return lax.all_to_all(rows, AXES, split_axis=0, concat_axis=0, tiled=True)  63 us
    all_to_all x1, waiting for transfers between devices, exchange(): return lax.all_to_all(rows, AXES, split_axis=0, concat_axis=0, tiled=True)  38.4 us
    dot_general x8, matrix products, contract(): lax.dot_general(left, right, (((left_dim,), (right_dim,)), ((), ())), pre...  24.8 us
    ppermute x7, waiting for transfers between devices, all_sum(): total = total + lax.ppermute(total, AXES, pairs)  12.9 us
    ppermute x7, starting transfers between devices, all_sum(): total = total + lax.ppermute(total, AXES, pairs)  7.27 us
    reshape x1, local copies, waits for them, and re-layouts, on_device(): jnp.concatenate([expert_out, grad_back], axis=1)  7.18 us
    reshape x1, local copies, waits for them, and re-layouts, on_device(): arrived_all = exchange(sent).reshape(slots, 2 * width)  6.88 us
    reshape x1, local copies, waits for them, and re-layouts, on_device(): returned = returned.reshape(slots, 2 * width)  6.88 us
  transfers between devices with their start and end apart: 8, of which 7 were waited for; matrix products, arithmetic and copies ran while one was open for 13% of the time, Pallas kernels for 0%

profile of v11, /device:TPU:0, one launch (start us, length us, event | category | flops | bytes accessed | tf_op | source)
XLA Modules:
  0.0 200.8 jit_solution(1317781078038878303)
XLA Ops:
  0.6 0.0 copy-start
  0.7 0.9 copy.37
  1.6 0.1 eq.57
  1.7 0.1 eq.53
  1.9 2.1 %convert_element_type.74 = f32[128,2048]{1,0:T(8,128)} convert(bf16[128,2048]{1,0:T(8,128)(2,1)} %param.15) | non-fusion elementwise | flops 262144 | bytes 1572864 | tf_op jit(solution)/shard_map/convert_element_type | solution.py:68
  4.0 0.1 copy.39
  4.1 0.2 fusion.46
  4.4 0.2 fusion.48
  4.6 0.1 reduce_sum.78
  4.8 0.1 copy.41
  4.8 0.7 multiply_add_fusion.1
  5.5 0.1 convert_reduce_fusion
  5.7 0.1 copy.42
  5.8 0.0 copy-start.7
  5.8 1.8 convolution_convert_fusion.3
  7.6 0.8 bitcast_convert_fusion
  8.4 0.3 pad_maximum_fusion
  8.7 3.2 %copy.44 = bf16[128,4,4096]{2,1,0:T(4,128)(2,1)S(1)} copy(bf16[128,4,4096]{2,0,1:T(8,128)(2,1)S(1)} %pad_maximum_fusion) | data formatting | bytes 8388608 | tf_op jit(solution)/shard_map/concatenate | solution.py:77
  12.0 63.0 %all_to_all.10 = bf16[128,4,4096]{2,1,0:T(4,128)(2,1)} all-to-all(bf16[128,4,4096]{2,1,0:T(4,128)(2,1)S(1)} %copy.44), channel_id=1, replica_groups=mesh['expert'=16,'dp'=8] {'expert','dp'}, dimensions={0} | all-to-all | bytes 8388608 | tf_op jit(solution)/shard_map/all_to_all | solution.py:10
  75.0 6.9 %reshape.108 = bf16[512,4096]{1,0:T(8,128)(2,1)} reshape(bf16[128,4,4096]{2,1,0:T(4,128)(2,1)} %all_to_all.10) | data formatting | bytes 8388608 | tf_op jit(solution)/shard_map/reshape | solution.py:78
  81.8 2.1 %fusion.4 = f32[512]{0:T(512)S(1)} fusion(bf16[512,4096]{1,0:T(8,128)(2,1)} %reshape.108), kind=kLoop, calls=%fused_computation.6 | loop fusion | flops 3145216 | bytes 2099200 | tf_op jit(solution)/shard_map/reduce_sum | solution.py:81
  83.9 0.0 copy-start.8
  83.9 0.0 copy-start.10
  84.0 4.5 %fusion.5 = f32[512,768]{1,0:T(8,128)S(1)} fusion(bf16[1,768,2048]{2,1,0:T(8,128)(2,1)} %param.14, bf16[512,4096]{1,0:T(8,128)(2,1)} %reshape.108), kind=kOutput, calls=%fused_computation.14 | convolution fusion | flops 1610612736 | bytes 6815744 | tf_op jit(solution)/shard_map/dot_general | solution.py:14
  88.5 0.2 copy-done.10
  88.7 1.9 fusion.15
  90.6 2.4 %multiply_convert_fusion.3 = (bf16[512,768]{1,0:T(8,128)(2,1)S(1)}, bf16[512,768]{1,0:T(8,128)(2,1)S(1)}, bf16[512,768]{1,0:T(8,128)(2,1)S(1)}) fusion(f32[512,768]{1,0:T(8,128)S(1)} %fusion.15, f32[512,768]{1,0:T(8,128)S(1)} %fusion.5, bf16[1,2048,768]{2,1,0:T(8,128)(2,1)S(1)} %copy-done, f32[2048]{0:T(1024)S(1)} %copy-done.8, f32[512]{0:T(512)S(1)} %add_rsqrt_fusion, ...), kind=kOutput, calls=%fused_computation.39 | convolution fusion | flops 1620705280 | bytes 10758144 | tf_op jit(solution)/shard_map/dot_general | solution.py:29
  92.9 0.0 copy-start.12
  92.9 0.0 copy-start.16
  93.0 1.8 fusion.9
  94.8 0.0 copy-start.11
  94.8 2.0 %fusion.3 = (f32[2048]{0:T(1024)S(1)}, bf16[512,2048]{1,0:T(8,128)(2,1)S(1)}) fusion(f32[512]{0:T(512)S(1)} %add_rsqrt_fusion, bf16[512,4096]{1,0:T(8,128)(2,1)S(1)} %copy-done.3, f32[512,2048]{1,0:T(8,128)S(1)} %fusion.9, bf16[512,768]{1,0:T(8,128)(2,1)S(1)} %get-tuple-element.31, bf16[1,2048,768]{2,1,0:T(8,128)(2,1)S(1)} %copy-done.10), kind=kOutput, calls=%fused_computation.5 | convolution fusion | flops 1617950720 | bytes 12331008 | tf_op jit(solution)/shard_map/dot_general | solution.py:14
  96.8 0.9 collective-permute-start
  97.8 2.8 %collective-permute-done = f32[2048]{0:T(1024)S(1)} collective-permute-done((f32[2048]{0:T(1024)S(1)}, f32[2048]{0:T(1024)S(1)}, u32[]{:S(2)}, u32[]{:S(2)}) %collective-permute-start) | collective-permute-done | bytes 8224 | tf_op jit(solution)/shard_map/ppermute | solution.py:23
  100.6 0.7 collective-permute-start.1
  101.3 1.8 fusion.17
  103.1 1.1 collective-permute-done.1
  104.2 2.1 %collective-permute-start.2 = (f32[2048]{0:T(1024)S(1)}, f32[2048]{0:T(1024)S(1)}, u32[]{:S(2)}, u32[]{:S(2)}) collective-permute-start(f32[2048]{0:T(1024)S(1)} %add.82), channel_id=1, source_target_pairs={{0,4},{1,5},{2,6},{3,7},{4,0},{5,1},{6,2},{7,3},{8,12},{9,13},{10,... | collective-permute-start | bytes 24584 | tf_op jit(solution)/shard_map/ppermute | solution.py:23
  106.3 2.5 %pad_maximum_fusion.1 = bf16[512,4096]{1,0:T(8,128)(2,1)} fusion(bf16[512,2048]{1,0:T(8,128)(2,1)S(1)} %get-tuple-element.36, bf16[512,2048]{1,0:T(8,128)(2,1)S(1)} %fusion.17), kind=kLoop, calls=%fused_computation.8 | loop fusion | flops 8388608 | bytes 8388608 | tf_op jit(solution)/shard_map/concatenate | solution.py:90
  108.8 7.2 %reshape.109 = bf16[128,4,4096]{2,1,0:T(4,128)(2,1)} reshape(bf16[512,4096]{1,0:T(8,128)(2,1)} %pad_maximum_fusion.1) | data formatting | bytes 8388608 | tf_op jit(solution)/shard_map/reshape | solution.py:90
  116.0 6.2 %all-to-all-start.1 = ((bf16[128,4,4096]{2,1,0:T(4,128)(2,1)}), bf16[128,4,4096]{2,1,0:T(4,128)(2,1)}, u32[]{:S(2)}, u32[]{:S(2)}) async-start(bf16[128,4,4096]{2,1,0:T(4,128)(2,1)} %reshape.109), calls=%async_computation.1 | async-start | bytes 8388608 | tf_op jit(solution)/shard_map/all_to_all | solution.py:10
  122.2 0.1 iota_compare_fusion
  122.4 5.3 %convolution_convert_fusion = bf16[768,2048]{1,0:T(8,128)(2,1)} fusion(bf16[512,768]{1,0:T(8,128)(2,1)S(1)} %copy-done.17, bf16[512,4096]{1,0:T(8,128)(2,1)} %reshape.108), kind=kOutput, calls=%fused_computation.11 | convolution fusion | flops 1612185600 | bytes 6029312 | tf_op jit(solution)/shard_map/dot_general | solution.py:14
  127.6 3.7 %convolution_convert_fusion.2 = bf16[2048,768]{1,0:T(8,128)(2,1)} fusion(bf16[512,768]{1,0:T(8,128)(2,1)S(1)} %copy-done.13, f32[2048]{0:T(1024)S(1)} %copy-done.8, f32[512]{0:T(512)S(1)} %add_rsqrt_fusion, bf16[512,4096]{1,0:T(8,128)(2,1)S(1)} %copy-done.4), kind=kOutput, calls=%fused_computation.13 | convolution fusion | flops 1616379904 | bytes 6039552 | tf_op jit(solution)/shard_map/dot_general | solution.py:14
  131.3 3.7 %convolution_convert_fusion.1 = bf16[2048,768]{1,0:T(8,128)(2,1)} fusion(bf16[512,768]{1,0:T(8,128)(2,1)S(1)} %copy-done.15, f32[2048]{0:T(1024)S(1)} %copy-done.8, f32[512]{0:T(512)S(1)} %add_rsqrt_fusion, bf16[512,4096]{1,0:T(8,128)(2,1)S(1)} %copy-done.4), kind=kOutput, calls=%fused_computation.12 | convolution fusion | flops 1616379904 | bytes 6039552 | tf_op jit(solution)/shard_map/dot_general | solution.py:14
  135.0 38.4 %all-to-all-done.1 = bf16[128,4,4096]{2,1,0:T(4,128)(2,1)} async-done(((bf16[128,4,4096]{2,1,0:T(4,128)(2,1)}), bf16[128,4,4096]{2,1,0:T(4,128)(2,1)}, u32[]{:S(2)}, u32[]{:S(2)}) %all-to-all-start.1) | async-done | bytes 4194336 | tf_op jit(solution)/shard_map/all_to_all | solution.py:10
  173.4 6.9 %reshape.110 = bf16[512,4096]{1,0:T(8,128)(2,1)} reshape(bf16[128,4,4096]{2,1,0:T(4,128)(2,1)} %all-to-all-done.1) | data formatting | bytes 8388608 | tf_op jit(solution)/shard_map/reshape | solution.py:106
  180.3 3.1 %fusion.44 = f32[128,4096]{1,0:T(8,128)S(1)} fusion(bf16[512,4096]{1,0:T(8,128)(2,1)} %reshape.110, pred[128,2,512]{2,0,1:T(32,128)(4,1)S(1)} %iota_compare_fusion), kind=kOutput, calls=%fused_computation.64 | convolution fusion | flops 536870912 | bytes 6356992 | tf_op jit(solution)/shard_map/dot_general | solution.py:14
  183.4 0.4 copy-done.2
  183.8 0.7 fusion.45
  184.5 0.3 copy-done.5
  184.8 0.2 fusion.31
  185.0 0.1 collective-permute-start.3
  185.1 0.6 fusion.27
  185.7 0.6 collective-permute-done.3
  186.2 1.2 collective-permute-start.4
  187.5 2.4 %collective-permute-done.4 = f32[2048]{0:T(1024)S(1)} collective-permute-done((f32[2048]{0:T(1024)S(1)}, f32[2048]{0:T(1024)S(1)}, u32[]{:S(2)}, u32[]{:S(2)}) %collective-permute-start.4) | collective-permute-done | bytes 8224 | tf_op jit(solution)/shard_map/ppermute | solution.py:23
  189.9 2.2 %collective-permute-start.5 = (f32[2048]{0:T(1024)S(1)}, f32[2048]{0:T(1024)S(1)}, u32[]{:S(2)}, u32[]{:S(2)}) collective-permute-start(f32[2048]{0:T(1024)S(1)} %add.87), channel_id=1, source_target_pairs={{0,32},{1,33},{2,34},{3,35},{4,36},{5,37},{6,38},{7,39},{8,40},{9,... | collective-permute-start | bytes 24584 | tf_op jit(solution)/shard_map/ppermute | solution.py:23
  192.1 1.4 fusion.34
  193.6 1.5 collective-permute-done.5
  195.1 0.0 collective-permute-start.6
  195.1 0.6 pad_maximum_fusion.2
  195.6 4.6 %collective-permute-done.6 = f32[2048]{0:T(1024)S(1)} collective-permute-done((f32[2048]{0:T(1024)S(1)}, f32[2048]{0:T(1024)S(1)}, u32[]{:S(2)}, u32[]{:S(2)}) %collective-permute-start.6) | collective-permute-done | bytes 8224 | tf_op jit(solution)/shard_map/ppermute | solution.py:23
  200.2 0.6 add.89
  (44 shorter events, 0.2 us)
Async XLA Ops:
  0.6 89.9 %copy-start = (bf16[1,2048,768]{2,1,0:T(8,128)(2,1)S(1)}, bf16[1,2048,768]{2,1,0:T(8,128)(2,1)}, u32[]{:S(2)}) copy-start(bf16[1,2048,768]{2,1,0:T(8,128)(2,1)} %param.13) | copy-start | bytes 9437188
  0.6 7.0 %copy-start.9 = (f32[128,2]{0,1:T(2,128)S(1)}, f32[128,2]{0,1:T(2,128)}, u32[]{:S(2)}) copy-start(f32[128,2]{0,1:T(2,128)} %param.10) | copy-start | bytes 3076
  5.8 1.9 copy-start.7
  83.9 4.5 %copy-start.3 = (bf16[512,4096]{1,0:T(8,128)(2,1)S(1)}, bf16[512,4096]{1,0:T(8,128)(2,1)}, u32[]{:S(2)}) copy-start(bf16[512,4096]{1,0:T(8,128)(2,1)} %reshape.108) | copy-start | bytes 12582916
  83.9 4.5 %copy-start.8 = (f32[2048]{0:T(1024)S(1)}, f32[2048]{0:T(1024)}, u32[]{:S(2)}) copy-start(f32[2048]{0:T(1024)} %param.11) | copy-start | bytes 24580
  83.9 4.7 %copy-start.10 = (bf16[1,2048,768]{2,1,0:T(8,128)(2,1)S(1)}, bf16[1,2048,768]{2,1,0:T(8,128)(2,1)}, u32[]{:S(2)}) copy-start(bf16[1,2048,768]{2,1,0:T(8,128)(2,1)} %param.12) | copy-start | bytes 9437188
  92.9 1.9 copy-start.14
  92.9 1.9 copy-start.12
  92.9 8.4 %copy-start.16 = (bf16[512,768]{1,0:T(8,128)(2,1)}, bf16[512,768]{1,0:T(8,128)(2,1)S(1)}, u32[]{:S(2)}) copy-start(bf16[512,768]{1,0:T(8,128)(2,1)S(1)} %get-tuple-element.30) | copy-start | bytes 2359300
  94.8 6.5 %copy-start.11 = (bf16[1,768,2048]{2,1,0:T(8,128)(2,1)S(1)}, bf16[1,768,2048]{2,1,0:T(8,128)(2,1)}, u32[]{:S(2)}) copy-start(bf16[1,768,2048]{2,1,0:T(8,128)(2,1)} %param.14) | copy-start | bytes 9437188
  96.8 3.7 %collective-permute-start = (f32[2048]{0:T(1024)S(1)}, f32[2048]{0:T(1024)S(1)}, u32[]{:S(2)}, u32[]{:S(2)}) collective-permute-start(f32[2048]{0:T(1024)S(1)} %get-tuple-element.35), channel_id=1, source_target_pairs={{0,1},{1,0},{2,3},{3,2},{4,5},{5,4},{6,7},{7,6},{8,9},{9,8},{10,11... | collective-permute-start | bytes 24584 | tf_op jit(solution)/shard_map/ppermute | solution.py:23
  100.6 3.7 %collective-permute-start.1 = (f32[2048]{0:T(1024)S(1)}, f32[2048]{0:T(1024)S(1)}, u32[]{:S(2)}, u32[]{:S(2)}) collective-permute-start(f32[2048]{0:T(1024)S(1)} %add.81), channel_id=1, source_target_pairs={{0,2},{1,3},{2,0},{3,1},{4,6},{5,7},{6,4},{7,5},{8,10},{9,11},{10,... | collective-permute-start | bytes 24584 | tf_op jit(solution)/shard_map/ppermute | solution.py:23
  104.2 11.7 %collective-permute-start.2 = (f32[2048]{0:T(1024)S(1)}, f32[2048]{0:T(1024)S(1)}, u32[]{:S(2)}, u32[]{:S(2)}) collective-permute-start(f32[2048]{0:T(1024)S(1)} %add.82), channel_id=1, source_target_pairs={{0,4},{1,5},{2,6},{3,7},{4,0},{5,1},{6,2},{7,3},{8,12},{9,13},{10,... | collective-permute-start | bytes 24584 | tf_op jit(solution)/shard_map/ppermute | solution.py:23
  115.9 6.4 %copy-start.17 = (bf16[512,768]{1,0:T(8,128)(2,1)S(1)}, bf16[512,768]{1,0:T(8,128)(2,1)}, u32[]{:S(2)}) copy-start(bf16[512,768]{1,0:T(8,128)(2,1)} %copy-done.16) | copy-start | bytes 2359300
  116.0 57.5 %all-to-all-start.1 = ((bf16[128,4,4096]{2,1,0:T(4,128)(2,1)}), bf16[128,4,4096]{2,1,0:T(4,128)(2,1)}, u32[]{:S(2)}, u32[]{:S(2)}) async-start(bf16[128,4,4096]{2,1,0:T(4,128)(2,1)} %reshape.109), calls=%async_computation.1 | async-start | bytes 8388608 | tf_op jit(solution)/shard_map/all_to_all | solution.py:10
  122.3 5.3 %copy-start.4 = (bf16[512,4096]{1,0:T(8,128)(2,1)S(1)}, bf16[512,4096]{1,0:T(8,128)(2,1)}, u32[]{:S(2)}) copy-start(bf16[512,4096]{1,0:T(8,128)(2,1)} %reshape.108) | copy-start | bytes 12582916
  122.3 5.3 %copy-start.13 = (bf16[512,768]{1,0:T(8,128)(2,1)S(1)}, bf16[512,768]{1,0:T(8,128)(2,1)}, u32[]{:S(2)}) copy-start(bf16[512,768]{1,0:T(8,128)(2,1)} %copy-done.12) | copy-start | bytes 2359300
  127.6 3.7 %copy-start.15 = (bf16[512,768]{1,0:T(8,128)(2,1)S(1)}, bf16[512,768]{1,0:T(8,128)(2,1)}, u32[]{:S(2)}) copy-start(bf16[512,768]{1,0:T(8,128)(2,1)} %copy-done.14) | copy-start | bytes 2359300
  180.3 3.4 %copy-start.2 = (bf16[512,4096]{1,0:T(8,128)(2,1)S(1)}, bf16[512,4096]{1,0:T(8,128)(2,1)}, u32[]{:S(2)}) copy-start(bf16[512,4096]{1,0:T(8,128)(2,1)} %reshape.110) | copy-start | bytes 12582916
  183.7 1.0 copy-start.5
  183.8 1.3 copy-start.6
  185.0 1.2 collective-permute-start.3
  186.2 3.7 %collective-permute-start.4 = (f32[2048]{0:T(1024)S(1)}, f32[2048]{0:T(1024)S(1)}, u32[]{:S(2)}, u32[]{:S(2)}) collective-permute-start(f32[2048]{0:T(1024)S(1)} %add.86), channel_id=1, source_target_pairs={{0,16},{1,17},{2,18},{3,19},{4,20},{5,21},{6,22},{7,23},{8,24},{9,... | collective-permute-start | bytes 24584 | tf_op jit(solution)/shard_map/ppermute | solution.py:23
  189.9 5.2 %collective-permute-start.5 = (f32[2048]{0:T(1024)S(1)}, f32[2048]{0:T(1024)S(1)}, u32[]{:S(2)}, u32[]{:S(2)}) collective-permute-start(f32[2048]{0:T(1024)S(1)} %add.87), channel_id=1, source_target_pairs={{0,32},{1,33},{2,34},{3,35},{4,36},{5,37},{6,38},{7,39},{8,40},{9,... | collective-permute-start | bytes 24584 | tf_op jit(solution)/shard_map/ppermute | solution.py:23
  192.1 8.7 %copy-start.1 = (bf16[1,2048,768]{2,1,0:T(8,128)(2,1)S(1)}, bf16[1,2048,768]{2,1,0:T(8,128)(2,1)}, u32[]{:S(2)}) copy-start(bf16[1,2048,768]{2,1,0:T(8,128)(2,1)} %param.13) | copy-start | bytes 9437188
  195.1 5.2 %collective-permute-start.6 = (f32[2048]{0:T(1024)S(1)}, f32[2048]{0:T(1024)S(1)}, u32[]{:S(2)}, u32[]{:S(2)}) collective-permute-start(f32[2048]{0:T(1024)S(1)} %add.88), channel_id=1, source_target_pairs={{0,64},{1,65},{2,66},{3,67},{4,68},{5,69},{6,70},{7,71},{8,72},{9,... | collective-permute-start | bytes 24584 | tf_op jit(solution)/shard_map/ppermute | solution.py:23
